TPU v7x, 128 devices: a whole 4x4x4 slice. The times are simulated.
128 devices in a mesh: tsink: 8 (over x, z_lo), mom: 16 (over y, z_hi, core).
Axes of the slice: x: 4, y: 4, z: 4 (z_hi: 2, z_lo: 2; z = z_hi * 2 + z_lo), core: 2. Of those that a mesh axis runs over, the one named last changes fastest.
Arguments:
- perambulators: bfloat16 [8, 4, 1024, 1024], P('tsink'), may hold values from -0.1875 to 0.1875
- elementals: bfloat16 [8, 16, 1024, 1024], P('tsink', 'mom'), may hold values from -6 to 6
- src_times: int32 [4], replicated, may hold values from 0 to 7, as said below
- diagrams: int32 [128, 2], replicated, may hold values from 0 to 15
Outputs:
- meson_blocks: bfloat16 [8, 16, 1024, 1024], P('tsink', 'mom')
- correlators: float32 [128, 8], P('mom', 'tsink')
Inputs may be any that keep to these rules, and one draw needn't show every extreme that they name: `src_times`: distinct time slices; the first and the last time slice are always among them.
All inputs are finite; a program needn't handle non-finite values.
Results may differ from a plain program's by a relative error of at most 0.0055.
Values may be sent and summed in bfloat16 or wider, within the bound.
No kernel may reach another device: no remote copies, remote signals or barrier semaphores. Data moves between devices by JAX's collectives and lax.ppermute only.
A program may use at most 192 MiB of HBM per device.

v0:
```python
import jax
import jax.numpy as jnp
from jax import lax
from jax.sharding import PartitionSpec as P

NSRC = 4


def from_root(block, axis, source):
    block = jnp.where(lax.axis_index(axis) == source, block, jnp.zeros_like(block))
    return lax.psum(block, axis)


def body(perambulators, elementals, src_times, diagrams):
    propagators = perambulators[0]
    own_elemental = elementals[0, 0]
    block_order = propagators.shape[1]
    summed = jnp.zeros((block_order, block_order), jnp.float32)
    for source in range(NSRC):
        elemental = from_root(own_elemental, "tsink", src_times[source])
        half_product = lax.dot_general(
            elemental,
            propagators[source],
            (((1,), (1,)), ((), ())),
            preferred_element_type=jnp.float32,
        ).astype(jnp.bfloat16)
        summed = summed + jnp.dot(
            propagators[source], half_product, preferred_element_type=jnp.float32
        )
    meson = summed.astype(jnp.bfloat16)
    gathered = lax.all_gather(meson[None], "mom", axis=0, tiled=True)
    per_device = diagrams.shape[0] // lax.axis_size("mom")
    own_diagrams = lax.dynamic_slice_in_dim(
        diagrams, lax.axis_index("mom") * per_device, per_device, 0
    )

    def whole_trace(diagram_pair):
        return (
            jnp.einsum(
                "ij,ji->",
                gathered[diagram_pair[0]],
                gathered[diagram_pair[1]],
                preferred_element_type=jnp.float32,
            )
            / block_order
        )

    traces = lax.map(whole_trace, own_diagrams)
    correlators = traces[:, None]
    return (meson[None, None], correlators)


def solution(mesh):
    in_specs = (P("tsink", None, None, None), P("tsink", "mom", None, None), P(), P())
    out_specs = (P("tsink", "mom", None, None), P("mom", "tsink"))
    return jax.shard_map(body, mesh=mesh, in_specs=in_specs, out_specs=out_specs, check_vma=False)
```

profile of v0, /device:TPU:1, one launch (start us, length us, event | category | flops | bytes accessed | tf_op | source)
XLA Modules:
  0.0 796.7 jit_solution(12772699762783100091)
XLA Ops:
  7.2 1.4 fusion.51
  11.1 5.1 select_bitcast_fusion.3
  16.3 342.8 %all-reduce.3.cloned.1.call-done = (bf16[1024,1024]{1,0:T(8,128)(2,1)}, bf16[1024,1024]{1,0:T(8,128)(2,1)}, bf16[1024,1024]{1,0:T(8,128)(2,1)}, bf16[1024,1024]{1,0:T(8,128)(2,1)}) async-done(((bf16[1024,1024]{1,0:T(8,128)(2,1)}, bf16[1024,1024]{1,0:T(8,128)(2,1)}, bf16[1024,1024]{1,0:T(8,128)(2,1)}, bf16[1024,1024]{1,0:T(8,128)(2,1)}), (bf16[1024,1024]{1,0:T(8,128)(2,1)}, bf16[1024,1024]{1,0:T(8,128)(2,1)}, ...) | async-done | bytes 8388624 | tf_op jit(solution)/shard_map/psum | solution.py:11
  359.2 9.5 %fusion = f32[1024,1024]{1,0:T(8,128)} fusion(bf16[1,4,1024,1024]{3,2,1,0:T(8,128)(2,1)} %param.6, bf16[1024,1024]{1,0:T(8,128)(2,1)} %get-tuple-element.39), kind=kOutput, calls=%fused_computation.4 | convolution fusion | flops 4296015872 | bytes 10485760 | tf_op jit(solution)/shard_map/dot_general | solution.py:27
  368.7 8.7 %fusion.4 = f32[1024,1024]{1,0:T(8,128)} fusion(bf16[1,4,1024,1024]{3,2,1,0:T(8,128)(2,1)} %param.6, bf16[1024,1024]{1,0:T(8,128)(2,1)S(1)} %copy-done.4), kind=kOutput, calls=%fused_computation.8 | convolution fusion | flops 4296015872 | bytes 10485760 | tf_op jit(solution)/shard_map/dot_general | solution.py:27
  377.4 9.7 %fusion.8 = f32[1024,1024]{1,0:T(8,128)} fusion(bf16[1,4,1024,1024]{3,2,1,0:T(8,128)(2,1)} %param.6, bf16[1024,1024]{1,0:T(8,128)(2,1)} %get-tuple-element.41), kind=kOutput, calls=%fused_computation.12 | convolution fusion | flops 4296015872 | bytes 10485760 | tf_op jit(solution)/shard_map/dot_general | solution.py:27
  387.1 11.6 %add_convert_fusion = bf16[1024,1024]{1,0:T(8,128)(2,1)} fusion(f32[1024,1024]{1,0:T(8,128)} %fusion, f32[1024,1024]{1,0:T(8,128)} %fusion.4, f32[1024,1024]{1,0:T(8,128)} %fusion.8, bf16[1,4,1024,1024]{3,2,1,0:T(8,128)(2,1)} %param.6, bf16[1024,1024]{1,0:T(8,128)(2,1)S(1)} %copy-done.3), kind=kOutput, calls=%fused_computation.3 | convolution fusion | flops 4300210176 | bytes 20971520 | tf_op jit(solution)/shard_map/dot_general | solution.py:27
  398.9 1.5 copy-done.2
  400.3 2.5 copy.7
  402.9 188.7 %all-gather.3.cloned.1.call-done = bf16[16384,1024]{0,1:T(8,128)(2,1)} async-done(((bf16[1024,1024]{0,1:T(8,128)(2,1)}), bf16[16384,1024]{0,1:T(8,128)(2,1)}) %all-gather.3.cloned.1.call-update) | async-done | bytes 33554448 | tf_op jit(solution)/shard_map/all_gather | solution.py:31
  591.6 43.9 %copy.13 = bf16[16384,1024]{1,0:T(8,128)(2,1)} copy(bf16[16384,1024]{0,1:T(8,128)(2,1)} %all-gather.3.cloned.1.call-done) | data formatting | bytes 67108864 | tf_op jit(solution)/shard_map/while | solution.py:48
  635.5 153.7 %while.10 = (s32[]{:T(128)}, f32[8]{0:T(128)S(1)}, s32[8,2]{0,1:T(2,128)S(1)}, bf16[16,1024,1024]{2,1,0:T(8,128)(2,1)}, s32[]{:T(128)}, /*index=5*/s32[]{:T(128)}, s32[]{:T(128)}, f32[]{:T(128)}) while((s32[]{:T(128)}, f32[8]{0:T(128)S(1)}, s32[8,2]{0,1:T(2,128)S(1)}, bf16[16,1024,1024]{2,1,0:T(8,128)(2,1)}, s32[]{:T(128)}, ...), condition=%wide.region_5.6_spmd, body=%wide.region_4.5_spmd.sunk | while | flops 4194312 | bytes 20971744 | solution.py:48
  635.6 0.5 fusion.57
  638.1 4.0 bitcast_convert_fusion.2
  642.1 5.4 copy.15
  649.3 4.6 multiply_reduce_fusion.2
  654.6 0.1 dynamic_update_slice.5
  654.8 0.5 fusion.57
  657.3 4.0 bitcast_convert_fusion.2
  661.3 5.4 copy.15
  668.5 4.6 multiply_reduce_fusion.2
  673.8 0.1 dynamic_update_slice.5
  674.0 0.5 fusion.57
  676.5 4.0 bitcast_convert_fusion.2
  680.5 5.4 copy.15
  687.7 4.6 multiply_reduce_fusion.2
  693.2 0.5 fusion.57
  695.7 4.0 bitcast_convert_fusion.2
  699.7 5.4 copy.15
  706.9 4.6 multiply_reduce_fusion.2
  712.4 0.5 fusion.57
  714.9 4.0 bitcast_convert_fusion.2
  718.9 5.4 copy.15
  726.2 4.6 multiply_reduce_fusion.2
  731.7 0.5 fusion.57
  734.1 4.0 bitcast_convert_fusion.2
  738.1 5.4 copy.15
  745.4 4.6 multiply_reduce_fusion.2
  750.9 0.5 fusion.57
  753.3 4.0 bitcast_convert_fusion.2
  757.4 5.4 copy.15
  764.6 4.6 multiply_reduce_fusion.2
  770.1 0.5 fusion.57
  772.5 4.0 bitcast_convert_fusion.2
  776.6 5.4 copy.15
  783.8 4.6 multiply_reduce_fusion.2
  789.2 0.5 copy-done.5
  789.7 0.2 copy-done.1
  (29 shorter events, 1.5 us)
Async XLA Ops:
  7.2 391.6 %copy-start = (s32[128,2]{0,1:T(2,128)S(1)}, s32[128,2]{0,1:T(2,128)}, u32[]{:S(2)}) copy-start(s32[128,2]{0,1:T(2,128)} %param.9) | copy-start | bytes 3076
  7.2 352.0 %all-reduce.3.cloned.1.call-start = ((), (), s32[]{:S(2)}) async-start(), calls=%async_computation.1 | async-start | bytes 16777216 | tf_op jit(solution)/shard_map/psum | solution.py:11
  16.3 575.3 %all-gather.3.cloned.1.call-start = ((), (), s32[]{:S(2)}) async-start(), calls=%async_computation | async-start | bytes 35651584 | tf_op jit(solution)/shard_map/all_gather | solution.py:31
  359.2 9.5 %copy-start.4 = (bf16[1024,1024]{1,0:T(8,128)(2,1)S(1)}, bf16[1024,1024]{1,0:T(8,128)(2,1)}, u32[]{:S(2)}) copy-start(bf16[1024,1024]{1,0:T(8,128)(2,1)} %get-tuple-element.40) | copy-start | bytes 6291460
  377.4 9.7 %copy-start.3 = (bf16[1024,1024]{1,0:T(8,128)(2,1)S(1)}, bf16[1024,1024]{1,0:T(8,128)(2,1)}, u32[]{:S(2)}) copy-start(bf16[1024,1024]{1,0:T(8,128)(2,1)} %get-tuple-element.42) | copy-start | bytes 6291460
  398.7 1.6 copy-start.2
  789.2 0.5 copy-start.5
  789.2 0.7 copy-start.1
Sparse Core Ops, SparseCore 0:
  16.4 342.7 all-reduce.2
  398.9 192.6 all-gather.2
where the time goes:
time: 799 us; the launch traced here: 797 us
  waiting for transfers between devices  532 us (67%)
  local copies, waits for them, and re-layouts  99.3 us (12%)
  other arithmetic  74.3 us (9%)
  matrix products  39.5 us (5%)
  loops' own time  35.4 us (4%)
  between operations  16.6 us (2%)
    psum x1, waiting for transfers between devices, from_root(): return lax.psum(block, axis)  343 us
    all_gather x1, waiting for transfers between devices, body(): gathered = lax.all_gather(meson[None], 'mom', axis=0, tiled=True)  189 us
    while x1, local copies, waits for them, and re-layouts, body(): traces = lax.map(whole_trace, own_diagrams)  43.9 us
    while x8, local copies, waits for them, and re-layouts  43.3 us
    dot_general x4, matrix products, body(): jnp.dot(propagators[source], half_product, preferred_element_type=jnp.flo...  39.5 us
    dot_general x8, other arithmetic, whole_trace(): jnp.einsum('ij,ji->', gathered[diagram_pair[0]], gathered[diagram_pair[1]...  37 us
    another operation x1, loops' own time, body(): traces = lax.map(whole_trace, own_diagrams)  35.4 us
    while x8, other arithmetic  32.1 us
  transfers between devices with their start and end apart: 2, of which 2 were waited for; matrix products, arithmetic and copies ran while one was open for 0% of the time, Pallas kernels for 0%

commit v1 on v0

v1 whole, which is shorter than its diff:
```python
import jax
import jax.numpy as jnp
from jax import lax
from jax.sharding import PartitionSpec as P

NSRC = 4


def source_elementals(own_elemental, src_times):
    n_t = lax.axis_size("tsink")
    order = own_elemental.shape[0]
    pieces = own_elemental.reshape(n_t, order // n_t, order)
    received = lax.all_to_all(pieces, "tsink", 0, 0)
    chosen = received[src_times]
    elementals = []
    for source in range(NSRC):
        gathered = lax.all_gather(chosen[source], "tsink", axis=0, tiled=True)
        elementals.append(gathered)
    return elementals


def body(perambulators, elementals, src_times, diagrams):
    propagators = perambulators[0]
    own_elemental = elementals[0, 0]
    block_order = propagators.shape[1]
    chosen = source_elementals(own_elemental, src_times)
    summed = jnp.zeros((block_order, block_order), jnp.float32)
    for source in range(NSRC):
        half_product = lax.dot_general(
            chosen[source],
            propagators[source],
            (((1,), (1,)), ((), ())),
            preferred_element_type=jnp.float32,
        ).astype(jnp.bfloat16)
        summed = summed + jnp.dot(
            propagators[source], half_product, preferred_element_type=jnp.float32
        )
    meson = summed.astype(jnp.bfloat16)

    n_m = lax.axis_size("mom")
    rows = block_order // n_m
    slices = jnp.stack(
        [meson.reshape(n_m, rows, block_order), meson.T.reshape(n_m, rows, block_order)],
        axis=1,
    )
    received = lax.all_to_all(slices, "mom", 0, 0)
    own_rows = received[:, 0].reshape(n_m, rows * block_order)
    own_cols = received[:, 1].reshape(n_m, rows * block_order)
    partial = lax.dot_general(
        own_rows, own_cols, (((1,), (1,)), ((), ())), preferred_element_type=jnp.float32
    )
    pair_traces = lax.psum(partial, "mom") / block_order

    per_device = diagrams.shape[0] // n_m
    own_diagrams = lax.dynamic_slice_in_dim(
        diagrams, lax.axis_index("mom") * per_device, per_device, 0
    )
    traces = pair_traces[own_diagrams[:, 0], own_diagrams[:, 1]]
    correlators = traces[:, None]
    return (meson[None, None], correlators)


def solution(mesh):
    in_specs = (P("tsink", None, None, None), P("tsink", "mom", None, None), P(), P())
    out_specs = (P("tsink", "mom", None, None), P("mom", "tsink"))
    return jax.shard_map(body, mesh=mesh, in_specs=in_specs, out_specs=out_specs, check_vma=False)
```

time: 799 us -> 391 us (0.49)
  waiting for transfers between devices: 532 us -> 265 us
  local copies, waits for them, and re-layouts: 99.3 us -> 13.1 us
  other arithmetic: 74.3 us -> 2 us
  loops' own time: 35.4 us -> 0 us
  blocking collectives: 0 us -> 34.7 us
  starting transfers between devices: 0.08 us -> 15.1 us
    psum x1 -> x0, waiting for transfers between devices: 343 us -> none  [from_root(): return lax.psum(block, axis)]
    while x9 -> x0, local copies, waits for them, and re-layouts: 87.2 us -> none  [the longest x1 43.9 us: body(): traces = lax.map(whole_trace, own_diagrams)]
    all_to_all x0 -> x2, waiting for transfers between devices: none -> 81 us  [the longest x1 50.5 us: body(): received = lax.all_to_all(slices, 'mom', 0, 0)]
    dot_general x8 -> x0, other arithmetic: 37 us -> none  [whole_trace(): jnp.einsum('ij,ji->', gathered[diagram_pair[0]], gathered[diagram_pair[1]...]
    another operation x1 -> x0, loops' own time: 35.4 us -> none  [body(): traces = lax.map(whole_trace, own_diagrams)]
    psum x0 -> x1, blocking collectives: none -> 34.7 us  [body(): pair_traces = lax.psum(partial, 'mom') / block_order]
    while x8 -> x0, other arithmetic: 32.1 us -> none
    all_to_all x0 -> x2, starting transfers between devices: none -> 15 us  [the longest x1 8.62 us: body(): received = lax.all_to_all(slices, 'mom', 0, 0)]
  transfers between devices with their start and end apart: 2 -> 6, of which waited for: 2 -> 6; matrix products, arithmetic and copies ran while one was open for 0% -> 8% of each run, Pallas kernels for 0% -> 0%
where the time goes in v1:
time: 391 us; the launch traced here: 388 us
  waiting for transfers between devices  265 us (68%)
  matrix products  43.8 us (11%)
  blocking collectives  34.7 us (9%)
  starting transfers between devices  15.1 us (4%)
  between operations  13.9 us (4%)
  local copies, waits for them, and re-layouts  13.1 us (3%)
    all_gather x4, waiting for transfers between devices, source_elementals(): gathered = lax.all_gather(chosen[source], 'tsink', axis=0, tiled=True)  182 us
    all_to_all x1, waiting for transfers between devices, body(): received = lax.all_to_all(slices, 'mom', 0, 0)  50.5 us
    dot_general x4, matrix products, body(): jnp.dot(propagators[source], half_product, preferred_element_type=jnp.flo...  39.4 us
    psum x1, blocking collectives, body(): pair_traces = lax.psum(partial, 'mom') / block_order  34.7 us
    all_to_all x1, waiting for transfers between devices, source_elementals(): received = lax.all_to_all(pieces, 'tsink', 0, 0)  30.5 us
    all_to_all x1, starting transfers between devices, body(): received = lax.all_to_all(slices, 'mom', 0, 0)  8.62 us
  transfers between devices with their start and end apart: 6, of which 6 were waited for; matrix products, arithmetic and copies ran while one was open for 8% of the time, Pallas kernels for 0%

profile of v1, /device:TPU:1, one launch (start us, length us, event | category | flops | bytes accessed | tf_op | source)
XLA Modules:
  0.0 387.8 jit_solution(18396445556078912893)
XLA Ops:
  7.2 0.0 copy-start
  7.2 0.0 copy-start.1
  7.2 6.3 %all-to-all-start = ((bf16[8,128,1024]{2,1,0:T(8,128)(2,1)}), bf16[8,128,1024]{2,1,0:T(8,128)(2,1)S(1)}, u32[]{:S(2)}, u32[]{:S(2)}) async-start(bf16[8,128,1024]{2,1,0:T(8,128)(2,1)} %bitcast.95), calls=%async_computation | async-start | bytes 4194304 | tf_op jit(solution)/shard_map/all_to_all | solution.py:13
  13.5 0.0 all-gather.15.cloned.1.call-start
  13.6 0.0 copy-done.1
  13.6 30.5 %all-to-all-done = bf16[8,128,1024]{2,1,0:T(8,128)(2,1)S(1)} async-done(((bf16[8,128,1024]{2,1,0:T(8,128)(2,1)}), bf16[8,128,1024]{2,1,0:T(8,128)(2,1)S(1)}, u32[]{:S(2)}, u32[]{:S(2)}) %all-to-all-start) | async-done | bytes 2097184 | tf_op jit(solution)/shard_map/all_to_all | solution.py:13
  44.1 0.6 gather_fusion
  44.8 1.0 fusion.81
  45.7 0.0 all-gather.15.cloned.1.call-update
  45.8 0.0 all-gather.11.cloned.1.call-start
  45.8 0.7 all-gather.11.cloned.1.call-update
  46.5 0.0 all-gather.13.cloned.1.call-start
  46.6 0.7 all-gather.13.cloned.1.call-update
  47.2 0.0 all-gather.9.cloned.1.call-start
  47.3 0.5 all-gather.9.cloned.1.call-update
  47.8 48.0 %all-gather.15.cloned.1.call-done = bf16[1,1024,1024]{2,1,0:T(8,128)(2,1)} async-done(((bf16[1,128,1024]{2,1,0:T(8,128)(2,1)}), bf16[1,1024,1024]{2,1,0:T(8,128)(2,1)}) %all-gather.15.cloned.1.call-update) | async-done | bytes 2097168 | tf_op jit(solution)/shard_map/all_gather | solution.py:17
  95.9 9.4 %fusion.1 = f32[1024,1024]{1,0:T(8,128)} fusion(bf16[1,4,1024,1024]{3,2,1,0:T(8,128)(2,1)} %param.4, bf16[1,1024,1024]{2,1,0:T(8,128)(2,1)} %all-gather.15.cloned.1.call-done), kind=kOutput, calls=%fused_computation.7 | convolution fusion | flops 4296015872 | bytes 10485760 | tf_op jit(solution)/shard_map/dot_general | solution.py:35
  105.2 44.7 %all-gather.11.cloned.1.call-done = bf16[1,1024,1024]{2,1,0:T(8,128)(2,1)} async-done(((bf16[1,128,1024]{2,1,0:T(8,128)(2,1)}), bf16[1,1024,1024]{2,1,0:T(8,128)(2,1)}) %all-gather.11.cloned.1.call-update) | async-done | bytes 2097168 | tf_op jit(solution)/shard_map/all_gather | solution.py:17
  149.9 9.4 %fusion.11 = f32[1024,1024]{1,0:T(8,128)} fusion(bf16[1,4,1024,1024]{3,2,1,0:T(8,128)(2,1)} %param.4, bf16[1,1024,1024]{2,1,0:T(8,128)(2,1)} %all-gather.11.cloned.1.call-done), kind=kOutput, calls=%fused_computation.17 | convolution fusion | flops 4296015872 | bytes 10485760 | tf_op jit(solution)/shard_map/dot_general | solution.py:35
  159.3 44.7 %all-gather.13.cloned.1.call-done = bf16[1,1024,1024]{2,1,0:T(8,128)(2,1)} async-done(((bf16[1,128,1024]{2,1,0:T(8,128)(2,1)}), bf16[1,1024,1024]{2,1,0:T(8,128)(2,1)}) %all-gather.13.cloned.1.call-update) | async-done | bytes 2097168 | tf_op jit(solution)/shard_map/all_gather | solution.py:17
  204.0 9.6 %fusion.6 = f32[1024,1024]{1,0:T(8,128)} fusion(bf16[1,4,1024,1024]{3,2,1,0:T(8,128)(2,1)} %param.4, bf16[1,1024,1024]{2,1,0:T(8,128)(2,1)} %all-gather.13.cloned.1.call-done), kind=kOutput, calls=%fused_computation.12 | convolution fusion | flops 4296015872 | bytes 10485760 | tf_op jit(solution)/shard_map/dot_general | solution.py:35
  213.6 44.9 %all-gather.9.cloned.1.call-done = bf16[1,1024,1024]{2,1,0:T(8,128)(2,1)} async-done(((bf16[1,128,1024]{2,1,0:T(8,128)(2,1)}), bf16[1,1024,1024]{2,1,0:T(8,128)(2,1)}) %all-gather.9.cloned.1.call-update) | async-done | bytes 2097168 | tf_op jit(solution)/shard_map/all_gather | solution.py:17
  258.5 11.0 %add_convert_fusion = bf16[1024,1024]{1,0:T(8,128)(2,1)S(1)} fusion(f32[1024,1024]{1,0:T(8,128)} %fusion.1, f32[1024,1024]{1,0:T(8,128)} %fusion.6, f32[1024,1024]{1,0:T(8,128)} %fusion.11, bf16[1,4,1024,1024]{3,2,1,0:T(8,128)(2,1)} %param.4, bf16[1,1024,1024]{2,1,0:T(8,128)(2,1)} %all-gather.9.cloned.1.call-done), kind=kOutput, calls=%fused_computation.3 | convolution fusion | flops 4300210176 | bytes 20971520 | tf_op jit(solution)/shard_map/dot_general | solution.py:35
  269.6 2.6 copy.13
  272.1 2.0 pad_maximum_fusion
  274.1 2.4 copy.14
  276.5 8.6 %all-to-all-start.1 = ((bf16[16,2,64,1024]{3,2,1,0:T(8,128)(2,1)}), bf16[16,2,64,1024]{3,2,1,0:T(8,128)(2,1)}, u32[]{:S(2)}, u32[]{:S(2)}) async-start(bf16[16,2,64,1024]{3,2,1,0:T(8,128)(2,1)} %copy.14), calls=%async_computation.1 | async-start | bytes 8388608 | tf_op jit(solution)/shard_map/all_to_all | solution.py:46
  285.1 0.0 copy-done
  285.1 0.1 constant_dynamic-slice_fusion
  285.2 2.6 copy.17
  287.8 50.5 %all-to-all-done.1 = bf16[16,2,64,1024]{3,2,1,0:T(8,128)(2,1)} async-done(((bf16[16,2,64,1024]{3,2,1,0:T(8,128)(2,1)}), bf16[16,2,64,1024]{3,2,1,0:T(8,128)(2,1)}, u32[]{:S(2)}, u32[]{:S(2)}) %all-to-all-start.1) | async-done | bytes 4194336 | tf_op jit(solution)/shard_map/all_to_all | solution.py:46
  338.2 2.7 fusion.80
  341.0 4.4 %fusion.73 = f32[16,16]{1,0:T(8,128)S(1)} fusion(bf16[16,1,64,1024]{3,2,1,0:T(8,128)(2,1)S(1)} %get-tuple-element.9, bf16[16,1,64,1024]{3,2,1,0:T(8,128)(2,1)S(1)} %get-tuple-element.8), kind=kOutput, calls=%fused_computation.39 | convolution fusion | flops 33554432 | bytes 4195328 | tf_op jit(solution)/shard_map/dot_general | solution.py:49
  345.4 34.7 %psum.7 = f32[16,16]{1,0:T(8,128)S(1)} all-reduce(f32[16,16]{1,0:T(8,128)S(1)} %fusion.73), channel_id=1, replica_groups=mesh['tsink'=8,'mom'=16] {'mom'}, use_global_device_ids=true, to_apply=%region_0.0 | all-reduce | flops 256 | bytes 2048 | tf_op jit(solution)/shard_map/psum | solution.py:52
  380.1 1.2 gather_fusion.1
  (4 shorter events, 0.0 us)
Async XLA Ops:
  7.2 278.0 %copy-start = (s32[128,2]{0,1:T(2,128)S(1)}, s32[128,2]{0,1:T(2,128)}, u32[]{:S(2)}) copy-start(s32[128,2]{0,1:T(2,128)} %param.7) | copy-start | bytes 3076
  7.2 6.4 %copy-start.1 = (s32[4]{0:T(128)S(1)}, s32[4]{0:T(128)}, u32[]{:S(2)}) copy-start(s32[4]{0:T(128)} %param.6) | copy-start | bytes 52
  7.2 37.0 %all-to-all-start = ((bf16[8,128,1024]{2,1,0:T(8,128)(2,1)}), bf16[8,128,1024]{2,1,0:T(8,128)(2,1)S(1)}, u32[]{:S(2)}, u32[]{:S(2)}) async-start(bf16[8,128,1024]{2,1,0:T(8,128)(2,1)} %bitcast.95), calls=%async_computation | async-start | bytes 4194304 | tf_op jit(solution)/shard_map/all_to_all | solution.py:13
  13.5 82.3 %all-gather.15.cloned.1.call-start = ((), (), s32[]{:S(2)}) async-start(), calls=%async_computation.5 | async-start | bytes 2359296 | tf_op jit(solution)/shard_map/all_gather | solution.py:17
  45.8 104.2 %all-gather.11.cloned.1.call-start = ((), (), s32[]{:S(2)}) async-start(), calls=%async_computation.3 | async-start | bytes 2359296 | tf_op jit(solution)/shard_map/all_gather | solution.py:17
  46.5 157.5 %all-gather.13.cloned.1.call-start = ((), (), s32[]{:S(2)}) async-start(), calls=%async_computation.4 | async-start | bytes 2359296 | tf_op jit(solution)/shard_map/all_gather | solution.py:17
  47.2 211.3 %all-gather.9.cloned.1.call-start = ((), (), s32[]{:S(2)}) async-start(), calls=%async_computation.2 | async-start | bytes 2359296 | tf_op jit(solution)/shard_map/all_gather | solution.py:17
  276.5 61.7 %all-to-all-start.1 = ((bf16[16,2,64,1024]{3,2,1,0:T(8,128)(2,1)}), bf16[16,2,64,1024]{3,2,1,0:T(8,128)(2,1)}, u32[]{:S(2)}, u32[]{:S(2)}) async-start(bf16[16,2,64,1024]{3,2,1,0:T(8,128)(2,1)} %copy.14), calls=%async_computation.1 | async-start | bytes 8388608 | tf_op jit(solution)/shard_map/all_to_all | solution.py:46
Sparse Core Ops, SparseCore 0:
  45.9 49.9 all-gather.14
  97.5 52.3 all-gather.10
  151.6 52.3 all-gather.12
  206.1 52.3 all-gather.8

commit v2 on v1

--- a/solution.py
+++ b/solution.py
@@ -12,11 +12,8 @@
     pieces = own_elemental.reshape(n_t, order // n_t, order)
     received = lax.all_to_all(pieces, "tsink", 0, 0)
     chosen = received[src_times]
-    elementals = []
-    for source in range(NSRC):
-        gathered = lax.all_gather(chosen[source], "tsink", axis=0, tiled=True)
-        elementals.append(gathered)
-    return elementals
+    gathered = lax.all_gather(chosen, "tsink", axis=1, tiled=True)
+    return [gathered[source] for source in range(NSRC)]
 
 
 def body(perambulators, elementals, src_times, diagrams):
@@ -49,14 +46,9 @@
     partial = lax.dot_general(
         own_rows, own_cols, (((1,), (1,)), ((), ())), preferred_element_type=jnp.float32
     )
-    pair_traces = lax.psum(partial, "mom") / block_order
-
-    per_device = diagrams.shape[0] // n_m
-    own_diagrams = lax.dynamic_slice_in_dim(
-        diagrams, lax.axis_index("mom") * per_device, per_device, 0
-    )
-    traces = pair_traces[own_diagrams[:, 0], own_diagrams[:, 1]]
-    correlators = traces[:, None]
+    per_diagram = partial[diagrams[:, 0], diagrams[:, 1]]
+    spread = lax.all_to_all(per_diagram.reshape(n_m, -1), "mom", 0, 0)
+    correlators = (jnp.sum(spread, axis=0) / block_order)[:, None]
     return (meson[None, None], correlators)
 
 

time: 391 us -> 358 us (0.916)
  blocking collectives: 34.7 us -> 0 us
  starting transfers between devices: 15.1 us -> 27.1 us
  waiting for transfers between devices: 265 us -> 257 us
    psum x1 -> x0, blocking collectives: 34.7 us -> none  [body(): pair_traces = lax.psum(partial, 'mom') / block_order]
    all_gather x4 -> x1, waiting for transfers between devices: 182 us -> 169 us  [source_elementals(): gathered = lax.all_gather(chosen, 'tsink', axis=1, tiled=True)]
    all_to_all x0 -> x1, starting transfers between devices: none -> 13.3 us  [body(): spread = lax.all_to_all(per_diagram.reshape(n_m, -1), 'mom', 0, 0)]
    all_to_all x0 -> x1, waiting for transfers between devices: none -> 4.46 us  [body(): spread = lax.all_to_all(per_diagram.reshape(n_m, -1), 'mom', 0, 0)]
  transfers between devices with their start and end apart: 6 -> 4, of which waited for: 6 -> 4; matrix products, arithmetic and copies ran while one was open for 8% -> 1% of each run, Pallas kernels for 0% -> 0%
where the time goes in v2:
time: 358 us
  waiting for transfers between devices  257 us (72%)
  matrix products  43.7 us (12%)
  starting transfers between devices  27.1 us (8%)
  between operations  14.1 us (4%)
  local copies, waits for them, and re-layouts  13.8 us (4%)
    all_gather x1, waiting for transfers between devices, source_elementals(): gathered = lax.all_gather(chosen, 'tsink', axis=1, tiled=True)  169 us
    all_to_all x1, waiting for transfers between devices, body(): received = lax.all_to_all(slices, 'mom', 0, 0)  53.1 us
    dot_general x4, matrix products, body(): jnp.dot(propagators[source], half_product, preferred_element_type=jnp.flo...  39.2 us
    all_to_all x1, waiting for transfers between devices, source_elementals(): received = lax.all_to_all(pieces, 'tsink', 0, 0)  30.5 us
    all_to_all x1, starting transfers between devices, body(): spread = lax.all_to_all(per_diagram.reshape(n_m, -1), 'mom', 0, 0)  13.3 us
    all_to_all x1, starting transfers between devices, body(): received = lax.all_to_all(slices, 'mom', 0, 0)  7.56 us
  transfers between devices with their start and end apart: 4, of which 4 were waited for; matrix products, arithmetic and copies ran while one was open for 1% of the time, Pallas kernels for 0%

profile of v2, /device:TPU:1, one launch (start us, length us, event | category | flops | bytes accessed | tf_op | source)
XLA Modules:
  0.0 358.1 jit_solution(10565608259464846351)
XLA Ops:
  7.2 0.0 copy-start.1
  7.2 6.2 %all-to-all-start = ((bf16[8,128,1024]{2,1,0:T(8,128)(2,1)}), bf16[8,128,1024]{2,1,0:T(8,128)(2,1)S(1)}, u32[]{:S(2)}, u32[]{:S(2)}) async-start(bf16[8,128,1024]{2,1,0:T(8,128)(2,1)} %bitcast.97), calls=%async_computation | async-start | bytes 4194304 | tf_op jit(solution)/shard_map/all_to_all | solution.py:13
  13.4 0.0 all-gather.3.cloned.1.call-start
  13.4 0.0 copy-done.1
  13.5 30.5 %all-to-all-done = bf16[8,128,1024]{2,1,0:T(8,128)(2,1)S(1)} async-done(((bf16[8,128,1024]{2,1,0:T(8,128)(2,1)}), bf16[8,128,1024]{2,1,0:T(8,128)(2,1)S(1)}, u32[]{:S(2)}, u32[]{:S(2)}) %all-to-all-start) | async-done | bytes 2097184 | tf_op jit(solution)/shard_map/all_to_all | solution.py:13
  44.0 1.6 gather_fusion
  45.6 0.0 all-gather.3.cloned.1.call-update
  45.6 168.7 %all-gather.3.cloned.1.call-done = bf16[4,1024,1024]{2,1,0:T(8,128)(2,1)} async-done(((bf16[4,128,1024]{2,1,0:T(8,128)(2,1)}), bf16[4,1024,1024]{2,1,0:T(8,128)(2,1)}) %all-gather.3.cloned.1.call-update) | async-done | bytes 8388624 | tf_op jit(solution)/shard_map/all_gather | solution.py:15
  214.3 9.3 %fusion.11 = f32[1024,1024]{1,0:T(8,128)} fusion(bf16[1,4,1024,1024]{3,2,1,0:T(8,128)(2,1)} %param.4, bf16[4,1024,1024]{2,1,0:T(8,128)(2,1)} %all-gather.3.cloned.1.call-done), kind=kOutput, calls=%fused_computation.21 | convolution fusion | flops 4296015872 | bytes 10485760 | tf_op jit(solution)/shard_map/dot_general | solution.py:32
  223.7 9.4 %fusion.5 = f32[1024,1024]{1,0:T(8,128)} fusion(bf16[1,4,1024,1024]{3,2,1,0:T(8,128)(2,1)} %param.4, bf16[4,1024,1024]{2,1,0:T(8,128)(2,1)} %all-gather.3.cloned.1.call-done), kind=kOutput, calls=%fused_computation.15 | convolution fusion | flops 4296015872 | bytes 10485760 | tf_op jit(solution)/shard_map/dot_general | solution.py:32
  233.0 9.5 %fusion.8 = f32[1024,1024]{1,0:T(8,128)} fusion(bf16[1,4,1024,1024]{3,2,1,0:T(8,128)(2,1)} %param.4, bf16[4,1024,1024]{2,1,0:T(8,128)(2,1)} %all-gather.3.cloned.1.call-done), kind=kOutput, calls=%fused_computation.18 | convolution fusion | flops 4296015872 | bytes 10485760 | tf_op jit(solution)/shard_map/dot_general | solution.py:32
  242.5 11.0 %add_convert_fusion = bf16[1024,1024]{1,0:T(8,128)(2,1)S(1)} fusion(f32[1024,1024]{1,0:T(8,128)} %fusion.5, f32[1024,1024]{1,0:T(8,128)} %fusion.8, f32[1024,1024]{1,0:T(8,128)} %fusion.11, bf16[1,4,1024,1024]{3,2,1,0:T(8,128)(2,1)} %param.4, bf16[4,1024,1024]{2,1,0:T(8,128)(2,1)} %all-gather.3.cloned.1.call-done), kind=kOutput, calls=%fused_computation.3 | convolution fusion | flops 4300210176 | bytes 20971520 | tf_op jit(solution)/shard_map/dot_general | solution.py:32
  253.6 2.6 copy.13
  256.1 2.0 pad_maximum_fusion
  258.1 2.4 copy.14
  260.5 0.0 copy-start
  260.5 7.6 %all-to-all-start.1 = ((bf16[16,2,64,1024]{3,2,1,0:T(8,128)(2,1)}), bf16[16,2,64,1024]{3,2,1,0:T(8,128)(2,1)}, u32[]{:S(2)}, u32[]{:S(2)}) async-start(bf16[16,2,64,1024]{3,2,1,0:T(8,128)(2,1)} %copy.14), calls=%async_computation.1 | async-start | bytes 8388608 | tf_op jit(solution)/shard_map/all_to_all | solution.py:43
  268.1 0.0 copy-done
  268.1 53.1 %all-to-all-done.1 = bf16[16,2,64,1024]{3,2,1,0:T(8,128)(2,1)} async-done(((bf16[16,2,64,1024]{3,2,1,0:T(8,128)(2,1)}), bf16[16,2,64,1024]{3,2,1,0:T(8,128)(2,1)}, u32[]{:S(2)}, u32[]{:S(2)}) %all-to-all-start.1) | async-done | bytes 4194336 | tf_op jit(solution)/shard_map/all_to_all | solution.py:43
  321.2 2.7 fusion.58
  323.9 4.4 %fusion.51 = f32[16,16]{1,0:T(8,128)S(1)} fusion(bf16[16,1,64,1024]{3,2,1,0:T(8,128)(2,1)S(1)} %get-tuple-element.9, bf16[16,1,64,1024]{3,2,1,0:T(8,128)(2,1)S(1)} %get-tuple-element.8), kind=kOutput, calls=%fused_computation.39 | convolution fusion | flops 33554432 | bytes 4195328 | tf_op jit(solution)/shard_map/dot_general | solution.py:46
  328.4 1.3 gather_fusion.1
  329.6 0.7 all_to_all.14
  330.3 13.3 %all-to-all-start.2 = ((f32[16,1,8]{2,1,0:T(1,128)}), f32[16,1,8]{2,1,0:T(1,128)S(1)}, u32[]{:S(2)}, u32[]{:S(2)}) async-start(f32[16,1,8]{2,1,0:T(1,128)} %bitcast.17), calls=%async_computation.2 | async-start | bytes 16384 | tf_op jit(solution)/shard_map/all_to_all | solution.py:50
  343.6 2.6 copy.18
  346.2 4.5 %all-to-all-done.2 = f32[16,1,8]{2,1,0:T(1,128)S(1)} async-done(((f32[16,1,8]{2,1,0:T(1,128)}), f32[16,1,8]{2,1,0:T(1,128)S(1)}, u32[]{:S(2)}, u32[]{:S(2)}) %all-to-all-start.2) | async-done | bytes 544 | tf_op jit(solution)/shard_map/all_to_all | solution.py:50
  350.7 0.5 multiply_bitcast_fusion
  (4 shorter events, 0.1 us)
Async XLA Ops:
  7.2 6.3 %copy-start.1 = (s32[4]{0:T(128)S(1)}, s32[4]{0:T(128)}, u32[]{:S(2)}) copy-start(s32[4]{0:T(128)} %param.6) | copy-start | bytes 52
  7.2 36.8 %all-to-all-start = ((bf16[8,128,1024]{2,1,0:T(8,128)(2,1)}), bf16[8,128,1024]{2,1,0:T(8,128)(2,1)S(1)}, u32[]{:S(2)}, u32[]{:S(2)}) async-start(bf16[8,128,1024]{2,1,0:T(8,128)(2,1)} %bitcast.97), calls=%async_computation | async-start | bytes 4194304 | tf_op jit(solution)/shard_map/all_to_all | solution.py:13
  13.4 200.9 %all-gather.3.cloned.1.call-start = ((), (), s32[]{:S(2)}) async-start(), calls=%async_computation.3 | async-start | bytes 9437184 | tf_op jit(solution)/shard_map/all_gather | solution.py:15
  260.5 7.6 %copy-start = (s32[128,2]{0,1:T(2,128)S(1)}, s32[128,2]{0,1:T(2,128)}, u32[]{:S(2)}) copy-start(s32[128,2]{0,1:T(2,128)} %param.7) | copy-start | bytes 3076
  260.5 60.7 %all-to-all-start.1 = ((bf16[16,2,64,1024]{3,2,1,0:T(8,128)(2,1)}), bf16[16,2,64,1024]{3,2,1,0:T(8,128)(2,1)}, u32[]{:S(2)}, u32[]{:S(2)}) async-start(bf16[16,2,64,1024]{3,2,1,0:T(8,128)(2,1)} %copy.14), calls=%async_computation.1 | async-start | bytes 8388608 | tf_op jit(solution)/shard_map/all_to_all | solution.py:43
  330.3 20.3 %all-to-all-start.2 = ((f32[16,1,8]{2,1,0:T(1,128)}), f32[16,1,8]{2,1,0:T(1,128)S(1)}, u32[]{:S(2)}, u32[]{:S(2)}) async-start(f32[16,1,8]{2,1,0:T(1,128)} %bitcast.17), calls=%async_computation.2 | async-start | bytes 16384 | tf_op jit(solution)/shard_map/all_to_all | solution.py:50
Sparse Core Ops, SparseCore 0:
  45.7 168.5 all-gather.2

commit v3 on v2

--- a/solution.py
+++ b/solution.py
@@ -6,31 +6,65 @@
 NSRC = 4
 
 
-def source_elementals(own_elemental, src_times):
+def shifted(block, offset, n_t):
+    pairs = [(t, (t + offset) % n_t) for t in range(n_t)]
+    return lax.ppermute(block, "tsink", pairs)
+
+
+def swapped(block, n_t):
+    return lax.ppermute(block, "tsink", [(t, t ^ 1) for t in range(n_t)])
+
+
+def source_pieces(own_elemental, src_times):
     n_t = lax.axis_size("tsink")
     order = own_elemental.shape[0]
-    pieces = own_elemental.reshape(n_t, order // n_t, order)
+    rows = order // n_t
+    half = rows // 2
+    pieces = own_elemental.reshape(n_t, rows, order)
     received = lax.all_to_all(pieces, "tsink", 0, 0)
-    chosen = received[src_times]
-    gathered = lax.all_gather(chosen, "tsink", axis=1, tiled=True)
-    return [gathered[source] for source in range(NSRC)]
+    own = received[src_times]
+    t = lax.axis_index("tsink")
+    step = 2
+    partner = swapped(own, n_t)
+    from_left = shifted(own, step, n_t)
+    from_right = shifted(own, -step, n_t)
+    far = jnp.concatenate(
+        [shifted(from_left[:, :half], step, n_t), shifted(from_right[:, half:], -step, n_t)], axis=1
+    )
+    partner_left = shifted(partner, step, n_t)
+    partner_right = shifted(partner, -step, n_t)
+    partner_far = jnp.concatenate(
+        [shifted(partner_left[:, :half], step, n_t), shifted(partner_right[:, half:], -step, n_t)],
+        axis=1,
+    )
+    return [
+        (t, own),
+        (t ^ 1, partner),
+        ((t - step) % n_t, from_left),
+        ((t + step) % n_t, from_right),
+        ((t + 2 * step) % n_t, far),
+        ((t - step) % n_t ^ 1, partner_left),
+        ((t + step) % n_t ^ 1, partner_right),
+        ((t + 2 * step) % n_t ^ 1, partner_far),
+    ]
 
 
 def body(perambulators, elementals, src_times, diagrams):
     propagators = perambulators[0]
     own_elemental = elementals[0, 0]
     block_order = propagators.shape[1]
-    chosen = source_elementals(own_elemental, src_times)
+    pieces = source_pieces(own_elemental, src_times)
+    rows = pieces[0][1].shape[1]
+    halves = jnp.zeros((NSRC, block_order, block_order), jnp.bfloat16)
+    for origin, piece in pieces:
+        block = jnp.einsum(
+            "sik,sjk->sij", piece, propagators, preferred_element_type=jnp.float32
+        ).astype(jnp.bfloat16)
+        halves = lax.dynamic_update_slice_in_dim(halves, block, origin * rows, 1)
     summed = jnp.zeros((block_order, block_order), jnp.float32)
     for source in range(NSRC):
-        half_product = lax.dot_general(
-            chosen[source],
-            propagators[source],
-            (((1,), (1,)), ((), ())),
-            preferred_element_type=jnp.float32,
-        ).astype(jnp.bfloat16)
         summed = summed + jnp.dot(
-            propagators[source], half_product, preferred_element_type=jnp.float32
+            propagators[source], halves[source], preferred_element_type=jnp.float32
         )
     meson = summed.astype(jnp.bfloat16)
 

time: 358 us -> 236 us (0.66); the launches traced: 358 us -> 232 us
  waiting for transfers between devices: 257 us -> 122 us
  starting transfers between devices: 27.1 us -> 42.6 us
  between operations: 14.1 us -> 1.31 us
    all_gather x1 -> x0, waiting for transfers between devices: 169 us -> none  [source_elementals(): gathered = lax.all_gather(chosen, 'tsink', axis=1, tiled=True)]
    ppermute x0 -> x9, waiting for transfers between devices: none -> 33.7 us  [the longest x8 33.7 us: shifted(): return lax.ppermute(block, 'tsink', pairs)]
    ppermute x0 -> x9, starting transfers between devices: none -> 11.4 us  [the longest x8 11.4 us: shifted(): return lax.ppermute(block, 'tsink', pairs)]
    all_to_all x1, starting transfers between devices: 7.56 us -> 11.8 us  [body(): received = lax.all_to_all(slices, 'mom', 0, 0)]
    dot_general x4 -> x12, matrix products: 39.2 us -> 42.4 us  [the longest x8 25 us: body(): jnp.einsum('sik,sjk->sij', piece, propagators, preferred_element_type=jnp...]
  transfers between devices with their start and end apart: 4 -> 12, of which waited for: 4 -> 6; matrix products, arithmetic and copies ran while one was open for 1% -> 11% of each run, Pallas kernels for 0% -> 0%
where the time goes in v3:
time: 236 us; the launch traced here: 232 us
  waiting for transfers between devices  122 us (52%)
  matrix products  46.9 us (20%)
  starting transfers between devices  42.6 us (18%)
  local copies, waits for them, and re-layouts  16.4 us (7%)
  other arithmetic  2.54 us (1%)
    all_to_all x1, waiting for transfers between devices, body(): received = lax.all_to_all(slices, 'mom', 0, 0)  53.1 us
    ppermute x8, waiting for transfers between devices, shifted(): return lax.ppermute(block, 'tsink', pairs)  33.7 us
    all_to_all x1, waiting for transfers between devices, source_pieces(): received = lax.all_to_all(pieces, 'tsink', 0, 0)  30.6 us
    dot_general x8, matrix products, body(): jnp.einsum('sik,sjk->sij', piece, propagators, preferred_element_type=jnp...  25 us
    dot_general x4, matrix products, body(): jnp.dot(propagators[source], halves[source], preferred_element_type=jnp.f...  17.4 us
    all_to_all x1, starting transfers between devices, body(): spread = lax.all_to_all(per_diagram.reshape(n_m, -1), 'mom', 0, 0)  13.3 us
    all_to_all x1, starting transfers between devices, body(): received = lax.all_to_all(slices, 'mom', 0, 0)  11.8 us
    ppermute x8, starting transfers between devices, shifted(): return lax.ppermute(block, 'tsink', pairs)  11.4 us
  transfers between devices with their start and end apart: 12, of which 6 were waited for; matrix products, arithmetic and copies ran while one was open for 11% of the time, Pallas kernels for 0%

profile of v3, /device:TPU:1, one launch (start us, length us, event | category | flops | bytes accessed | tf_op | source)
XLA Modules:
  0.0 231.6 jit_solution(1848621002748705968)
XLA Ops:
  0.6 6.2 %all-to-all-start = ((bf16[8,128,1024]{2,1,0:T(8,128)(2,1)}), bf16[8,128,1024]{2,1,0:T(8,128)(2,1)S(1)}, u32[]{:S(2)}, u32[]{:S(2)}) async-start(bf16[8,128,1024]{2,1,0:T(8,128)(2,1)} %bitcast.110), calls=%async_computation | async-start | bytes 4194304 | tf_op jit(solution)/shard_map/all_to_all | solution.py:24
  6.9 30.6 %all-to-all-done = bf16[8,128,1024]{2,1,0:T(8,128)(2,1)S(1)} async-done(((bf16[8,128,1024]{2,1,0:T(8,128)(2,1)}), bf16[8,128,1024]{2,1,0:T(8,128)(2,1)S(1)}, u32[]{:S(2)}, u32[]{:S(2)}) %all-to-all-start) | async-done | bytes 2097184 | tf_op jit(solution)/shard_map/all_to_all | solution.py:24
  37.5 0.6 gather_fusion
  38.1 0.1 collective-permute-start.1
  38.2 2.7 %collective-permute-start.2 = (bf16[4,128,1024]{2,1,0:T(8,128)(2,1)S(1)}, bf16[4,128,1024]{2,1,0:T(8,128)(2,1)S(1)}, u32[]{:S(2)}, u32[]{:S(2)}) collective-permute-start(bf16[4,128,1024]{2,1,0:T(8,128)(2,1)S(1)} %gather_fusion), channel_id=1, source_target_pairs={{0,96},{16,112},{32,0},{48,16},{64,32},{80,48},{96,64},{112,80},{1... | collective-permute-start | bytes 3145736 | tf_op jit(solution)/shard_map/ppermute | solution.py:11
  40.8 0.0 collective-permute-start
  40.8 1.1 broadcast_in_dim.12
  41.9 2.3 copy-done
  44.2 3.0 %fusion.74 = bf16[4,1024,1024]{2,1,0:T(8,128)(2,1)S(1)} fusion(bf16[4,1024,1024]{2,1,0:T(8,128)(2,1)S(1)} %broadcast_in_dim.12, s32[]{:T(128)S(6)} %select_n.57, bf16[4,128,1024]{2,1,0:T(8,128)(2,1)S(1)} %gather_fusion, bf16[1,4,1024,1024]{3,2,1,0:T(8,128)(2,1)S(1)} %copy-done), kind=kOutput, calls=%fused_computation.54 | convolution fusion | flops 1074266112 | bytes 10485764 | tf_op jit(solution)/shard_map/sik,sjk->sij/dot_general | solution.py:60
  47.2 15.3 %collective-permute-done.1 = bf16[4,128,1024]{2,1,0:T(8,128)(2,1)S(1)} collective-permute-done((bf16[4,128,1024]{2,1,0:T(8,128)(2,1)S(1)}, bf16[4,128,1024]{2,1,0:T(8,128)(2,1)S(1)}, u32[]{:S(2)}, u32[]{:S(2)}) %collective-permute-start.1) | collective-permute-done | bytes 1048608 | tf_op jit(solution)/shard_map/ppermute | solution.py:11
  62.5 0.1 collective-permute-start.3
  62.6 0.0 collective-permute-done.2
  62.7 2.7 %collective-permute-start.4 = (bf16[4,64,1024]{2,1,0:T(8,128)(2,1)S(1)}, bf16[4,64,1024]{2,1,0:T(8,128)(2,1)S(1)}, u32[]{:S(2)}, u32[]{:S(2)}) collective-permute-start(bf16[4,64,1024]{2,1,0:T(8,128)(2,1)S(1)} %slice.73), channel_id=1, source_target_pairs={{0,96},{16,112},{32,0},{48,16},{64,32},{80,48},{96,64},{112,80},{1... | collective-permute-start | bytes 1572872 | tf_op jit(solution)/shard_map/ppermute | solution.py:11
  65.4 0.0 collective-permute-done
  65.4 0.0 collective-permute-start.5
  65.4 2.8 %collective-permute-start.6 = (bf16[4,128,1024]{2,1,0:T(8,128)(2,1)}, bf16[4,128,1024]{2,1,0:T(8,128)(2,1)S(1)}, u32[]{:S(2)}, u32[]{:S(2)}) collective-permute-start(bf16[4,128,1024]{2,1,0:T(8,128)(2,1)} %collective-permute-done), channel_id=1, source_target_pairs={{0,96},{16,112},{32,0},{48,16},{64,32},{80,48},{96,64},{112,80},{1... | collective-permute-start | bytes 3145736 | tf_op jit(solution)/shard_map/ppermute | solution.py:11
  68.2 4.3 %fusion.71 = bf16[4,1024,1024]{2,1,0:T(8,128)(2,1)S(1)} fusion(bf16[4,1024,1024]{2,1,0:T(8,128)(2,1)S(1)} %fusion.74, s32[]{:T(128)S(6)} %select_n.58, bf16[4,128,1024]{2,1,0:T(8,128)(2,1)} %collective-permute-done, bf16[1,4,1024,1024]{3,2,1,0:T(8,128)(2,1)S(1)} %copy-done), kind=kOutput, calls=%fused_computation.53 | convolution fusion | flops 1074266112 | bytes 10485764 | tf_op jit(solution)/shard_map/sik,sjk->sij/dot_general | solution.py:60
  72.5 3.0 %fusion.68 = bf16[4,1024,1024]{2,1,0:T(8,128)(2,1)S(1)} fusion(bf16[4,1024,1024]{2,1,0:T(8,128)(2,1)S(1)} %fusion.71, s32[]{:T(128)S(6)} %select_n.60, bf16[4,128,1024]{2,1,0:T(8,128)(2,1)S(1)} %collective-permute-done.1, bf16[1,4,1024,1024]{3,2,1,0:T(8,128)(2,1)S(1)} %copy-done), kind=kOutput, calls=%fused_computation.52 | convolution fusion | flops 1074266112 | bytes 10485764 | tf_op jit(solution)/shard_map/sik,sjk->sij/dot_general | solution.py:60
  75.5 3.0 %fusion.65 = bf16[4,1024,1024]{2,1,0:T(8,128)(2,1)S(1)} fusion(bf16[4,1024,1024]{2,1,0:T(8,128)(2,1)S(1)} %fusion.68, s32[]{:T(128)S(6)} %select_n.62, bf16[4,128,1024]{2,1,0:T(8,128)(2,1)S(1)} %collective-permute-done.2, bf16[1,4,1024,1024]{3,2,1,0:T(8,128)(2,1)S(1)} %copy-done), kind=kOutput, calls=%fused_computation.51 | convolution fusion | flops 1074266112 | bytes 10485764 | tf_op jit(solution)/shard_map/sik,sjk->sij/dot_general | solution.py:60
  78.5 0.0 collective-permute-done.3
  78.5 0.0 collective-permute-done.4
  78.5 2.9 %fusion.62 = bf16[4,1024,1024]{2,1,0:T(8,128)(2,1)S(1)} fusion(bf16[4,1024,1024]{2,1,0:T(8,128)(2,1)S(1)} %fusion.65, s32[]{:T(128)S(6)} %select_n.64, bf16[1,4,1024,1024]{3,2,1,0:T(8,128)(2,1)S(1)} %copy-done, bf16[4,64,1024]{2,1,0:T(8,128)(2,1)S(1)} %collective-permute-done.4, bf16[4,64,1024]{2,1,0:T(8,128)(2,1)S(1)} %collective-permute-done.3), kind=kOutput, calls=%fused_computation.50 | convolution fusion | flops 1076363264 | bytes 10485764 | tf_op jit(solution)/shard_map/sik,sjk->sij/dot_general | solution.py:60
  81.4 15.9 %collective-permute-done.5 = bf16[4,128,1024]{2,1,0:T(8,128)(2,1)S(1)} collective-permute-done((bf16[4,128,1024]{2,1,0:T(8,128)(2,1)}, bf16[4,128,1024]{2,1,0:T(8,128)(2,1)S(1)}, u32[]{:S(2)}, u32[]{:S(2)}) %collective-permute-start.5) | collective-permute-done | bytes 1048608 | tf_op jit(solution)/shard_map/ppermute | solution.py:11
  97.4 0.1 collective-permute-start.7
  97.5 0.0 collective-permute-done.6
  97.5 2.9 %collective-permute-start.8 = (bf16[4,64,1024]{2,1,0:T(8,128)(2,1)S(1)}, bf16[4,64,1024]{2,1,0:T(8,128)(2,1)S(1)}, u32[]{:S(2)}, u32[]{:S(2)}) collective-permute-start(bf16[4,64,1024]{2,1,0:T(8,128)(2,1)S(1)} %slice.75), channel_id=1, source_target_pairs={{0,96},{16,112},{32,0},{48,16},{64,32},{80,48},{96,64},{112,80},{1... | collective-permute-start | bytes 1572872 | tf_op jit(solution)/shard_map/ppermute | solution.py:11
  100.5 3.0 %fusion.59 = bf16[4,1024,1024]{2,1,0:T(8,128)(2,1)S(1)} fusion(bf16[4,1024,1024]{2,1,0:T(8,128)(2,1)S(1)} %fusion.62, s32[]{:T(128)S(6)} %select_n.65, bf16[4,128,1024]{2,1,0:T(8,128)(2,1)S(1)} %collective-permute-done.5, bf16[1,4,1024,1024]{3,2,1,0:T(8,128)(2,1)S(1)} %copy-done), kind=kOutput, calls=%fused_computation.49 | convolution fusion | flops 1074266112 | bytes 10485764 | tf_op jit(solution)/shard_map/sik,sjk->sij/dot_general | solution.py:60
  103.5 2.9 %fusion.56 = bf16[4,1024,1024]{2,1,0:T(8,128)(2,1)S(1)} fusion(bf16[4,1024,1024]{2,1,0:T(8,128)(2,1)S(1)} %fusion.59, s32[]{:T(128)S(6)} %select_n.66, bf16[4,128,1024]{2,1,0:T(8,128)(2,1)S(1)} %collective-permute-done.6, bf16[1,4,1024,1024]{3,2,1,0:T(8,128)(2,1)S(1)} %copy-done), kind=kOutput, calls=%fused_computation.48 | convolution fusion | flops 1074266112 | bytes 10485764 | tf_op jit(solution)/shard_map/sik,sjk->sij/dot_general | solution.py:60
  106.4 2.5 %collective-permute-done.7 = bf16[4,64,1024]{2,1,0:T(8,128)(2,1)S(1)} collective-permute-done((bf16[4,64,1024]{2,1,0:T(8,128)(2,1)S(1)}, bf16[4,64,1024]{2,1,0:T(8,128)(2,1)S(1)}, u32[]{:S(2)}, u32[]{:S(2)}) %collective-permute-start.7) | collective-permute-done | bytes 524320 | tf_op jit(solution)/shard_map/ppermute | solution.py:11
  108.9 0.0 collective-permute-done.8
  108.9 3.0 %fusion.53 = bf16[4,1024,1024]{2,1,0:T(8,128)(2,1)S(1)} fusion(bf16[4,1024,1024]{2,1,0:T(8,128)(2,1)S(1)} %fusion.56, s32[]{:T(128)S(6)} %select_n.67, bf16[1,4,1024,1024]{3,2,1,0:T(8,128)(2,1)S(1)} %copy-done, bf16[4,64,1024]{2,1,0:T(8,128)(2,1)S(1)} %collective-permute-done.8, bf16[4,64,1024]{2,1,0:T(8,128)(2,1)S(1)} %collective-permute-done.7), kind=kOutput, calls=%fused_computation.47 | convolution fusion | flops 1076363264 | bytes 10485764 | tf_op jit(solution)/shard_map/sik,sjk->sij/dot_general | solution.py:60
  111.9 2.4 %fusion.16 = f32[1024,1024]{1,0:T(8,128)S(1)} fusion(bf16[4,1024,1024]{2,1,0:T(8,128)(2,1)S(1)} %fusion.53, bf16[1,4,1024,1024]{3,2,1,0:T(8,128)(2,1)S(1)} %copy-done), kind=kOutput, calls=%fused_computation.21 | convolution fusion | flops 2147483648 | bytes 8388608 | tf_op jit(solution)/shard_map/dot_general | solution.py:66
  114.3 4.4 %fusion.17 = f32[1024,1024]{1,0:T(8,128)} fusion(bf16[4,1024,1024]{2,1,0:T(8,128)(2,1)S(1)} %fusion.53, bf16[1,4,1024,1024]{3,2,1,0:T(8,128)(2,1)S(1)} %copy-done), kind=kOutput, calls=%fused_computation.23 | convolution fusion | flops 2147483648 | bytes 8388608 | tf_op jit(solution)/shard_map/dot_general | solution.py:66
  118.6 4.7 %fusion.18 = f32[1024,1024]{1,0:T(8,128)} fusion(bf16[4,1024,1024]{2,1,0:T(8,128)(2,1)S(1)} %fusion.53, bf16[1,4,1024,1024]{3,2,1,0:T(8,128)(2,1)S(1)} %copy-done), kind=kOutput, calls=%fused_computation.25 | convolution fusion | flops 2147483648 | bytes 8388608 | tf_op jit(solution)/shard_map/dot_general | solution.py:66
  123.3 6.0 %add_convert_fusion = bf16[1024,1024]{1,0:T(8,128)(2,1)S(1)} fusion(f32[1024,1024]{1,0:T(8,128)S(1)} %fusion.16, f32[1024,1024]{1,0:T(8,128)} %fusion.17, f32[1024,1024]{1,0:T(8,128)} %fusion.18, bf16[1,4,1024,1024]{3,2,1,0:T(8,128)(2,1)S(1)} %copy-done, bf16[4,1024,1024]{2,1,0:T(8,128)(2,1)S(1)} %fusion.53), kind=kOutput, calls=%fused_computation.19 | convolution fusion | flops 2151677952 | bytes 18874368 | tf_op jit(solution)/shard_map/dot_general | solution.py:66
  129.3 2.6 %copy.13 = bf16[1024,1024]{1,0:T(8,128)(2,1)} copy(bf16[1024,1024]{0,1:T(8,128)(2,1)S(1)} %bitcast.106) | data formatting | bytes 4194304 | tf_op jit(solution)/shard_map/convert_element_type | solution.py:69
  131.8 2.0 pad_maximum_fusion
  133.8 2.4 %copy.14 = bf16[16,2,64,1024]{3,2,1,0:T(8,128)(2,1)} copy(bf16[16,2,64,1024]{3,2,0,1:T(8,128)(2,1)S(1)} %pad_maximum_fusion) | data formatting | bytes 8388608 | tf_op jit(solution)/shard_map/stack | solution.py:73
  136.2 11.8 %all-to-all-start.1 = ((bf16[16,2,64,1024]{3,2,1,0:T(8,128)(2,1)}), bf16[16,2,64,1024]{3,2,1,0:T(8,128)(2,1)}, u32[]{:S(2)}, u32[]{:S(2)}) async-start(bf16[16,2,64,1024]{3,2,1,0:T(8,128)(2,1)} %copy.14), calls=%async_computation.1 | async-start | bytes 8388608 | tf_op jit(solution)/shard_map/all_to_all | solution.py:77
  148.0 53.1 %all-to-all-done.1 = bf16[16,2,64,1024]{3,2,1,0:T(8,128)(2,1)} async-done(((bf16[16,2,64,1024]{3,2,1,0:T(8,128)(2,1)}), bf16[16,2,64,1024]{3,2,1,0:T(8,128)(2,1)}, u32[]{:S(2)}, u32[]{:S(2)}) %all-to-all-start.1) | async-done | bytes 4194336 | tf_op jit(solution)/shard_map/all_to_all | solution.py:77
  201.1 2.7 %fusion.94 = (bf16[16,1,64,1024]{3,2,1,0:T(8,128)(2,1)S(1)}, bf16[16,1,64,1024]{3,2,1,0:T(8,128)(2,1)S(1)}) fusion(bf16[16,2,64,1024]{3,2,1,0:T(8,128)(2,1)} %all-to-all-done.1), kind=kLoop, calls=%fused_computation.75 | loop fusion | bytes 8388608 | tf_op jit(solution)/shard_map/slice | solution.py:78
  203.8 4.4 %fusion.79 = f32[16,16]{1,0:T(8,128)S(1)} fusion(bf16[16,1,64,1024]{3,2,1,0:T(8,128)(2,1)S(1)} %get-tuple-element.9, bf16[16,1,64,1024]{3,2,1,0:T(8,128)(2,1)S(1)} %get-tuple-element.8), kind=kOutput, calls=%fused_computation.55 | convolution fusion | flops 33554432 | bytes 4195328 | tf_op jit(solution)/shard_map/dot_general | solution.py:80
  208.3 1.3 gather_fusion.1
  209.6 0.7 all_to_all.14
  210.2 13.3 %all-to-all-start.2 = ((f32[16,1,8]{2,1,0:T(1,128)}), f32[16,1,8]{2,1,0:T(1,128)S(1)}, u32[]{:S(2)}, u32[]{:S(2)}) async-start(f32[16,1,8]{2,1,0:T(1,128)} %bitcast.18), calls=%async_computation.2 | async-start | bytes 16384 | tf_op jit(solution)/shard_map/all_to_all | solution.py:84
  223.6 2.6 %copy.18 = bf16[1,1,1024,1024]{3,2,1,0:T(8,128)(2,1)} copy(bf16[1,1,1024,1024]{2,3,1,0:T(8,128)(2,1)S(1)} %bitcast.108) | data formatting | bytes 4194304
  226.1 4.5 %all-to-all-done.2 = f32[16,1,8]{2,1,0:T(1,128)S(1)} async-done(((f32[16,1,8]{2,1,0:T(1,128)}), f32[16,1,8]{2,1,0:T(1,128)S(1)}, u32[]{:S(2)}, u32[]{:S(2)}) %all-to-all-start.2) | async-done | bytes 544 | tf_op jit(solution)/shard_map/all_to_all | solution.py:84
  230.6 0.5 multiply_bitcast_fusion
  (13 shorter events, 0.2 us)
Async XLA Ops:
  0.6 6.2 %copy-start.2 = (s32[4]{0:T(128)S(1)}, s32[4]{0:T(128)}, u32[]{:S(2)}) copy-start(s32[4]{0:T(128)} %param.6) | copy-start | bytes 52
  0.6 36.8 %all-to-all-start = ((bf16[8,128,1024]{2,1,0:T(8,128)(2,1)}), bf16[8,128,1024]{2,1,0:T(8,128)(2,1)S(1)}, u32[]{:S(2)}, u32[]{:S(2)}) async-start(bf16[8,128,1024]{2,1,0:T(8,128)(2,1)} %bitcast.110), calls=%async_computation | async-start | bytes 4194304 | tf_op jit(solution)/shard_map/all_to_all | solution.py:24
  38.1 24.4 %collective-permute-start.1 = (bf16[4,128,1024]{2,1,0:T(8,128)(2,1)S(1)}, bf16[4,128,1024]{2,1,0:T(8,128)(2,1)S(1)}, u32[]{:S(2)}, u32[]{:S(2)}) collective-permute-start(bf16[4,128,1024]{2,1,0:T(8,128)(2,1)S(1)} %gather_fusion), channel_id=1, source_target_pairs={{0,32},{16,48},{32,64},{48,80},{64,96},{80,112},{96,0},{112,16},{1... | collective-permute-start | bytes 3145736 | tf_op jit(solution)/shard_map/ppermute | solution.py:11
  38.2 24.5 %collective-permute-start.2 = (bf16[4,128,1024]{2,1,0:T(8,128)(2,1)S(1)}, bf16[4,128,1024]{2,1,0:T(8,128)(2,1)S(1)}, u32[]{:S(2)}, u32[]{:S(2)}) collective-permute-start(bf16[4,128,1024]{2,1,0:T(8,128)(2,1)S(1)} %gather_fusion), channel_id=1, source_target_pairs={{0,96},{16,112},{32,0},{48,16},{64,32},{80,48},{96,64},{112,80},{1... | collective-permute-start | bytes 3145736 | tf_op jit(solution)/shard_map/ppermute | solution.py:11
  40.8 24.6 %collective-permute-start = (bf16[4,128,1024]{2,1,0:T(8,128)(2,1)S(1)}, bf16[4,128,1024]{2,1,0:T(8,128)(2,1)}, u32[]{:S(2)}, u32[]{:S(2)}) collective-permute-start(bf16[4,128,1024]{2,1,0:T(8,128)(2,1)S(1)} %gather_fusion), channel_id=1, source_target_pairs={{0,16},{16,0},{32,48},{48,32},{64,80},{80,64},{96,112},{112,96},{1... | collective-permute-start | bytes 3145736 | tf_op jit(solution)/shard_map/ppermute | solution.py:15
  40.8 3.4 %copy-start = (bf16[1,4,1024,1024]{3,2,1,0:T(8,128)(2,1)S(1)}, bf16[1,4,1024,1024]{3,2,1,0:T(8,128)(2,1)}, u32[]{:S(2)}) copy-start(bf16[1,4,1024,1024]{3,2,1,0:T(8,128)(2,1)} %param.4) | copy-start | bytes 25165828
  62.5 16.0 %collective-permute-start.3 = (bf16[4,64,1024]{2,1,0:T(8,128)(2,1)S(1)}, bf16[4,64,1024]{2,1,0:T(8,128)(2,1)S(1)}, u32[]{:S(2)}, u32[]{:S(2)}) collective-permute-start(bf16[4,64,1024]{2,1,0:T(8,128)(2,1)S(1)} %slice.72), channel_id=1, source_target_pairs={{0,32},{16,48},{32,64},{48,80},{64,96},{80,112},{96,0},{112,16},{1... | collective-permute-start | bytes 1572872 | tf_op jit(solution)/shard_map/ppermute | solution.py:11
  62.7 15.8 %collective-permute-start.4 = (bf16[4,64,1024]{2,1,0:T(8,128)(2,1)S(1)}, bf16[4,64,1024]{2,1,0:T(8,128)(2,1)S(1)}, u32[]{:S(2)}, u32[]{:S(2)}) collective-permute-start(bf16[4,64,1024]{2,1,0:T(8,128)(2,1)S(1)} %slice.73), channel_id=1, source_target_pairs={{0,96},{16,112},{32,0},{48,16},{64,32},{80,48},{96,64},{112,80},{1... | collective-permute-start | bytes 1572872 | tf_op jit(solution)/shard_map/ppermute | solution.py:11
  65.4 31.9 %collective-permute-start.5 = (bf16[4,128,1024]{2,1,0:T(8,128)(2,1)}, bf16[4,128,1024]{2,1,0:T(8,128)(2,1)S(1)}, u32[]{:S(2)}, u32[]{:S(2)}) collective-permute-start(bf16[4,128,1024]{2,1,0:T(8,128)(2,1)} %collective-permute-done), channel_id=1, source_target_pairs={{0,32},{16,48},{32,64},{48,80},{64,96},{80,112},{96,0},{112,16},{1... | collective-permute-start | bytes 3145736 | tf_op jit(solution)/shard_map/ppermute | solution.py:11
  65.4 32.1 %collective-permute-start.6 = (bf16[4,128,1024]{2,1,0:T(8,128)(2,1)}, bf16[4,128,1024]{2,1,0:T(8,128)(2,1)S(1)}, u32[]{:S(2)}, u32[]{:S(2)}) collective-permute-start(bf16[4,128,1024]{2,1,0:T(8,128)(2,1)} %collective-permute-done), channel_id=1, source_target_pairs={{0,96},{16,112},{32,0},{48,16},{64,32},{80,48},{96,64},{112,80},{1... | collective-permute-start | bytes 3145736 | tf_op jit(solution)/shard_map/ppermute | solution.py:11
  97.4 11.5 %collective-permute-start.7 = (bf16[4,64,1024]{2,1,0:T(8,128)(2,1)S(1)}, bf16[4,64,1024]{2,1,0:T(8,128)(2,1)S(1)}, u32[]{:S(2)}, u32[]{:S(2)}) collective-permute-start(bf16[4,64,1024]{2,1,0:T(8,128)(2,1)S(1)} %slice.74), channel_id=1, source_target_pairs={{0,32},{16,48},{32,64},{48,80},{64,96},{80,112},{96,0},{112,16},{1... | collective-permute-start | bytes 1572872 | tf_op jit(solution)/shard_map/ppermute | solution.py:11
  97.5 11.3 %collective-permute-start.8 = (bf16[4,64,1024]{2,1,0:T(8,128)(2,1)S(1)}, bf16[4,64,1024]{2,1,0:T(8,128)(2,1)S(1)}, u32[]{:S(2)}, u32[]{:S(2)}) collective-permute-start(bf16[4,64,1024]{2,1,0:T(8,128)(2,1)S(1)} %slice.75), channel_id=1, source_target_pairs={{0,96},{16,112},{32,0},{48,16},{64,32},{80,48},{96,64},{112,80},{1... | collective-permute-start | bytes 1572872 | tf_op jit(solution)/shard_map/ppermute | solution.py:11
  136.2 11.8 %copy-start.1 = (s32[128,2]{0,1:T(2,128)S(1)}, s32[128,2]{0,1:T(2,128)}, u32[]{:S(2)}) copy-start(s32[128,2]{0,1:T(2,128)} %param.7) | copy-start | bytes 3076
  136.2 64.9 %all-to-all-start.1 = ((bf16[16,2,64,1024]{3,2,1,0:T(8,128)(2,1)}), bf16[16,2,64,1024]{3,2,1,0:T(8,128)(2,1)}, u32[]{:S(2)}, u32[]{:S(2)}) async-start(bf16[16,2,64,1024]{3,2,1,0:T(8,128)(2,1)} %copy.14), calls=%async_computation.1 | async-start | bytes 8388608 | tf_op jit(solution)/shard_map/all_to_all | solution.py:77
  210.2 20.3 %all-to-all-start.2 = ((f32[16,1,8]{2,1,0:T(1,128)}), f32[16,1,8]{2,1,0:T(1,128)S(1)}, u32[]{:S(2)}, u32[]{:S(2)}) async-start(f32[16,1,8]{2,1,0:T(1,128)} %bitcast.18), calls=%async_computation.2 | async-start | bytes 16384 | tf_op jit(solution)/shard_map/all_to_all | solution.py:84

commit v4 on v3

--- a/solution.py
+++ b/solution.py
@@ -69,17 +69,32 @@
     meson = summed.astype(jnp.bfloat16)
 
     n_m = lax.axis_size("mom")
-    rows = block_order // n_m
+    width = 128
+    upper, upper_t, weights = [], [], []
+    transposed = meson.T
+    for col in range(block_order // width):
+        height = width * (col + 1)
+        upper.append(meson[:height, col * width:(col + 1) * width])
+        upper_t.append(transposed[:height, col * width:(col + 1) * width])
+        row_index = lax.broadcasted_iota(jnp.int32, (height, width), 0)
+        col_index = lax.broadcasted_iota(jnp.int32, (height, width), 1) + col * width
+        weights.append(
+            jnp.where(row_index < col_index, 1.0, jnp.where(row_index == col_index, 0.5, 0.0))
+        )
+    weight = jnp.concatenate(weights, axis=0).astype(jnp.bfloat16)
+    upper = jnp.concatenate(upper, axis=0) * weight
+    upper_t = jnp.concatenate(upper_t, axis=0)
+    share = upper.shape[0] // n_m
     slices = jnp.stack(
-        [meson.reshape(n_m, rows, block_order), meson.T.reshape(n_m, rows, block_order)],
-        axis=1,
+        [upper.reshape(n_m, share, width), upper_t.reshape(n_m, share, width)], axis=1
     )
     received = lax.all_to_all(slices, "mom", 0, 0)
-    own_rows = received[:, 0].reshape(n_m, rows * block_order)
-    own_cols = received[:, 1].reshape(n_m, rows * block_order)
+    own_rows = received[:, 0].reshape(n_m, share * width)
+    own_cols = received[:, 1].reshape(n_m, share * width)
     partial = lax.dot_general(
         own_rows, own_cols, (((1,), (1,)), ((), ())), preferred_element_type=jnp.float32
     )
+    partial = partial + partial.T
     per_diagram = partial[diagrams[:, 0], diagrams[:, 1]]
     spread = lax.all_to_all(per_diagram.reshape(n_m, -1), "mom", 0, 0)
     correlators = (jnp.sum(spread, axis=0) / block_order)[:, None]

time: 236 us -> 204 us (0.86); the launches traced: 232 us -> 204 us
  waiting for transfers between devices: 122 us -> 93.7 us
  other arithmetic: 2.54 us -> 9.98 us
  starting transfers between devices: 42.6 us -> 35.7 us
  local copies, waits for them, and re-layouts: 16.4 us -> 19.3 us
  matrix products: 46.9 us -> 44 us
    all_to_all x1, waiting for transfers between devices: 53.1 us -> 31.2 us  [body(): received = lax.all_to_all(slices, 'mom', 0, 0)]
    all_to_all x1, starting transfers between devices: 13.3 us -> 6.53 us  [body(): spread = lax.all_to_all(per_diagram.reshape(n_m, -1), 'mom', 0, 0)]
    unnamed x0 -> x7, other arithmetic: none -> 5.47 us
    unnamed x7 -> x23, local copies, waits for them, and re-layouts: 4.88 us -> 9.82 us
    all_to_all x1, waiting for transfers between devices: 30.6 us -> 26.7 us  [source_pieces(): received = lax.all_to_all(pieces, 'tsink', 0, 0)]
    dot_general x1, matrix products: 4.43 us -> 0.73 us  [body(): lax.dot_general(own_rows, own_cols, (((1,), (1,)), ((), ())), preferred_e...]
    convert_element_type x1 -> x0, local copies, waits for them, and re-layouts: 2.56 us -> none  [body(): meson = summed.astype(jnp.bfloat16)]
  transfers between devices with their start and end apart: 12 -> 12, of which waited for: 6 -> 6; matrix products, arithmetic and copies ran while one was open for 11% -> 16% of each run, Pallas kernels for 0% -> 0%
where the time goes in v4:
time: 204 us
  waiting for transfers between devices  93.7 us (46%)
  matrix products  44 us (22%)
  starting transfers between devices  35.7 us (18%)
  local copies, waits for them, and re-layouts  19.3 us (9%)
  other arithmetic  9.98 us (5%)
    ppermute x8, waiting for transfers between devices, shifted(): return lax.ppermute(block, 'tsink', pairs)  31.4 us
    all_to_all x1, waiting for transfers between devices, body(): received = lax.all_to_all(slices, 'mom', 0, 0)  31.2 us
    all_to_all x1, waiting for transfers between devices, source_pieces(): received = lax.all_to_all(pieces, 'tsink', 0, 0)  26.7 us
    dot_general x8, matrix products, body(): jnp.einsum('sik,sjk->sij', piece, propagators, preferred_element_type=jnp...  25.8 us
    dot_general x4, matrix products, body(): jnp.dot(propagators[source], halves[source], preferred_element_type=jnp.f...  17.5 us
    all_to_all x1, starting transfers between devices, body(): received = lax.all_to_all(slices, 'mom', 0, 0)  11.8 us
    ppermute x8, starting transfers between devices, shifted(): return lax.ppermute(block, 'tsink', pairs)  11.2 us
    unnamed x23, local copies, waits for them, and re-layouts  9.82 us
  transfers between devices with their start and end apart: 12, of which 6 were waited for; matrix products, arithmetic and copies ran while one was open for 16% of the time, Pallas kernels for 0%

profile of v4, /device:TPU:1, one launch (start us, length us, event | category | flops | bytes accessed | tf_op | source)
XLA Modules:
  0.0 203.7 jit_solution(11746726184944080716)
XLA Ops:
  0.6 6.2 %all-to-all-start = ((bf16[8,128,1024]{2,1,0:T(8,128)(2,1)}), bf16[8,128,1024]{2,1,0:T(8,128)(2,1)S(1)}, u32[]{:S(2)}, u32[]{:S(2)}) async-start(bf16[8,128,1024]{2,1,0:T(8,128)(2,1)} %bitcast.118), calls=%async_computation | async-start | bytes 4194304 | tf_op jit(solution)/shard_map/all_to_all | solution.py:24
  7.6 0.7 fusion.92
  8.4 0.8 fusion.91
  9.1 0.8 fusion.90
  9.9 0.9 fusion.89
  10.8 26.7 %all-to-all-done = bf16[8,128,1024]{2,1,0:T(8,128)(2,1)S(1)} async-done(((bf16[8,128,1024]{2,1,0:T(8,128)(2,1)}), bf16[8,128,1024]{2,1,0:T(8,128)(2,1)S(1)}, u32[]{:S(2)}, u32[]{:S(2)}) %all-to-all-start) | async-done | bytes 2097184 | tf_op jit(solution)/shard_map/all_to_all | solution.py:24
  38.2 2.7 %collective-permute-start.2 = (bf16[4,128,1024]{2,1,0:T(8,128)(2,1)S(1)}, bf16[4,128,1024]{2,1,0:T(8,128)(2,1)S(1)}, u32[]{:S(2)}, u32[]{:S(2)}) collective-permute-start(bf16[4,128,1024]{2,1,0:T(8,128)(2,1)S(1)} %gather_fusion), channel_id=1, source_target_pairs={{0,96},{16,112},{32,0},{48,16},{64,32},{80,48},{96,64},{112,80},{1... | collective-permute-start | bytes 3145736 | tf_op jit(solution)/shard_map/ppermute | solution.py:11
  40.8 0.9 fusion.88
  41.7 0.8 fusion.87
  42.5 1.1 broadcast_in_dim.108
  43.6 2.3 %copy-done = bf16[1,4,1024,1024]{3,2,1,0:T(8,128)(2,1)S(1)} copy-done((bf16[1,4,1024,1024]{3,2,1,0:T(8,128)(2,1)S(1)}, bf16[1,4,1024,1024]{3,2,1,0:T(8,128)(2,1)}, u32[]{:S(2)}) %copy-start) | copy-done | bytes 8388632
  45.9 2.9 %fusion.73 = bf16[4,1024,1024]{2,1,0:T(8,128)(2,1)S(1)} fusion(bf16[4,1024,1024]{2,1,0:T(8,128)(2,1)S(1)} %broadcast_in_dim.108, s32[]{:T(128)S(6)} %select_n.121, bf16[4,128,1024]{2,1,0:T(8,128)(2,1)S(1)} %gather_fusion, bf16[1,4,1024,1024]{3,2,1,0:T(8,128)(2,1)S(1)} %copy-done), kind=kOutput, calls=%fused_computation.51 | convolution fusion | flops 1074266112 | bytes 10485764 | tf_op jit(solution)/shard_map/sik,sjk->sij/dot_general | solution.py:60
  48.8 13.7 %collective-permute-done.1 = bf16[4,128,1024]{2,1,0:T(8,128)(2,1)S(1)} collective-permute-done((bf16[4,128,1024]{2,1,0:T(8,128)(2,1)S(1)}, bf16[4,128,1024]{2,1,0:T(8,128)(2,1)S(1)}, u32[]{:S(2)}, u32[]{:S(2)}) %collective-permute-start.1) | collective-permute-done | bytes 1048608 | tf_op jit(solution)/shard_map/ppermute | solution.py:11
  62.7 2.7 %collective-permute-start.4 = (bf16[4,64,1024]{2,1,0:T(8,128)(2,1)S(1)}, bf16[4,64,1024]{2,1,0:T(8,128)(2,1)}, u32[]{:S(2)}, u32[]{:S(2)}) collective-permute-start(bf16[4,64,1024]{2,1,0:T(8,128)(2,1)S(1)} %slice.137), channel_id=1, source_target_pairs={{0,96},{16,112},{32,0},{48,16},{64,32},{80,48},{96,64},{112,80},{1... | collective-permute-start | bytes 1572872 | tf_op jit(solution)/shard_map/ppermute | solution.py:11
  65.4 2.7 %collective-permute-start.6 = (bf16[4,128,1024]{2,1,0:T(8,128)(2,1)}, bf16[4,128,1024]{2,1,0:T(8,128)(2,1)S(1)}, u32[]{:S(2)}, u32[]{:S(2)}) collective-permute-start(bf16[4,128,1024]{2,1,0:T(8,128)(2,1)} %collective-permute-done), channel_id=1, source_target_pairs={{0,96},{16,112},{32,0},{48,16},{64,32},{80,48},{96,64},{112,80},{1... | collective-permute-start | bytes 3145736 | tf_op jit(solution)/shard_map/ppermute | solution.py:11
  68.1 4.2 %fusion.70 = bf16[4,1024,1024]{2,1,0:T(8,128)(2,1)S(1)} fusion(bf16[4,1024,1024]{2,1,0:T(8,128)(2,1)S(1)} %fusion.73, s32[]{:T(128)S(6)} %select_n.122, bf16[4,128,1024]{2,1,0:T(8,128)(2,1)} %collective-permute-done, bf16[1,4,1024,1024]{3,2,1,0:T(8,128)(2,1)S(1)} %copy-done), kind=kOutput, calls=%fused_computation.50 | convolution fusion | flops 1074266112 | bytes 10485764 | tf_op jit(solution)/shard_map/sik,sjk->sij/dot_general | solution.py:60
  72.3 3.0 %fusion.67 = bf16[4,1024,1024]{2,1,0:T(8,128)(2,1)S(1)} fusion(bf16[4,1024,1024]{2,1,0:T(8,128)(2,1)S(1)} %fusion.70, s32[]{:T(128)S(6)} %select_n.124, bf16[4,128,1024]{2,1,0:T(8,128)(2,1)S(1)} %collective-permute-done.1, bf16[1,4,1024,1024]{3,2,1,0:T(8,128)(2,1)S(1)} %copy-done), kind=kOutput, calls=%fused_computation.49 | convolution fusion | flops 1074266112 | bytes 10485764 | tf_op jit(solution)/shard_map/sik,sjk->sij/dot_general | solution.py:60
  75.3 3.0 %fusion.64 = bf16[4,1024,1024]{2,1,0:T(8,128)(2,1)S(1)} fusion(bf16[4,1024,1024]{2,1,0:T(8,128)(2,1)S(1)} %fusion.67, s32[]{:T(128)S(6)} %select_n.126, bf16[4,128,1024]{2,1,0:T(8,128)(2,1)S(1)} %collective-permute-done.2, bf16[1,4,1024,1024]{3,2,1,0:T(8,128)(2,1)S(1)} %copy-done), kind=kOutput, calls=%fused_computation.48 | convolution fusion | flops 1074266112 | bytes 10485764 | tf_op jit(solution)/shard_map/sik,sjk->sij/dot_general | solution.py:60
  78.3 4.0 %fusion.61 = bf16[4,1024,1024]{2,1,0:T(8,128)(2,1)S(1)} fusion(bf16[4,1024,1024]{2,1,0:T(8,128)(2,1)S(1)} %fusion.64, s32[]{:T(128)S(6)} %select_n.128, bf16[1,4,1024,1024]{3,2,1,0:T(8,128)(2,1)S(1)} %copy-done, bf16[4,64,1024]{2,1,0:T(8,128)(2,1)} %collective-permute-done.4, bf16[4,64,1024]{2,1,0:T(8,128)(2,1)S(1)} %collective-permute-done.3), kind=kOutput, calls=%fused_computation.47 | convolution fusion | flops 1076363264 | bytes 10485764 | tf_op jit(solution)/shard_map/sik,sjk->sij/dot_general | solution.py:60
  82.3 15.1 %collective-permute-done.5 = bf16[4,128,1024]{2,1,0:T(8,128)(2,1)S(1)} collective-permute-done((bf16[4,128,1024]{2,1,0:T(8,128)(2,1)}, bf16[4,128,1024]{2,1,0:T(8,128)(2,1)S(1)}, u32[]{:S(2)}, u32[]{:S(2)}) %collective-permute-start.5) | collective-permute-done | bytes 1048608 | tf_op jit(solution)/shard_map/ppermute | solution.py:11
  97.5 2.9 %collective-permute-start.8 = (bf16[4,64,1024]{2,1,0:T(8,128)(2,1)S(1)}, bf16[4,64,1024]{2,1,0:T(8,128)(2,1)S(1)}, u32[]{:S(2)}, u32[]{:S(2)}) collective-permute-start(bf16[4,64,1024]{2,1,0:T(8,128)(2,1)S(1)} %slice.139), channel_id=1, source_target_pairs={{0,96},{16,112},{32,0},{48,16},{64,32},{80,48},{96,64},{112,80},{1... | collective-permute-start | bytes 1572872 | tf_op jit(solution)/shard_map/ppermute | solution.py:11
  100.5 2.9 %fusion.58 = bf16[4,1024,1024]{2,1,0:T(8,128)(2,1)S(1)} fusion(bf16[4,1024,1024]{2,1,0:T(8,128)(2,1)S(1)} %fusion.61, s32[]{:T(128)S(6)} %select_n.129, bf16[4,128,1024]{2,1,0:T(8,128)(2,1)S(1)} %collective-permute-done.5, bf16[1,4,1024,1024]{3,2,1,0:T(8,128)(2,1)S(1)} %copy-done), kind=kOutput, calls=%fused_computation.46 | convolution fusion | flops 1074266112 | bytes 10485764 | tf_op jit(solution)/shard_map/sik,sjk->sij/dot_general | solution.py:60
  103.4 2.9 %fusion.55 = bf16[4,1024,1024]{2,1,0:T(8,128)(2,1)S(1)} fusion(bf16[4,1024,1024]{2,1,0:T(8,128)(2,1)S(1)} %fusion.58, s32[]{:T(128)S(6)} %select_n.130, bf16[4,128,1024]{2,1,0:T(8,128)(2,1)S(1)} %collective-permute-done.6, bf16[1,4,1024,1024]{3,2,1,0:T(8,128)(2,1)S(1)} %copy-done), kind=kOutput, calls=%fused_computation.45 | convolution fusion | flops 1074266112 | bytes 10485764 | tf_op jit(solution)/shard_map/sik,sjk->sij/dot_general | solution.py:60
  106.3 2.6 %collective-permute-done.7 = bf16[4,64,1024]{2,1,0:T(8,128)(2,1)S(1)} collective-permute-done((bf16[4,64,1024]{2,1,0:T(8,128)(2,1)S(1)}, bf16[4,64,1024]{2,1,0:T(8,128)(2,1)S(1)}, u32[]{:S(2)}, u32[]{:S(2)}) %collective-permute-start.7) | collective-permute-done | bytes 524320 | tf_op jit(solution)/shard_map/ppermute | solution.py:11
  108.9 2.9 %fusion.52 = bf16[4,1024,1024]{2,1,0:T(8,128)(2,1)S(1)} fusion(bf16[4,1024,1024]{2,1,0:T(8,128)(2,1)S(1)} %fusion.55, s32[]{:T(128)S(6)} %select_n.131, bf16[1,4,1024,1024]{3,2,1,0:T(8,128)(2,1)S(1)} %copy-done, bf16[4,64,1024]{2,1,0:T(8,128)(2,1)S(1)} %collective-permute-done.8, bf16[4,64,1024]{2,1,0:T(8,128)(2,1)S(1)} %collective-permute-done.7), kind=kOutput, calls=%fused_computation.44 | convolution fusion | flops 1076363264 | bytes 10485764 | tf_op jit(solution)/shard_map/sik,sjk->sij/dot_general | solution.py:60
  111.8 2.4 %fusion.16 = f32[1024,1024]{1,0:T(8,128)S(1)} fusion(bf16[4,1024,1024]{2,1,0:T(8,128)(2,1)S(1)} %fusion.52, bf16[1,4,1024,1024]{3,2,1,0:T(8,128)(2,1)S(1)} %copy-done), kind=kOutput, calls=%fused_computation.21 | convolution fusion | flops 2147483648 | bytes 8388608 | tf_op jit(solution)/shard_map/dot_general | solution.py:66
  114.2 4.3 %fusion.17 = f32[1024,1024]{1,0:T(8,128)} fusion(bf16[4,1024,1024]{2,1,0:T(8,128)(2,1)S(1)} %fusion.52, bf16[1,4,1024,1024]{3,2,1,0:T(8,128)(2,1)S(1)} %copy-done), kind=kOutput, calls=%fused_computation.23 | convolution fusion | flops 2147483648 | bytes 8388608 | tf_op jit(solution)/shard_map/dot_general | solution.py:66
  118.5 4.7 %fusion.18 = f32[1024,1024]{1,0:T(8,128)} fusion(bf16[4,1024,1024]{2,1,0:T(8,128)(2,1)S(1)} %fusion.52, bf16[1,4,1024,1024]{3,2,1,0:T(8,128)(2,1)S(1)} %copy-done), kind=kOutput, calls=%fused_computation.25 | convolution fusion | flops 2147483648 | bytes 8388608 | tf_op jit(solution)/shard_map/dot_general | solution.py:66
  123.2 6.1 %add_convert_fusion = bf16[1024,1024]{1,0:T(8,128)(2,1)S(1)} fusion(f32[1024,1024]{1,0:T(8,128)S(1)} %fusion.16, f32[1024,1024]{1,0:T(8,128)} %fusion.17, f32[1024,1024]{1,0:T(8,128)} %fusion.18, bf16[1,4,1024,1024]{3,2,1,0:T(8,128)(2,1)S(1)} %copy-done, bf16[4,1024,1024]{2,1,0:T(8,128)(2,1)S(1)} %fusion.52), kind=kOutput, calls=%fused_computation.18 | convolution fusion | flops 2151677952 | bytes 18874368 | tf_op jit(solution)/shard_map/dot_general | solution.py:66
  130.1 0.9 fusion.86
  131.0 1.5 mul.45
  132.5 1.4 copy.15
  135.3 0.7 slice_dynamic-update-slice_fusion.8
  136.0 0.7 slice_dynamic-update-slice_fusion.6
  136.7 0.7 slice_dynamic-update-slice_fusion.4
  137.4 0.7 slice_dynamic-update-slice_fusion.2
  138.2 0.8 slice_dynamic-update-slice_fusion
  138.9 1.5 pad_maximum_fusion
  140.4 1.6 copy.16
  142.1 11.8 %all-to-all-start.1 = ((bf16[16,2,288,128]{3,2,1,0:T(8,128)(2,1)}), bf16[16,2,288,128]{3,2,1,0:T(8,128)(2,1)}, u32[]{:S(2)}, u32[]{:S(2)}) async-start(bf16[16,2,288,128]{3,2,1,0:T(8,128)(2,1)} %copy.16), calls=%async_computation.1 | async-start | bytes 4718592 | tf_op jit(solution)/shard_map/all_to_all | solution.py:91
  153.9 31.2 %all-to-all-done.1 = bf16[16,2,288,128]{3,2,1,0:T(8,128)(2,1)} async-done(((bf16[16,2,288,128]{3,2,1,0:T(8,128)(2,1)}), bf16[16,2,288,128]{3,2,1,0:T(8,128)(2,1)}, u32[]{:S(2)}, u32[]{:S(2)}) %all-to-all-start.1) | async-done | bytes 2359328 | tf_op jit(solution)/shard_map/all_to_all | solution.py:91
  185.1 1.8 fusion.101
  186.8 0.7 fusion.79
  187.7 1.3 gather_fusion.1
  188.9 0.7 all_to_all.14
  189.6 6.5 %all-to-all-start.2 = ((f32[16,1,8]{2,1,0:T(1,128)}), f32[16,1,8]{2,1,0:T(1,128)S(1)}, u32[]{:S(2)}, u32[]{:S(2)}) async-start(f32[16,1,8]{2,1,0:T(1,128)} %bitcast.19), calls=%async_computation.2 | async-start | bytes 16384 | tf_op jit(solution)/shard_map/all_to_all | solution.py:99
  196.2 2.6 %copy.21 = bf16[1,1,1024,1024]{3,2,1,0:T(8,128)(2,1)} copy(bf16[1,1,1024,1024]{2,3,1,0:T(8,128)(2,1)S(1)} %bitcast.116) | data formatting | bytes 4194304
  198.7 4.5 %all-to-all-done.2 = f32[16,1,8]{2,1,0:T(1,128)S(1)} async-done(((f32[16,1,8]{2,1,0:T(1,128)}), f32[16,1,8]{2,1,0:T(1,128)S(1)}, u32[]{:S(2)}, u32[]{:S(2)}) %all-to-all-start.2) | async-done | bytes 544 | tf_op jit(solution)/shard_map/all_to_all | solution.py:99
  (48 shorter events, 4.4 us)
Async XLA Ops:
  0.6 6.3 %copy-start.3 = (s32[4]{0:T(128)S(1)}, s32[4]{0:T(128)}, u32[]{:S(2)}) copy-start(s32[4]{0:T(128)} %param.6) | copy-start | bytes 52
  0.6 36.8 %all-to-all-start = ((bf16[8,128,1024]{2,1,0:T(8,128)(2,1)}), bf16[8,128,1024]{2,1,0:T(8,128)(2,1)S(1)}, u32[]{:S(2)}, u32[]{:S(2)}) async-start(bf16[8,128,1024]{2,1,0:T(8,128)(2,1)} %bitcast.118), calls=%async_computation | async-start | bytes 4194304 | tf_op jit(solution)/shard_map/all_to_all | solution.py:24
  38.1 24.4 %collective-permute-start.1 = (bf16[4,128,1024]{2,1,0:T(8,128)(2,1)S(1)}, bf16[4,128,1024]{2,1,0:T(8,128)(2,1)S(1)}, u32[]{:S(2)}, u32[]{:S(2)}) collective-permute-start(bf16[4,128,1024]{2,1,0:T(8,128)(2,1)S(1)} %gather_fusion), channel_id=1, source_target_pairs={{0,32},{16,48},{32,64},{48,80},{64,96},{80,112},{96,0},{112,16},{1... | collective-permute-start | bytes 3145736 | tf_op jit(solution)/shard_map/ppermute | solution.py:11
  38.2 24.5 %collective-permute-start.2 = (bf16[4,128,1024]{2,1,0:T(8,128)(2,1)S(1)}, bf16[4,128,1024]{2,1,0:T(8,128)(2,1)S(1)}, u32[]{:S(2)}, u32[]{:S(2)}) collective-permute-start(bf16[4,128,1024]{2,1,0:T(8,128)(2,1)S(1)} %gather_fusion), channel_id=1, source_target_pairs={{0,96},{16,112},{32,0},{48,16},{64,32},{80,48},{96,64},{112,80},{1... | collective-permute-start | bytes 3145736 | tf_op jit(solution)/shard_map/ppermute | solution.py:11
  40.8 24.6 %collective-permute-start = (bf16[4,128,1024]{2,1,0:T(8,128)(2,1)S(1)}, bf16[4,128,1024]{2,1,0:T(8,128)(2,1)}, u32[]{:S(2)}, u32[]{:S(2)}) collective-permute-start(bf16[4,128,1024]{2,1,0:T(8,128)(2,1)S(1)} %gather_fusion), channel_id=1, source_target_pairs={{0,16},{16,0},{32,48},{48,32},{64,80},{80,64},{96,112},{112,96},{1... | collective-permute-start | bytes 3145736 | tf_op jit(solution)/shard_map/ppermute | solution.py:15
  42.5 3.4 %copy-start = (bf16[1,4,1024,1024]{3,2,1,0:T(8,128)(2,1)S(1)}, bf16[1,4,1024,1024]{3,2,1,0:T(8,128)(2,1)}, u32[]{:S(2)}) copy-start(bf16[1,4,1024,1024]{3,2,1,0:T(8,128)(2,1)} %param.4) | copy-start | bytes 25165828
  62.5 15.7 %collective-permute-start.3 = (bf16[4,64,1024]{2,1,0:T(8,128)(2,1)S(1)}, bf16[4,64,1024]{2,1,0:T(8,128)(2,1)S(1)}, u32[]{:S(2)}, u32[]{:S(2)}) collective-permute-start(bf16[4,64,1024]{2,1,0:T(8,128)(2,1)S(1)} %slice.136), channel_id=1, source_target_pairs={{0,32},{16,48},{32,64},{48,80},{64,96},{80,112},{96,0},{112,16},{1... | collective-permute-start | bytes 1572872 | tf_op jit(solution)/shard_map/ppermute | solution.py:11
  62.7 15.6 %collective-permute-start.4 = (bf16[4,64,1024]{2,1,0:T(8,128)(2,1)S(1)}, bf16[4,64,1024]{2,1,0:T(8,128)(2,1)}, u32[]{:S(2)}, u32[]{:S(2)}) collective-permute-start(bf16[4,64,1024]{2,1,0:T(8,128)(2,1)S(1)} %slice.137), channel_id=1, source_target_pairs={{0,96},{16,112},{32,0},{48,16},{64,32},{80,48},{96,64},{112,80},{1... | collective-permute-start | bytes 1572872 | tf_op jit(solution)/shard_map/ppermute | solution.py:11
  65.4 31.9 %collective-permute-start.5 = (bf16[4,128,1024]{2,1,0:T(8,128)(2,1)}, bf16[4,128,1024]{2,1,0:T(8,128)(2,1)S(1)}, u32[]{:S(2)}, u32[]{:S(2)}) collective-permute-start(bf16[4,128,1024]{2,1,0:T(8,128)(2,1)} %collective-permute-done), channel_id=1, source_target_pairs={{0,32},{16,48},{32,64},{48,80},{64,96},{80,112},{96,0},{112,16},{1... | collective-permute-start | bytes 3145736 | tf_op jit(solution)/shard_map/ppermute | solution.py:11
  65.4 32.1 %collective-permute-start.6 = (bf16[4,128,1024]{2,1,0:T(8,128)(2,1)}, bf16[4,128,1024]{2,1,0:T(8,128)(2,1)S(1)}, u32[]{:S(2)}, u32[]{:S(2)}) collective-permute-start(bf16[4,128,1024]{2,1,0:T(8,128)(2,1)} %collective-permute-done), channel_id=1, source_target_pairs={{0,96},{16,112},{32,0},{48,16},{64,32},{80,48},{96,64},{112,80},{1... | collective-permute-start | bytes 3145736 | tf_op jit(solution)/shard_map/ppermute | solution.py:11
  97.4 11.5 %collective-permute-start.7 = (bf16[4,64,1024]{2,1,0:T(8,128)(2,1)S(1)}, bf16[4,64,1024]{2,1,0:T(8,128)(2,1)S(1)}, u32[]{:S(2)}, u32[]{:S(2)}) collective-permute-start(bf16[4,64,1024]{2,1,0:T(8,128)(2,1)S(1)} %slice.138), channel_id=1, source_target_pairs={{0,32},{16,48},{32,64},{48,80},{64,96},{80,112},{96,0},{112,16},{1... | collective-permute-start | bytes 1572872 | tf_op jit(solution)/shard_map/ppermute | solution.py:11
  97.5 11.3 %collective-permute-start.8 = (bf16[4,64,1024]{2,1,0:T(8,128)(2,1)S(1)}, bf16[4,64,1024]{2,1,0:T(8,128)(2,1)S(1)}, u32[]{:S(2)}, u32[]{:S(2)}) collective-permute-start(bf16[4,64,1024]{2,1,0:T(8,128)(2,1)S(1)} %slice.139), channel_id=1, source_target_pairs={{0,96},{16,112},{32,0},{48,16},{64,32},{80,48},{96,64},{112,80},{1... | collective-permute-start | bytes 1572872 | tf_op jit(solution)/shard_map/ppermute | solution.py:11
  134.0 5.0 %copy-start.1 = (bf16[4608,128]{1,0:T(8,128)(2,1)S(1)}, bf16[4608,128]{1,0:T(8,128)(2,1)}, u32[]{:S(2)}) copy-start(bf16[4608,128]{1,0:T(8,128)(2,1)} %copy.15) | copy-start | bytes 3538948
  142.1 11.8 %copy-start.2 = (s32[128,2]{0,1:T(2,128)S(1)}, s32[128,2]{0,1:T(2,128)}, u32[]{:S(2)}) copy-start(s32[128,2]{0,1:T(2,128)} %param.7) | copy-start | bytes 3076
  142.1 43.0 %all-to-all-start.1 = ((bf16[16,2,288,128]{3,2,1,0:T(8,128)(2,1)}), bf16[16,2,288,128]{3,2,1,0:T(8,128)(2,1)}, u32[]{:S(2)}, u32[]{:S(2)}) async-start(bf16[16,2,288,128]{3,2,1,0:T(8,128)(2,1)} %copy.16), calls=%async_computation.1 | async-start | bytes 4718592 | tf_op jit(solution)/shard_map/all_to_all | solution.py:91
  189.6 13.6 %all-to-all-start.2 = ((f32[16,1,8]{2,1,0:T(1,128)}), f32[16,1,8]{2,1,0:T(1,128)S(1)}, u32[]{:S(2)}, u32[]{:S(2)}) async-start(f32[16,1,8]{2,1,0:T(1,128)} %bitcast.19), calls=%async_computation.2 | async-start | bytes 16384 | tf_op jit(solution)/shard_map/all_to_all | solution.py:99

commit v5 on v4

--- a/solution.py
+++ b/solution.py
@@ -55,16 +55,14 @@
     block_order = propagators.shape[1]
     pieces = source_pieces(own_elemental, src_times)
     rows = pieces[0][1].shape[1]
-    halves = jnp.zeros((NSRC, block_order, block_order), jnp.bfloat16)
+    summed = jnp.zeros((block_order, block_order), jnp.float32)
     for origin, piece in pieces:
-        block = jnp.einsum(
+        half_product = jnp.einsum(
             "sik,sjk->sij", piece, propagators, preferred_element_type=jnp.float32
         ).astype(jnp.bfloat16)
-        halves = lax.dynamic_update_slice_in_dim(halves, block, origin * rows, 1)
-    summed = jnp.zeros((block_order, block_order), jnp.float32)
-    for source in range(NSRC):
-        summed = summed + jnp.dot(
-            propagators[source], halves[source], preferred_element_type=jnp.float32
+        columns = lax.dynamic_slice_in_dim(propagators, origin * rows, rows, 2)
+        summed = summed + jnp.einsum(
+            "sik,skj->ij", columns, half_product, preferred_element_type=jnp.float32
         )
     meson = summed.astype(jnp.bfloat16)
 

time: 204 us -> 221 us (1.083)
  matrix products: 44 us -> 85.9 us
  waiting for transfers between devices: 93.7 us -> 68.6 us
  blocking collectives: 0 us -> 13.3 us
  starting transfers between devices: 35.7 us -> 29.1 us
  local copies, waits for them, and re-layouts: 19.3 us -> 14.6 us
    dot_general x4 -> x8, matrix products: 17.5 us -> 78.7 us  [body(): jnp.einsum('sik,skj->ij', columns, half_product, preferred_element_type=j...]
    ppermute x8, waiting for transfers between devices: 31.4 us -> 11.2 us  [shifted(): return lax.ppermute(block, 'tsink', pairs)]
    dot_general x8 -> x1, matrix products: 25.8 us -> 6.44 us  [body(): jnp.einsum('sik,sjk->sij', piece, propagators, preferred_element_type=jnp...]
    all_to_all x0 -> x1, blocking collectives: none -> 13.3 us  [body(): spread = lax.all_to_all(per_diagram.reshape(n_m, -1), 'mom', 0, 0)]
    all_to_all x1 -> x0, starting transfers between devices: 6.53 us -> none  [body(): spread = lax.all_to_all(per_diagram.reshape(n_m, -1), 'mom', 0, 0)]
    all_to_all x1 -> x0, waiting for transfers between devices: 4.46 us -> none  [body(): spread = lax.all_to_all(per_diagram.reshape(n_m, -1), 'mom', 0, 0)]
    unnamed x23 -> x26, local copies, waits for them, and re-layouts: 9.82 us -> 5.45 us
  transfers between devices with their start and end apart: 12 -> 11, of which waited for: 6 -> 3; matrix products, arithmetic and copies ran while one was open for 16% -> 35% of each run, Pallas kernels for 0% -> 0%
where the time goes in v5:
time: 221 us
  matrix products  85.9 us (39%)
  waiting for transfers between devices  68.6 us (31%)
  starting transfers between devices  29.1 us (13%)
  local copies, waits for them, and re-layouts  14.6 us (7%)
  blocking collectives  13.3 us (6%)
  other arithmetic  8.63 us (4%)
    dot_general x8, matrix products, body(): jnp.einsum('sik,skj->ij', columns, half_product, preferred_element_type=j...  78.7 us
    all_to_all x1, waiting for transfers between devices, body(): received = lax.all_to_all(slices, 'mom', 0, 0)  31.1 us
    all_to_all x1, waiting for transfers between devices, source_pieces(): received = lax.all_to_all(pieces, 'tsink', 0, 0)  26.3 us
    all_to_all x1, blocking collectives, body(): spread = lax.all_to_all(per_diagram.reshape(n_m, -1), 'mom', 0, 0)  13.3 us
    all_to_all x1, starting transfers between devices, body(): received = lax.all_to_all(slices, 'mom', 0, 0)  11.7 us
    ppermute x8, waiting for transfers between devices, shifted(): return lax.ppermute(block, 'tsink', pairs)  11.2 us
    ppermute x8, starting transfers between devices, shifted(): return lax.ppermute(block, 'tsink', pairs)  11.1 us
    dot_general x1, matrix products, body(): jnp.einsum('sik,sjk->sij', piece, propagators, preferred_element_type=jnp...  6.44 us
  transfers between devices with their start and end apart: 11, of which 3 were waited for; matrix products, arithmetic and copies ran while one was open for 35% of the time, Pallas kernels for 0%

profile of v5, /device:TPU:1, one launch (start us, length us, event | category | flops | bytes accessed | tf_op | source)
XLA Modules:
  0.0 221.0 jit_solution(16726381903726240869)
XLA Ops:
  0.6 6.2 %all-to-all-start = ((bf16[8,128,1024]{2,1,0:T(8,128)(2,1)}), bf16[8,128,1024]{2,1,0:T(8,128)(2,1)S(1)}, u32[]{:S(2)}, u32[]{:S(2)}) async-start(bf16[8,128,1024]{2,1,0:T(8,128)(2,1)} %bitcast.143), calls=%async_computation | async-start | bytes 4194304 | tf_op jit(solution)/shard_map/all_to_all | solution.py:24
  6.9 0.6 constant_dynamic-update-slice_fusion.1
  7.6 0.7 fusion.94
  8.2 0.7 fusion.89
  8.9 0.7 fusion.88
  9.6 0.7 fusion.87
  10.4 0.8 fusion.86
  11.2 26.3 %all-to-all-done = bf16[8,128,1024]{2,1,0:T(8,128)(2,1)S(1)} async-done(((bf16[8,128,1024]{2,1,0:T(8,128)(2,1)}), bf16[8,128,1024]{2,1,0:T(8,128)(2,1)S(1)}, u32[]{:S(2)}, u32[]{:S(2)}) %all-to-all-start) | async-done | bytes 2097184 | tf_op jit(solution)/shard_map/all_to_all | solution.py:24
  37.5 0.6 gather_fusion
  38.2 2.7 %collective-permute-start.2 = (bf16[4,128,1024]{2,1,0:T(8,128)(2,1)S(1)}, bf16[4,128,1024]{2,1,0:T(8,128)(2,1)S(1)}, u32[]{:S(2)}, u32[]{:S(2)}) collective-permute-start(bf16[4,128,1024]{2,1,0:T(8,128)(2,1)S(1)} %gather_fusion), channel_id=1, source_target_pairs={{0,96},{16,112},{32,0},{48,16},{64,32},{80,48},{96,64},{112,80},{1... | collective-permute-start | bytes 3145736 | tf_op jit(solution)/shard_map/ppermute | solution.py:11
  40.8 0.8 fusion.85
  41.6 9.7 %fusion.72 = f32[1024,1024,1]{1,0,2:T(8,128)} fusion(bf16[4,128,1024]{2,1,0:T(8,128)(2,1)S(1)} %gather_fusion, bf16[1,4,1024,1024]{3,2,1,0:T(8,128)(2,1)} %param.4, s32[]{:T(128)S(6)} %select_n.120), kind=kOutput, calls=%fused_computation.58 | convolution fusion | flops 2148007936 | bytes 14680068 | tf_op jit(solution)/shard_map/sik,skj->ij/dot_general | solution.py:64
  51.3 11.2 %collective-permute-done.1 = bf16[4,128,1024]{2,1,0:T(8,128)(2,1)S(1)} collective-permute-done((bf16[4,128,1024]{2,1,0:T(8,128)(2,1)S(1)}, bf16[4,128,1024]{2,1,0:T(8,128)(2,1)S(1)}, u32[]{:S(2)}, u32[]{:S(2)}) %collective-permute-start.1) | collective-permute-done | bytes 1048608 | tf_op jit(solution)/shard_map/ppermute | solution.py:11
  62.5 0.8 slice.100
  63.4 0.8 slice.101
  64.2 2.7 %collective-permute-start.4 = (bf16[4,64,1024]{2,1,0:T(8,128)(2,1)}, bf16[4,64,1024]{2,1,0:T(8,128)(2,1)}, u32[]{:S(2)}, u32[]{:S(2)}) collective-permute-start(bf16[4,64,1024]{2,1,0:T(8,128)(2,1)} %slice.101), channel_id=1, source_target_pairs={{0,96},{16,112},{32,0},{48,16},{64,32},{80,48},{96,64},{112,80},{1... | collective-permute-start | bytes 1572872 | tf_op jit(solution)/shard_map/ppermute | solution.py:11
  66.9 2.7 %collective-permute-start.6 = (bf16[4,128,1024]{2,1,0:T(8,128)(2,1)}, bf16[4,128,1024]{2,1,0:T(8,128)(2,1)}, u32[]{:S(2)}, u32[]{:S(2)}) collective-permute-start(bf16[4,128,1024]{2,1,0:T(8,128)(2,1)} %collective-permute-done), channel_id=1, source_target_pairs={{0,96},{16,112},{32,0},{48,16},{64,32},{80,48},{96,64},{112,80},{1... | collective-permute-start | bytes 3145736 | tf_op jit(solution)/shard_map/ppermute | solution.py:11
  69.5 9.7 %fusion.60 = f32[1024,1024,1]{1,0,2:T(8,128)} fusion(bf16[4,128,1024]{2,1,0:T(8,128)(2,1)S(1)} %collective-permute-done.2, bf16[1,4,1024,1024]{3,2,1,0:T(8,128)(2,1)} %param.4, s32[]{:T(128)S(6)} %select_n.126), kind=kOutput, calls=%fused_computation.52 | convolution fusion | flops 2148007936 | bytes 14680068 | tf_op jit(solution)/shard_map/sik,skj->ij/dot_general | solution.py:64
  79.3 9.7 %fusion.64 = f32[1024,1024,1]{1,0,2:T(8,128)} fusion(bf16[4,128,1024]{2,1,0:T(8,128)(2,1)S(1)} %collective-permute-done.1, bf16[1,4,1024,1024]{3,2,1,0:T(8,128)(2,1)} %param.4, s32[]{:T(128)S(6)} %select_n.124), kind=kOutput, calls=%fused_computation.54 | convolution fusion | flops 2148007936 | bytes 14680068 | tf_op jit(solution)/shard_map/sik,skj->ij/dot_general | solution.py:64
  89.0 10.0 %fusion.68 = f32[1024,1024,1]{1,0,2:T(8,128)} fusion(bf16[4,128,1024]{2,1,0:T(8,128)(2,1)} %collective-permute-done, bf16[1,4,1024,1024]{3,2,1,0:T(8,128)(2,1)} %param.4, s32[]{:T(128)S(6)} %select_n.122), kind=kOutput, calls=%fused_computation.56 | convolution fusion | flops 2148007936 | bytes 14680068 | tf_op jit(solution)/shard_map/sik,skj->ij/dot_general | solution.py:64
  99.0 10.0 %fusion.58 = f32[1024,1024,1]{1,0,2:T(8,128)} fusion(bf16[1,4,1024,1024]{3,2,1,0:T(8,128)(2,1)} %param.4, s32[]{:T(128)S(6)} %select_n.128, bf16[4,64,1024]{2,1,0:T(8,128)(2,1)} %collective-permute-done.4, bf16[4,64,1024]{2,1,0:T(8,128)(2,1)} %collective-permute-done.3), kind=kOutput, calls=%fused_computation.50 | convolution fusion | flops 2150105088 | bytes 14680068 | tf_op jit(solution)/shard_map/sik,skj->ij/dot_general | solution.py:64
  109.1 0.3 collective-permute-start.7
  109.4 1.1 slice.103
  110.5 2.7 %collective-permute-start.8 = (bf16[4,64,1024]{2,1,0:T(8,128)(2,1)S(1)}, bf16[4,64,1024]{2,1,0:T(8,128)(2,1)S(1)}, u32[]{:S(2)}, u32[]{:S(2)}) collective-permute-start(bf16[4,64,1024]{2,1,0:T(8,128)(2,1)S(1)} %slice.103), channel_id=1, source_target_pairs={{0,96},{16,112},{32,0},{48,16},{64,32},{80,48},{96,64},{112,80},{1... | collective-permute-start | bytes 1572872 | tf_op jit(solution)/shard_map/ppermute | solution.py:11
  113.2 9.7 %fusion.54 = f32[1024,1024,1]{1,0,2:T(8,128)} fusion(bf16[4,128,1024]{2,1,0:T(8,128)(2,1)S(1)} %collective-permute-done.5, bf16[1,4,1024,1024]{3,2,1,0:T(8,128)(2,1)} %param.4, s32[]{:T(128)S(6)} %select_n.129), kind=kOutput, calls=%fused_computation.48 | convolution fusion | flops 2148007936 | bytes 14680068 | tf_op jit(solution)/shard_map/sik,skj->ij/dot_general | solution.py:64
  122.9 10.1 %fusion.50 = f32[1024,1024,1]{1,0,2:T(8,128)} fusion(bf16[4,128,1024]{2,1,0:T(8,128)(2,1)} %collective-permute-done.6, bf16[1,4,1024,1024]{3,2,1,0:T(8,128)(2,1)} %param.4, s32[]{:T(128)S(6)} %select_n.130), kind=kOutput, calls=%fused_computation.46 | convolution fusion | flops 2148007936 | bytes 14680068 | tf_op jit(solution)/shard_map/sik,skj->ij/dot_general | solution.py:64
  133.0 6.4 %fusion.38 = bf16[4,128,1024]{2,1,0:T(8,128)(2,1)S(1)} fusion(bf16[1,4,1024,1024]{3,2,1,0:T(8,128)(2,1)} %param.4, bf16[4,64,1024]{2,1,0:T(8,128)(2,1)S(1)} %collective-permute-done.8, bf16[4,64,1024]{2,1,0:T(8,128)(2,1)S(1)} %collective-permute-done.7), kind=kOutput, calls=%fused_computation.34 | convolution fusion | flops 1076363264 | bytes 10485760 | tf_op jit(solution)/shard_map/sik,sjk->sij/dot_general | solution.py:60
  139.4 9.8 %fusion.16 = bf16[1024,1024]{1,0:T(8,128)(2,1)S(1)} fusion(f32[1024,1024,1]{1,0,2:T(8,128)} %fusion.50, f32[1024,1024,1]{1,0,2:T(8,128)} %fusion.54, f32[1024,1024,1]{1,0,2:T(8,128)} %fusion.58, f32[1024,1024,1]{1,0,2:T(8,128)S(1)} %copy-done.1, f32[1024,1024,1]{1,0,2:T(8,128)} %fusion.64, f32[1024,1024,1]{1,0,2:T(8,128)} %fusion.68, ...), kind=kOutput, calls=%fused_computation.19 | convolution fusion | flops 1082130432 | bytes 33554436 | tf_op jit(solution)/shard_map/sik,skj->ij/dot_general | solution.py:64
  149.6 0.9 constant_dynamic-update-slice_fusion.2
  150.6 0.6 slice_dynamic-update-slice_fusion.12
  151.2 0.7 slice_dynamic-update-slice_fusion.10
  151.9 0.7 slice_dynamic-update-slice_fusion.8
  152.6 0.7 slice_dynamic-update-slice_fusion.6
  153.3 0.7 slice_dynamic-update-slice_fusion.4
  154.0 0.8 slice_dynamic-update-slice_fusion.2
  154.7 0.8 slice_dynamic-update-slice_fusion
  155.5 1.7 copy.13
  157.2 0.9 fusion.84
  158.1 1.9 mul.45
  160.0 0.2 pad_maximum_fusion
  160.3 1.7 copy.14
  161.9 11.7 %all-to-all-start.1 = ((bf16[16,2,288,128]{3,2,1,0:T(8,128)(2,1)}), bf16[16,2,288,128]{3,2,1,0:T(8,128)(2,1)S(1)}, u32[]{:S(2)}, u32[]{:S(2)}) async-start(bf16[16,2,288,128]{3,2,1,0:T(8,128)(2,1)} %copy.14), calls=%async_computation.1 | async-start | bytes 4718592 | tf_op jit(solution)/shard_map/all_to_all | solution.py:89
  173.7 31.1 %all-to-all-done.1 = bf16[16,2,288,128]{3,2,1,0:T(8,128)(2,1)S(1)} async-done(((bf16[16,2,288,128]{3,2,1,0:T(8,128)(2,1)}), bf16[16,2,288,128]{3,2,1,0:T(8,128)(2,1)S(1)}, u32[]{:S(2)}, u32[]{:S(2)}) %all-to-all-start.1) | async-done | bytes 2359328 | tf_op jit(solution)/shard_map/all_to_all | solution.py:89
  204.8 0.2 fusion.112
  204.9 0.7 fusion.42
  205.7 1.3 gather_fusion.1
  207.1 13.3 %all_to_all.19 = f32[16,1,8]{2,1,0:T(1,128)S(1)} all-to-all(f32[16,1,8]{2,1,0:T(1,128)S(1)} %bitcast.144), channel_id=1, replica_groups=mesh['tsink'=8,'mom'=16] {'mom'}, dimensions={0} | all-to-all | bytes 1024 | tf_op jit(solution)/shard_map/all_to_all | solution.py:97
  220.5 0.5 multiply_bitcast_fusion
  (46 shorter events, 0.8 us)
Async XLA Ops:
  0.6 6.3 %copy-start.5 = (s32[4]{0:T(128)S(1)}, s32[4]{0:T(128)}, u32[]{:S(2)}) copy-start(s32[4]{0:T(128)} %param.6) | copy-start | bytes 52
  0.6 36.8 %all-to-all-start = ((bf16[8,128,1024]{2,1,0:T(8,128)(2,1)}), bf16[8,128,1024]{2,1,0:T(8,128)(2,1)S(1)}, u32[]{:S(2)}, u32[]{:S(2)}) async-start(bf16[8,128,1024]{2,1,0:T(8,128)(2,1)} %bitcast.143), calls=%async_computation | async-start | bytes 4194304 | tf_op jit(solution)/shard_map/all_to_all | solution.py:24
  38.1 24.4 %collective-permute-start.1 = (bf16[4,128,1024]{2,1,0:T(8,128)(2,1)S(1)}, bf16[4,128,1024]{2,1,0:T(8,128)(2,1)S(1)}, u32[]{:S(2)}, u32[]{:S(2)}) collective-permute-start(bf16[4,128,1024]{2,1,0:T(8,128)(2,1)S(1)} %gather_fusion), channel_id=1, source_target_pairs={{0,32},{16,48},{32,64},{48,80},{64,96},{80,112},{96,0},{112,16},{1... | collective-permute-start | bytes 3145736 | tf_op jit(solution)/shard_map/ppermute | solution.py:11
  38.2 25.2 %collective-permute-start.2 = (bf16[4,128,1024]{2,1,0:T(8,128)(2,1)S(1)}, bf16[4,128,1024]{2,1,0:T(8,128)(2,1)S(1)}, u32[]{:S(2)}, u32[]{:S(2)}) collective-permute-start(bf16[4,128,1024]{2,1,0:T(8,128)(2,1)S(1)} %gather_fusion), channel_id=1, source_target_pairs={{0,96},{16,112},{32,0},{48,16},{64,32},{80,48},{96,64},{112,80},{1... | collective-permute-start | bytes 3145736 | tf_op jit(solution)/shard_map/ppermute | solution.py:11
  40.8 26.0 %collective-permute-start = (bf16[4,128,1024]{2,1,0:T(8,128)(2,1)S(1)}, bf16[4,128,1024]{2,1,0:T(8,128)(2,1)}, u32[]{:S(2)}, u32[]{:S(2)}) collective-permute-start(bf16[4,128,1024]{2,1,0:T(8,128)(2,1)S(1)} %gather_fusion), channel_id=1, source_target_pairs={{0,16},{16,0},{32,48},{48,32},{64,80},{80,64},{96,112},{112,96},{1... | collective-permute-start | bytes 3145736 | tf_op jit(solution)/shard_map/ppermute | solution.py:15
  63.4 35.6 %collective-permute-start.3 = (bf16[4,64,1024]{2,1,0:T(8,128)(2,1)}, bf16[4,64,1024]{2,1,0:T(8,128)(2,1)}, u32[]{:S(2)}, u32[]{:S(2)}) collective-permute-start(bf16[4,64,1024]{2,1,0:T(8,128)(2,1)} %slice.100), channel_id=1, source_target_pairs={{0,32},{16,48},{32,64},{48,80},{64,96},{80,112},{96,0},{112,16},{1... | collective-permute-start | bytes 1572872 | tf_op jit(solution)/shard_map/ppermute | solution.py:11
  64.2 34.8 %collective-permute-start.4 = (bf16[4,64,1024]{2,1,0:T(8,128)(2,1)}, bf16[4,64,1024]{2,1,0:T(8,128)(2,1)}, u32[]{:S(2)}, u32[]{:S(2)}) collective-permute-start(bf16[4,64,1024]{2,1,0:T(8,128)(2,1)} %slice.101), channel_id=1, source_target_pairs={{0,96},{16,112},{32,0},{48,16},{64,32},{80,48},{96,64},{112,80},{1... | collective-permute-start | bytes 1572872 | tf_op jit(solution)/shard_map/ppermute | solution.py:11
  66.9 42.1 %collective-permute-start.5 = (bf16[4,128,1024]{2,1,0:T(8,128)(2,1)}, bf16[4,128,1024]{2,1,0:T(8,128)(2,1)S(1)}, u32[]{:S(2)}, u32[]{:S(2)}) collective-permute-start(bf16[4,128,1024]{2,1,0:T(8,128)(2,1)} %collective-permute-done), channel_id=1, source_target_pairs={{0,32},{16,48},{32,64},{48,80},{64,96},{80,112},{96,0},{112,16},{1... | collective-permute-start | bytes 3145736 | tf_op jit(solution)/shard_map/ppermute | solution.py:11
  66.9 42.5 %collective-permute-start.6 = (bf16[4,128,1024]{2,1,0:T(8,128)(2,1)}, bf16[4,128,1024]{2,1,0:T(8,128)(2,1)}, u32[]{:S(2)}, u32[]{:S(2)}) collective-permute-start(bf16[4,128,1024]{2,1,0:T(8,128)(2,1)} %collective-permute-done), channel_id=1, source_target_pairs={{0,96},{16,112},{32,0},{48,16},{64,32},{80,48},{96,64},{112,80},{1... | collective-permute-start | bytes 3145736 | tf_op jit(solution)/shard_map/ppermute | solution.py:11
  109.1 23.9 %collective-permute-start.7 = (bf16[4,64,1024]{2,1,0:T(8,128)(2,1)S(1)}, bf16[4,64,1024]{2,1,0:T(8,128)(2,1)S(1)}, u32[]{:S(2)}, u32[]{:S(2)}) collective-permute-start(bf16[4,64,1024]{2,1,0:T(8,128)(2,1)S(1)} %slice.102), channel_id=1, source_target_pairs={{0,32},{16,48},{32,64},{48,80},{64,96},{80,112},{96,0},{112,16},{1... | collective-permute-start | bytes 1572872 | tf_op jit(solution)/shard_map/ppermute | solution.py:11
  110.5 22.5 %collective-permute-start.8 = (bf16[4,64,1024]{2,1,0:T(8,128)(2,1)S(1)}, bf16[4,64,1024]{2,1,0:T(8,128)(2,1)S(1)}, u32[]{:S(2)}, u32[]{:S(2)}) collective-permute-start(bf16[4,64,1024]{2,1,0:T(8,128)(2,1)S(1)} %slice.103), channel_id=1, source_target_pairs={{0,96},{16,112},{32,0},{48,16},{64,32},{80,48},{96,64},{112,80},{1... | collective-permute-start | bytes 1572872 | tf_op jit(solution)/shard_map/ppermute | solution.py:11
  132.9 6.5 %copy-start = (f32[1024,1024,1]{1,0,2:T(8,128)S(1)}, f32[1024,1024,1]{1,0,2:T(8,128)}, u32[]{:S(2)}) copy-start(f32[1024,1024,1]{1,0,2:T(8,128)} %fusion.72) | copy-start | bytes 12582916
  132.9 6.5 %copy-start.1 = (f32[1024,1024,1]{1,0,2:T(8,128)S(1)}, f32[1024,1024,1]{1,0,2:T(8,128)}, u32[]{:S(2)}) copy-start(f32[1024,1024,1]{1,0,2:T(8,128)} %fusion.60) | copy-start | bytes 12582916
  149.3 7.9 %copy-start.2 = (bf16[1024,1024]{1,0:T(8,128)(2,1)}, bf16[1024,1024]{1,0:T(8,128)(2,1)S(1)}, u32[]{:S(2)}) copy-start(bf16[1024,1024]{1,0:T(8,128)(2,1)S(1)} %fusion.16) | copy-start | bytes 6291460
  149.6 5.1 %copy-start.3 = (bf16[4608,128]{1,0:T(8,128)(2,1)}, bf16[4608,128]{1,0:T(8,128)(2,1)S(1)}, u32[]{:S(2)}) copy-start(bf16[4608,128]{1,0:T(8,128)(2,1)S(1)} %slice_dynamic-update-slice_fusion.3) | copy-start | bytes 3538948
  161.9 11.8 %copy-start.4 = (s32[128,2]{0,1:T(2,128)S(1)}, s32[128,2]{0,1:T(2,128)}, u32[]{:S(2)}) copy-start(s32[128,2]{0,1:T(2,128)} %param.7) | copy-start | bytes 3076
  161.9 42.9 %all-to-all-start.1 = ((bf16[16,2,288,128]{3,2,1,0:T(8,128)(2,1)}), bf16[16,2,288,128]{3,2,1,0:T(8,128)(2,1)S(1)}, u32[]{:S(2)}, u32[]{:S(2)}) async-start(bf16[16,2,288,128]{3,2,1,0:T(8,128)(2,1)} %copy.14), calls=%async_computation.1 | async-start | bytes 4718592 | tf_op jit(solution)/shard_map/all_to_all | solution.py:89

commit v6 on v4

--- a/solution.py
+++ b/solution.py
@@ -20,32 +20,40 @@
     order = own_elemental.shape[0]
     rows = order // n_t
     half = rows // 2
+    quarter = half // 2
     pieces = own_elemental.reshape(n_t, rows, order)
     received = lax.all_to_all(pieces, "tsink", 0, 0)
     own = received[src_times]
     t = lax.axis_index("tsink")
     step = 2
-    partner = swapped(own, n_t)
     from_left = shifted(own, step, n_t)
     from_right = shifted(own, -step, n_t)
+    partner_a = swapped(own[:, :half], n_t)
     far = jnp.concatenate(
         [shifted(from_left[:, :half], step, n_t), shifted(from_right[:, half:], -step, n_t)], axis=1
     )
-    partner_left = shifted(partner, step, n_t)
-    partner_right = shifted(partner, -step, n_t)
-    partner_far = jnp.concatenate(
-        [shifted(partner_left[:, :half], step, n_t), shifted(partner_right[:, half:], -step, n_t)],
+    partner_b = swapped(
+        jnp.stack([own[:, half:], from_left[:, half:], from_right[:, half:]]), n_t
+    )
+    partner_left_a = shifted(partner_a, step, n_t)
+    partner_right_a = shifted(partner_a, -step, n_t)
+    partner_far_a = jnp.concatenate(
+        [
+            shifted(partner_left_a[:, :quarter], step, n_t),
+            shifted(partner_right_a[:, quarter:], -step, n_t),
+        ],
         axis=1,
     )
+    partner_far_b = swapped(far[:, half:], n_t)
     return [
         (t, own),
-        (t ^ 1, partner),
         ((t - step) % n_t, from_left),
         ((t + step) % n_t, from_right),
         ((t + 2 * step) % n_t, far),
-        ((t - step) % n_t ^ 1, partner_left),
-        ((t + step) % n_t ^ 1, partner_right),
-        ((t + 2 * step) % n_t ^ 1, partner_far),
+        (t ^ 1, jnp.concatenate([partner_a, partner_b[0]], axis=1)),
+        ((t - step) % n_t ^ 1, jnp.concatenate([partner_left_a, partner_b[1]], axis=1)),
+        ((t + step) % n_t ^ 1, jnp.concatenate([partner_right_a, partner_b[2]], axis=1)),
+        ((t + 2 * step) % n_t ^ 1, jnp.concatenate([partner_far_a, partner_far_b], axis=1)),
     ]
 
 

time: 204 us -> 208 us (1.020)
  starting transfers between devices: 35.7 us -> 40 us
    ppermute x8, waiting for transfers between devices: 31.4 us -> 19.3 us  [shifted(): return lax.ppermute(block, 'tsink', pairs)]
    ppermute x1 -> x3, waiting for transfers between devices: 0.01 us -> 10.9 us  [swapped(): return lax.ppermute(block, 'tsink', [(t, t ^ 1) for t in range(n_t)])]
    all_to_all x1, starting transfers between devices: 11.8 us -> 18.3 us  [body(): received = lax.all_to_all(slices, 'mom', 0, 0)]
    ppermute x8, starting transfers between devices: 11.2 us -> 8.52 us  [shifted(): return lax.ppermute(block, 'tsink', pairs)]
    unnamed x23 -> x31, local copies, waits for them, and re-layouts: 9.82 us -> 10.5 us
  transfers between devices with their start and end apart: 12 -> 14, of which waited for: 6 -> 10; matrix products, arithmetic and copies ran while one was open for 16% -> 16% of each run, Pallas kernels for 0% -> 0%
where the time goes in v6:
time: 208 us; the launch traced here: 207 us
  waiting for transfers between devices  91.8 us (44%)
  matrix products  43.7 us (21%)
  starting transfers between devices  40 us (19%)
  local copies, waits for them, and re-layouts  20.4 us (10%)
  other arithmetic  10.1 us (5%)
    all_to_all x1, waiting for transfers between devices, body(): received = lax.all_to_all(slices, 'mom', 0, 0)  31.2 us
    all_to_all x1, waiting for transfers between devices, source_pieces(): received = lax.all_to_all(pieces, 'tsink', 0, 0)  25.9 us
    dot_general x8, matrix products, body(): jnp.einsum('sik,sjk->sij', piece, propagators, preferred_element_type=jnp...  25.6 us
    ppermute x8, waiting for transfers between devices, shifted(): return lax.ppermute(block, 'tsink', pairs)  19.3 us
    all_to_all x1, starting transfers between devices, body(): received = lax.all_to_all(slices, 'mom', 0, 0)  18.3 us
    dot_general x4, matrix products, body(): jnp.dot(propagators[source], halves[source], preferred_element_type=jnp.f...  17.4 us
    ppermute x3, waiting for transfers between devices, swapped(): return lax.ppermute(block, 'tsink', [(t, t ^ 1) for t in range(n_t)])  10.9 us
    unnamed x31, local copies, waits for them, and re-layouts  10.5 us
  transfers between devices with their start and end apart: 14, of which 10 were waited for; matrix products, arithmetic and copies ran while one was open for 16% of the time, Pallas kernels for 0%

profile of v6, /device:TPU:1, one launch (start us, length us, event | category | flops | bytes accessed | tf_op | source)
XLA Modules:
  0.0 207.0 jit_solution(12841968380046372328)
XLA Ops:
  0.6 6.2 %all-to-all-start = ((bf16[8,128,1024]{2,1,0:T(8,128)(2,1)}), bf16[8,128,1024]{2,1,0:T(8,128)(2,1)S(1)}, u32[]{:S(2)}, u32[]{:S(2)}) async-start(bf16[8,128,1024]{2,1,0:T(8,128)(2,1)} %bitcast.127), calls=%async_computation | async-start | bytes 4194304 | tf_op jit(solution)/shard_map/all_to_all | solution.py:25
  7.7 0.7 fusion.103
  8.4 0.8 fusion.102
  9.2 0.8 fusion.101
  10.0 0.8 fusion.100
  10.8 0.8 fusion.99
  11.6 25.9 %all-to-all-done = bf16[8,128,1024]{2,1,0:T(8,128)(2,1)S(1)} async-done(((bf16[8,128,1024]{2,1,0:T(8,128)(2,1)}), bf16[8,128,1024]{2,1,0:T(8,128)(2,1)S(1)}, u32[]{:S(2)}, u32[]{:S(2)}) %all-to-all-start) | async-done | bytes 2097184 | tf_op jit(solution)/shard_map/all_to_all | solution.py:25
  38.2 0.9 fusion.98
  39.0 1.5 collective-permute-start
  40.7 1.1 broadcast_in_dim.108
  41.7 2.2 %copy-done = bf16[1,4,1024,1024]{3,2,1,0:T(8,128)(2,1)S(1)} copy-done((bf16[1,4,1024,1024]{3,2,1,0:T(8,128)(2,1)S(1)}, bf16[1,4,1024,1024]{3,2,1,0:T(8,128)(2,1)}, u32[]{:S(2)}) %copy-start) | copy-done | bytes 8388632
  44.0 3.0 %fusion.73 = bf16[4,1024,1024]{2,1,0:T(8,128)(2,1)S(1)} fusion(bf16[4,1024,1024]{2,1,0:T(8,128)(2,1)S(1)} %broadcast_in_dim.108, s32[]{:T(128)S(6)} %select_n.121, bf16[4,128,1024]{2,1,0:T(8,128)(2,1)S(1)} %gather_fusion, bf16[1,4,1024,1024]{3,2,1,0:T(8,128)(2,1)S(1)} %copy-done), kind=kOutput, calls=%fused_computation.52 | convolution fusion | flops 1074266112 | bytes 10485764 | tf_op jit(solution)/shard_map/sik,sjk->sij/dot_general | solution.py:68
  46.9 5.2 %collective-permute-done.4 = bf16[4,64,1024]{2,1,0:T(8,128)(2,1)} collective-permute-done((bf16[4,64,1024]{2,1,0:T(8,128)(2,1)S(1)}, bf16[4,64,1024]{2,1,0:T(8,128)(2,1)}, u32[]{:S(2)}, u32[]{:S(2)}) %collective-permute-start.4) | collective-permute-done | bytes 524320 | tf_op jit(solution)/shard_map/ppermute | solution.py:15
  52.4 2.4 %collective-permute-start.7 = (bf16[4,64,1024]{2,1,0:T(8,128)(2,1)}, bf16[4,64,1024]{2,1,0:T(8,128)(2,1)S(1)}, u32[]{:S(2)}, u32[]{:S(2)}) collective-permute-start(bf16[4,64,1024]{2,1,0:T(8,128)(2,1)} %collective-permute-done.4), channel_id=1, source_target_pairs={{0,96},{16,112},{32,0},{48,16},{64,32},{80,48},{96,64},{112,80},{1... | collective-permute-start | bytes 1572872 | tf_op jit(solution)/shard_map/ppermute | solution.py:11
  54.8 6.5 %collective-permute-done.1 = bf16[4,128,1024]{2,1,0:T(8,128)(2,1)S(1)} collective-permute-done((bf16[4,128,1024]{2,1,0:T(8,128)(2,1)S(1)}, bf16[4,128,1024]{2,1,0:T(8,128)(2,1)S(1)}, u32[]{:S(2)}, u32[]{:S(2)}) %collective-permute-start.1) | collective-permute-done | bytes 1048608 | tf_op jit(solution)/shard_map/ppermute | solution.py:11
  61.4 1.6 collective-permute-start.3
  63.8 10.8 %collective-permute-done.6 = bf16[4,64,1024]{2,1,0:T(8,128)(2,1)S(1)} collective-permute-done((bf16[4,64,1024]{2,1,0:T(8,128)(2,1)}, bf16[4,64,1024]{2,1,0:T(8,128)(2,1)S(1)}, u32[]{:S(2)}, u32[]{:S(2)}) %collective-permute-start.6) | collective-permute-done | bytes 524320 | tf_op jit(solution)/shard_map/ppermute | solution.py:11
  75.6 2.6 %collective-permute-start.9 = (bf16[4,32,1024]{2,1,0:T(8,128)(2,1)S(1)}, bf16[4,32,1024]{2,1,0:T(8,128)(2,1)S(1)}, u32[]{:S(2)}, u32[]{:S(2)}) collective-permute-start(bf16[4,32,1024]{2,1,0:T(8,128)(2,1)S(1)} %slice.170), channel_id=1, source_target_pairs={{0,96},{16,112},{32,0},{48,16},{64,32},{80,48},{96,64},{112,80},{1... | collective-permute-start | bytes 786440 | tf_op jit(solution)/shard_map/ppermute | solution.py:11
  78.2 2.9 %fusion.70 = bf16[4,1024,1024]{2,1,0:T(8,128)(2,1)S(1)} fusion(bf16[4,1024,1024]{2,1,0:T(8,128)(2,1)S(1)} %fusion.73, s32[]{:T(128)S(6)} %select_n.123, bf16[4,128,1024]{2,1,0:T(8,128)(2,1)S(1)} %collective-permute-done, bf16[1,4,1024,1024]{3,2,1,0:T(8,128)(2,1)S(1)} %copy-done), kind=kOutput, calls=%fused_computation.51 | convolution fusion | flops 1074266112 | bytes 10485764 | tf_op jit(solution)/shard_map/sik,sjk->sij/dot_general | solution.py:68
  81.1 2.9 %fusion.67 = bf16[4,1024,1024]{2,1,0:T(8,128)(2,1)S(1)} fusion(bf16[4,1024,1024]{2,1,0:T(8,128)(2,1)S(1)} %fusion.70, s32[]{:T(128)S(6)} %select_n.125, bf16[4,128,1024]{2,1,0:T(8,128)(2,1)S(1)} %collective-permute-done.1, bf16[1,4,1024,1024]{3,2,1,0:T(8,128)(2,1)S(1)} %copy-done), kind=kOutput, calls=%fused_computation.50 | convolution fusion | flops 1074266112 | bytes 10485764 | tf_op jit(solution)/shard_map/sik,sjk->sij/dot_general | solution.py:68
  84.3 1.5 collective-permute-done.2
  85.9 4.0 %fusion.64 = bf16[4,1024,1024]{2,1,0:T(8,128)(2,1)S(1)} fusion(bf16[4,1024,1024]{2,1,0:T(8,128)(2,1)S(1)} %fusion.67, s32[]{:T(128)S(6)} %select_n.127, bf16[1,4,1024,1024]{3,2,1,0:T(8,128)(2,1)S(1)} %copy-done, bf16[4,64,1024]{2,1,0:T(8,128)(2,1)} %collective-permute-done.3, bf16[4,64,1024]{2,1,0:T(8,128)(2,1)S(1)} %collective-permute-done.2), kind=kOutput, calls=%fused_computation.49 | convolution fusion | flops 1076363264 | bytes 10485764 | tf_op jit(solution)/shard_map/sik,sjk->sij/dot_general | solution.py:68
  89.9 4.7 %collective-permute-done.5 = bf16[3,4,64,1024]{3,2,1,0:T(8,128)(2,1)S(1)} collective-permute-done((bf16[3,4,64,1024]{3,2,1,0:T(8,128)(2,1)S(1)}, bf16[3,4,64,1024]{3,2,1,0:T(8,128)(2,1)S(1)}, u32[]{:S(2)}, u32[]{:S(2)}) %collective-permute-start.5) | collective-permute-done | bytes 1572896 | tf_op jit(solution)/shard_map/ppermute | solution.py:15
  94.8 4.0 %fusion.61 = bf16[4,1024,1024]{2,1,0:T(8,128)(2,1)S(1)} fusion(bf16[4,1024,1024]{2,1,0:T(8,128)(2,1)S(1)} %fusion.64, s32[]{:T(128)S(6)} %select_n.128, bf16[1,4,1024,1024]{3,2,1,0:T(8,128)(2,1)S(1)} %copy-done, bf16[4,64,1024]{2,1,0:T(8,128)(2,1)S(1)} %get-tuple-element.12, bf16[4,64,1024]{2,1,0:T(8,128)(2,1)} %collective-permute-done.4), kind=kOutput, calls=%fused_computation.48 | convolution fusion | flops 1076363264 | bytes 10485764 | tf_op jit(solution)/shard_map/sik,sjk->sij/dot_general | solution.py:68
  98.8 2.9 %fusion.58 = bf16[4,1024,1024]{2,1,0:T(8,128)(2,1)S(1)} fusion(bf16[4,1024,1024]{2,1,0:T(8,128)(2,1)S(1)} %fusion.61, s32[]{:T(128)S(6)} %select_n.129, bf16[1,4,1024,1024]{3,2,1,0:T(8,128)(2,1)S(1)} %copy-done, bf16[4,64,1024]{2,1,0:T(8,128)(2,1)S(1)} %get-tuple-element.11, bf16[4,64,1024]{2,1,0:T(8,128)(2,1)S(1)} %copy-done.5), kind=kOutput, calls=%fused_computation.47 | convolution fusion | flops 1076363264 | bytes 10485764 | tf_op jit(solution)/shard_map/sik,sjk->sij/dot_general | solution.py:68
  101.7 2.9 %fusion.55 = bf16[4,1024,1024]{2,1,0:T(8,128)(2,1)S(1)} fusion(bf16[4,1024,1024]{2,1,0:T(8,128)(2,1)S(1)} %fusion.58, s32[]{:T(128)S(6)} %select_n.130, bf16[1,4,1024,1024]{3,2,1,0:T(8,128)(2,1)S(1)} %copy-done, bf16[4,64,1024]{2,1,0:T(8,128)(2,1)S(1)} %get-tuple-element.10, bf16[4,64,1024]{2,1,0:T(8,128)(2,1)S(1)} %copy-done.3), kind=kOutput, calls=%fused_computation.46 | convolution fusion | flops 1076363264 | bytes 10485764 | tf_op jit(solution)/shard_map/sik,sjk->sij/dot_general | solution.py:68
  104.7 1.1 collective-permute-done.10
  105.8 2.9 %fusion.52 = bf16[4,1024,1024]{2,1,0:T(8,128)(2,1)S(1)} fusion(bf16[4,1024,1024]{2,1,0:T(8,128)(2,1)S(1)} %fusion.55, s32[]{:T(128)S(6)} %select_n.131, bf16[1,4,1024,1024]{3,2,1,0:T(8,128)(2,1)S(1)} %copy-done, bf16[4,64,1024]{2,1,0:T(8,128)(2,1)S(1)} %collective-permute-done.10, bf16[4,32,1024]{2,1,0:T(8,128)(2,1)S(1)} %collective-permute-done.9, ...), kind=kOutput, calls=%fused_computation.45 | convolution fusion | flops 1077411840 | bytes 10485764 | tf_op jit(solution)/shard_map/sik,sjk->sij/dot_general | solution.py:68
  108.7 2.6 %fusion.16 = f32[1024,1024]{1,0:T(8,128)S(1)} fusion(bf16[4,1024,1024]{2,1,0:T(8,128)(2,1)S(1)} %fusion.52, bf16[1,4,1024,1024]{3,2,1,0:T(8,128)(2,1)S(1)} %copy-done), kind=kOutput, calls=%fused_computation.21 | convolution fusion | flops 2147483648 | bytes 8388608 | tf_op jit(solution)/shard_map/dot_general | solution.py:74
  111.3 4.3 %fusion.17 = f32[1024,1024]{1,0:T(8,128)} fusion(bf16[4,1024,1024]{2,1,0:T(8,128)(2,1)S(1)} %fusion.52, bf16[1,4,1024,1024]{3,2,1,0:T(8,128)(2,1)S(1)} %copy-done), kind=kOutput, calls=%fused_computation.23 | convolution fusion | flops 2147483648 | bytes 8388608 | tf_op jit(solution)/shard_map/dot_general | solution.py:74
  115.7 4.4 %fusion.18 = f32[1024,1024]{1,0:T(8,128)} fusion(bf16[4,1024,1024]{2,1,0:T(8,128)(2,1)S(1)} %fusion.52, bf16[1,4,1024,1024]{3,2,1,0:T(8,128)(2,1)S(1)} %copy-done), kind=kOutput, calls=%fused_computation.25 | convolution fusion | flops 2147483648 | bytes 8388608 | tf_op jit(solution)/shard_map/dot_general | solution.py:74
  120.1 6.0 %add_convert_fusion = bf16[1024,1024]{1,0:T(8,128)(2,1)S(1)} fusion(f32[1024,1024]{1,0:T(8,128)S(1)} %fusion.16, f32[1024,1024]{1,0:T(8,128)} %fusion.17, f32[1024,1024]{1,0:T(8,128)} %fusion.18, bf16[1,4,1024,1024]{3,2,1,0:T(8,128)(2,1)S(1)} %copy-done, bf16[4,1024,1024]{2,1,0:T(8,128)(2,1)S(1)} %fusion.52), kind=kOutput, calls=%fused_computation.18 | convolution fusion | flops 2151677952 | bytes 18874368 | tf_op jit(solution)/shard_map/dot_general | solution.py:74
  126.9 0.9 fusion.97
  127.7 1.5 mul.45
  129.3 1.4 copy.15
  133.4 0.7 slice_dynamic-update-slice_fusion.4
  134.1 0.7 slice_dynamic-update-slice_fusion.2
  134.9 0.8 slice_dynamic-update-slice_fusion
  135.7 1.5 pad_maximum_fusion
  137.1 1.7 copy.16
  138.8 18.3 %all-to-all-start.1 = ((bf16[16,2,288,128]{3,2,1,0:T(8,128)(2,1)}), bf16[16,2,288,128]{3,2,1,0:T(8,128)(2,1)}, u32[]{:S(2)}, u32[]{:S(2)}) async-start(bf16[16,2,288,128]{3,2,1,0:T(8,128)(2,1)} %copy.16), calls=%async_computation.1 | async-start | bytes 4718592 | tf_op jit(solution)/shard_map/all_to_all | solution.py:99
  157.1 31.2 %all-to-all-done.1 = bf16[16,2,288,128]{3,2,1,0:T(8,128)(2,1)} async-done(((bf16[16,2,288,128]{3,2,1,0:T(8,128)(2,1)}), bf16[16,2,288,128]{3,2,1,0:T(8,128)(2,1)}, u32[]{:S(2)}, u32[]{:S(2)}) %all-to-all-start.1) | async-done | bytes 2359328 | tf_op jit(solution)/shard_map/all_to_all | solution.py:99
  188.3 1.8 fusion.115
  190.1 0.7 fusion.79
  190.9 1.3 gather_fusion.1
  192.9 6.5 %all-to-all-start.2 = ((f32[16,1,8]{2,1,0:T(1,128)}), f32[16,1,8]{2,1,0:T(1,128)S(1)}, u32[]{:S(2)}, u32[]{:S(2)}) async-start(f32[16,1,8]{2,1,0:T(1,128)} %bitcast.25), calls=%async_computation.2 | async-start | bytes 16384 | tf_op jit(solution)/shard_map/all_to_all | solution.py:107
  199.4 2.6 %copy.21 = bf16[1,1,1024,1024]{3,2,1,0:T(8,128)(2,1)} copy(bf16[1,1,1024,1024]{2,3,1,0:T(8,128)(2,1)S(1)} %bitcast.125) | data formatting | bytes 4194304
  202.0 4.5 %all-to-all-done.2 = f32[16,1,8]{2,1,0:T(1,128)S(1)} async-done(((f32[16,1,8]{2,1,0:T(1,128)}), f32[16,1,8]{2,1,0:T(1,128)S(1)}, u32[]{:S(2)}, u32[]{:S(2)}) %all-to-all-start.2) | async-done | bytes 544 | tf_op jit(solution)/shard_map/all_to_all | solution.py:107
  (63 shorter events, 8.9 us)
Async XLA Ops:
  0.6 6.4 %copy-start.7 = (s32[4]{0:T(128)S(1)}, s32[4]{0:T(128)}, u32[]{:S(2)}) copy-start(s32[4]{0:T(128)} %param.6) | copy-start | bytes 52
  0.6 36.8 %all-to-all-start = ((bf16[8,128,1024]{2,1,0:T(8,128)(2,1)}), bf16[8,128,1024]{2,1,0:T(8,128)(2,1)S(1)}, u32[]{:S(2)}, u32[]{:S(2)}) async-start(bf16[8,128,1024]{2,1,0:T(8,128)(2,1)} %bitcast.127), calls=%async_computation | async-start | bytes 4194304 | tf_op jit(solution)/shard_map/all_to_all | solution.py:25
  38.1 23.2 %collective-permute-start.1 = (bf16[4,128,1024]{2,1,0:T(8,128)(2,1)S(1)}, bf16[4,128,1024]{2,1,0:T(8,128)(2,1)S(1)}, u32[]{:S(2)}, u32[]{:S(2)}) collective-permute-start(bf16[4,128,1024]{2,1,0:T(8,128)(2,1)S(1)} %gather_fusion), channel_id=1, source_target_pairs={{0,96},{16,112},{32,0},{48,16},{64,32},{80,48},{96,64},{112,80},{1... | collective-permute-start | bytes 3145736 | tf_op jit(solution)/shard_map/ppermute | solution.py:11
  39.0 24.4 %collective-permute-start = (bf16[4,128,1024]{2,1,0:T(8,128)(2,1)S(1)}, bf16[4,128,1024]{2,1,0:T(8,128)(2,1)S(1)}, u32[]{:S(2)}, u32[]{:S(2)}) collective-permute-start(bf16[4,128,1024]{2,1,0:T(8,128)(2,1)S(1)} %gather_fusion), channel_id=1, source_target_pairs={{0,32},{16,48},{32,64},{48,80},{64,96},{80,112},{96,0},{112,16},{1... | collective-permute-start | bytes 3145736 | tf_op jit(solution)/shard_map/ppermute | solution.py:11
  40.6 3.4 %copy-start = (bf16[1,4,1024,1024]{3,2,1,0:T(8,128)(2,1)S(1)}, bf16[1,4,1024,1024]{3,2,1,0:T(8,128)(2,1)}, u32[]{:S(2)}) copy-start(bf16[1,4,1024,1024]{3,2,1,0:T(8,128)(2,1)} %param.4) | copy-start | bytes 25165828
  40.6 11.5 %collective-permute-start.4 = (bf16[4,64,1024]{2,1,0:T(8,128)(2,1)S(1)}, bf16[4,64,1024]{2,1,0:T(8,128)(2,1)}, u32[]{:S(2)}, u32[]{:S(2)}) collective-permute-start(bf16[4,64,1024]{2,1,0:T(8,128)(2,1)S(1)} %get-tuple-element.13), channel_id=1, source_target_pairs={{0,16},{16,0},{32,48},{48,32},{64,80},{80,64},{96,112},{112,96},{1... | collective-permute-start | bytes 1572872 | tf_op jit(solution)/shard_map/ppermute | solution.py:15
  52.1 22.5 %collective-permute-start.6 = (bf16[4,64,1024]{2,1,0:T(8,128)(2,1)}, bf16[4,64,1024]{2,1,0:T(8,128)(2,1)S(1)}, u32[]{:S(2)}, u32[]{:S(2)}) collective-permute-start(bf16[4,64,1024]{2,1,0:T(8,128)(2,1)} %collective-permute-done.4), channel_id=1, source_target_pairs={{0,32},{16,48},{32,64},{48,80},{64,96},{80,112},{96,0},{112,16},{1... | collective-permute-start | bytes 1572872 | tf_op jit(solution)/shard_map/ppermute | solution.py:11
  52.4 22.3 %collective-permute-start.7 = (bf16[4,64,1024]{2,1,0:T(8,128)(2,1)}, bf16[4,64,1024]{2,1,0:T(8,128)(2,1)S(1)}, u32[]{:S(2)}, u32[]{:S(2)}) collective-permute-start(bf16[4,64,1024]{2,1,0:T(8,128)(2,1)} %collective-permute-done.4), channel_id=1, source_target_pairs={{0,96},{16,112},{32,0},{48,16},{64,32},{80,48},{96,64},{112,80},{1... | collective-permute-start | bytes 1572872 | tf_op jit(solution)/shard_map/ppermute | solution.py:11
  61.4 22.7 %collective-permute-start.3 = (bf16[4,64,1024]{2,1,0:T(8,128)(2,1)S(1)}, bf16[4,64,1024]{2,1,0:T(8,128)(2,1)}, u32[]{:S(2)}, u32[]{:S(2)}) collective-permute-start(bf16[4,64,1024]{2,1,0:T(8,128)(2,1)S(1)} %get-tuple-element.18), channel_id=1, source_target_pairs={{0,96},{16,112},{32,0},{48,16},{64,32},{80,48},{96,64},{112,80},{1... | collective-permute-start | bytes 1572872 | tf_op jit(solution)/shard_map/ppermute | solution.py:11
  63.5 22.4 %collective-permute-start.2 = (bf16[4,64,1024]{2,1,0:T(8,128)(2,1)S(1)}, bf16[4,64,1024]{2,1,0:T(8,128)(2,1)S(1)}, u32[]{:S(2)}, u32[]{:S(2)}) collective-permute-start(bf16[4,64,1024]{2,1,0:T(8,128)(2,1)S(1)} %get-tuple-element.16), channel_id=1, source_target_pairs={{0,32},{16,48},{32,64},{48,80},{64,96},{80,112},{96,0},{112,16},{1... | collective-permute-start | bytes 1572872 | tf_op jit(solution)/shard_map/ppermute | solution.py:11
  63.7 30.8 %collective-permute-start.5 = (bf16[3,4,64,1024]{3,2,1,0:T(8,128)(2,1)S(1)}, bf16[3,4,64,1024]{3,2,1,0:T(8,128)(2,1)S(1)}, u32[]{:S(2)}, u32[]{:S(2)}) collective-permute-start(bf16[3,4,64,1024]{3,2,1,0:T(8,128)(2,1)S(1)} %pad_maximum_fusion.1), channel_id=1, source_target_pairs={{0,16},{16,0},{32,48},{48,32},{64,80},{80,64},{96,112},{112,96},{1... | collective-permute-start | bytes 4718600 | tf_op jit(solution)/shard_map/ppermute | solution.py:15
  74.6 0.8 copy-start.4
  74.6 30.0 %collective-permute-start.8 = (bf16[4,32,1024]{2,1,0:T(8,128)(2,1)S(1)}, bf16[4,32,1024]{2,1,0:T(8,128)(2,1)S(1)}, u32[]{:S(2)}, u32[]{:S(2)}) collective-permute-start(bf16[4,32,1024]{2,1,0:T(8,128)(2,1)S(1)} %slice.169), channel_id=1, source_target_pairs={{0,32},{16,48},{32,64},{48,80},{64,96},{80,112},{96,0},{112,16},{1... | collective-permute-start | bytes 786440 | tf_op jit(solution)/shard_map/ppermute | solution.py:11
  74.7 0.8 copy-start.2
  75.6 29.1 %collective-permute-start.9 = (bf16[4,32,1024]{2,1,0:T(8,128)(2,1)S(1)}, bf16[4,32,1024]{2,1,0:T(8,128)(2,1)S(1)}, u32[]{:S(2)}, u32[]{:S(2)}) collective-permute-start(bf16[4,32,1024]{2,1,0:T(8,128)(2,1)S(1)} %slice.170), channel_id=1, source_target_pairs={{0,96},{16,112},{32,0},{48,16},{64,32},{80,48},{96,64},{112,80},{1... | collective-permute-start | bytes 786440 | tf_op jit(solution)/shard_map/ppermute | solution.py:11
  84.0 21.7 %collective-permute-start.10 = (bf16[4,64,1024]{2,1,0:T(8,128)(2,1)}, bf16[4,64,1024]{2,1,0:T(8,128)(2,1)S(1)}, u32[]{:S(2)}, u32[]{:S(2)}) collective-permute-start(bf16[4,64,1024]{2,1,0:T(8,128)(2,1)} %collective-permute-done.3), channel_id=1, source_target_pairs={{0,16},{16,0},{32,48},{48,32},{64,80},{80,64},{96,112},{112,96},{1... | collective-permute-start | bytes 1572872 | tf_op jit(solution)/shard_map/ppermute | solution.py:15
  94.7 4.1 %copy-start.5 = (bf16[4,64,1024]{2,1,0:T(8,128)(2,1)S(1)}, bf16[4,64,1024]{2,1,0:T(8,128)(2,1)}, u32[]{:S(2)}) copy-start(bf16[4,64,1024]{2,1,0:T(8,128)(2,1)} %copy-done.4) | copy-start | bytes 1572868
  98.8 2.9 %copy-start.3 = (bf16[4,64,1024]{2,1,0:T(8,128)(2,1)S(1)}, bf16[4,64,1024]{2,1,0:T(8,128)(2,1)}, u32[]{:S(2)}) copy-start(bf16[4,64,1024]{2,1,0:T(8,128)(2,1)} %copy-done.2) | copy-start | bytes 1572868
  130.7 5.0 %copy-start.1 = (bf16[4608,128]{1,0:T(8,128)(2,1)S(1)}, bf16[4608,128]{1,0:T(8,128)(2,1)}, u32[]{:S(2)}) copy-start(bf16[4608,128]{1,0:T(8,128)(2,1)} %copy.15) | copy-start | bytes 3538948
  138.8 18.3 %copy-start.6 = (s32[128,2]{0,1:T(2,128)S(1)}, s32[128,2]{0,1:T(2,128)}, u32[]{:S(2)}) copy-start(s32[128,2]{0,1:T(2,128)} %param.7) | copy-start | bytes 3076
  138.8 49.5 %all-to-all-start.1 = ((bf16[16,2,288,128]{3,2,1,0:T(8,128)(2,1)}), bf16[16,2,288,128]{3,2,1,0:T(8,128)(2,1)}, u32[]{:S(2)}, u32[]{:S(2)}) async-start(bf16[16,2,288,128]{3,2,1,0:T(8,128)(2,1)} %copy.16), calls=%async_computation.1 | async-start | bytes 4718592 | tf_op jit(solution)/shard_map/all_to_all | solution.py:99
  192.9 13.6 %all-to-all-start.2 = ((f32[16,1,8]{2,1,0:T(1,128)}), f32[16,1,8]{2,1,0:T(1,128)S(1)}, u32[]{:S(2)}, u32[]{:S(2)}) async-start(f32[16,1,8]{2,1,0:T(1,128)} %bitcast.25), calls=%async_computation.2 | async-start | bytes 16384 | tf_op jit(solution)/shard_map/all_to_all | solution.py:107

commit v7 on v6

--- a/solution.py
+++ b/solution.py
@@ -63,16 +63,26 @@
     block_order = propagators.shape[1]
     pieces = source_pieces(own_elemental, src_times)
     rows = pieces[0][1].shape[1]
-    halves = jnp.zeros((NSRC, block_order, block_order), jnp.bfloat16)
-    for origin, piece in pieces:
-        block = jnp.einsum(
+    columns = jnp.concatenate(
+        [lax.dynamic_slice_in_dim(propagators, origin * rows, rows, 2) for origin, _ in pieces],
+        axis=2,
+    )
+    blocks = [
+        jnp.einsum(
             "sik,sjk->sij", piece, propagators, preferred_element_type=jnp.float32
         ).astype(jnp.bfloat16)
-        halves = lax.dynamic_update_slice_in_dim(halves, block, origin * rows, 1)
+        for _, piece in pieces
+    ]
+    halves = jnp.concatenate(blocks, axis=1)
+    early = 4 * rows
     summed = jnp.zeros((block_order, block_order), jnp.float32)
     for source in range(NSRC):
         summed = summed + jnp.dot(
-            propagators[source], halves[source], preferred_element_type=jnp.float32
+            columns[source, :, :early], halves[source, :early], preferred_element_type=jnp.float32
+        )
+    for source in range(NSRC):
+        summed = summed + jnp.dot(
+            columns[source, :, early:], halves[source, early:], preferred_element_type=jnp.float32
         )
     meson = summed.astype(jnp.bfloat16)
 

time: 208 us -> 212 us (1.019)
  matrix products: 43.7 us -> 59.8 us
  starting transfers between devices: 40 us -> 26.5 us
  blocking collectives: 0 us -> 13.3 us
  waiting for transfers between devices: 91.8 us -> 81.9 us
    dot_general x4 -> x8, matrix products: 17.4 us -> 32.2 us  [the longest x4 19.3 us: body(): jnp.dot(columns[source, :, early:], halves[source, early:], preferred_ele...]
    all_to_all x0 -> x1, blocking collectives: none -> 13.3 us  [body(): spread = lax.all_to_all(per_diagram.reshape(n_m, -1), 'mom', 0, 0)]
    all_to_all x1, starting transfers between devices: 18.3 us -> 11.3 us  [body(): received = lax.all_to_all(slices, 'mom', 0, 0)]
    all_to_all x1 -> x0, starting transfers between devices: 6.53 us -> none  [body(): spread = lax.all_to_all(per_diagram.reshape(n_m, -1), 'mom', 0, 0)]
    concatenate x0 -> x3, other arithmetic: none -> 4.95 us  [the longest x1 3.87 us: body(): jnp.concatenate([lax.dynamic_slice_in_dim(propagators, origin * rows, row...]
    unnamed x7 -> x8, other arithmetic: 5.41 us -> 0.53 us
    dynamic_slice x0 -> x1, local copies, waits for them, and re-layouts: none -> 4.52 us  [body(): lax.dynamic_slice_in_dim(propagators, origin * rows, rows, 2)]
    all_to_all x1 -> x0, waiting for transfers between devices: 4.46 us -> none  [body(): spread = lax.all_to_all(per_diagram.reshape(n_m, -1), 'mom', 0, 0)]
  transfers between devices with their start and end apart: 14 -> 13, of which waited for: 10 -> 9; matrix products, arithmetic and copies ran while one was open for 16% -> 20% of each run, Pallas kernels for 0% -> 0%
where the time goes in v7:
time: 212 us
  waiting for transfers between devices  81.9 us (39%)
  matrix products  59.8 us (28%)
  starting transfers between devices  26.5 us (12%)
  local copies, waits for them, and re-layouts  20.1 us (9%)
  blocking collectives  13.3 us (6%)
  other arithmetic  9.21 us (4%)
    all_to_all x1, waiting for transfers between devices, body(): received = lax.all_to_all(slices, 'mom', 0, 0)  31.1 us
    dot_general x8, matrix products, body(): jnp.einsum('sik,sjk->sij', piece, propagators, preferred_element_type=jnp...  26.9 us
    all_to_all x1, waiting for transfers between devices, source_pieces(): received = lax.all_to_all(pieces, 'tsink', 0, 0)  21.5 us
    ppermute x8, waiting for transfers between devices, shifted(): return lax.ppermute(block, 'tsink', pairs)  20.1 us
    dot_general x4, matrix products, body(): jnp.dot(columns[source, :, early:], halves[source, early:], preferred_ele...  19.3 us
    all_to_all x1, blocking collectives, body(): spread = lax.all_to_all(per_diagram.reshape(n_m, -1), 'mom', 0, 0)  13.3 us
    dot_general x4, matrix products, body(): jnp.dot(columns[source, :, :early], halves[source, :early], preferred_ele...  12.9 us
    all_to_all x1, starting transfers between devices, body(): received = lax.all_to_all(slices, 'mom', 0, 0)  11.3 us
  transfers between devices with their start and end apart: 13, of which 9 were waited for; matrix products, arithmetic and copies ran while one was open for 20% of the time, Pallas kernels for 0%

profile of v7, /device:TPU:1, one launch (start us, length us, event | category | flops | bytes accessed | tf_op | source)
XLA Modules:
  0.0 212.0 jit_solution(11942208195791534190)
XLA Ops:
  0.6 6.2 %all-to-all-start = ((bf16[8,128,1024]{2,1,0:T(8,128)(2,1)}), bf16[8,128,1024]{2,1,0:T(8,128)(2,1)S(1)}, u32[]{:S(2)}, u32[]{:S(2)}) async-start(bf16[8,128,1024]{2,1,0:T(8,128)(2,1)} %bitcast.149), calls=%async_computation | async-start | bytes 4194304 | tf_op jit(solution)/shard_map/all_to_all | solution.py:25
  7.5 4.5 %dynamic-slice_bitcast_fusion.7 = (bf16[4,1024,128]{2,1,0:T(8,128)(2,1)S(1)}, bf16[4,1024,128]{2,1,0:T(8,128)(2,1)S(1)}, bf16[4,1024,128]{2,1,0:T(8,128)(2,1)S(1...) fusion(bf16[1,4,1024,1024]{3,2,1,0:T(8,128)(2,1)} %param.4, ...), kind=kLoop, calls=%fused_computation.84 | loop fusion | bytes 16777248 | tf_op jit(solution)/shard_map/dynamic_slice | solution.py:67
  12.1 3.9 %pad_maximum_fusion = (bf16[4,1024,512]{2,1,0:T(8,128)(2,1)}, bf16[4,1024,512]{2,1,0:T(8,128)(2,1)}) fusion(bf16[4,1024,128]{2,1,0:T(8,128)(2,1)S(1)} %get-tuple-element.5, bf16[4,1024,128]{2,1,0:T(8,128)(2,1)S(1)} %get-tuple-element.6, bf16[4,1024,128]{2,1,0:T(8,128)(2,1)S(1)} %get-tuple-element.7, bf16[4,1024,128]{2,1,0:T(8,128)(2,1)S(1)} %get-tuple-element.2, ...), kind=kLoop, calls=%fused_computation.18 | loop fusion | flops 33554432 | bytes 16777216 | tf_op jit(solution)/shard_map/concatenate | solution.py:66
  15.9 21.5 %all-to-all-done = bf16[8,128,1024]{2,1,0:T(8,128)(2,1)S(1)} async-done(((bf16[8,128,1024]{2,1,0:T(8,128)(2,1)}), bf16[8,128,1024]{2,1,0:T(8,128)(2,1)S(1)}, u32[]{:S(2)}, u32[]{:S(2)}) %all-to-all-start) | async-done | bytes 2097184 | tf_op jit(solution)/shard_map/all_to_all | solution.py:25
  38.2 0.8 fusion.66
  39.0 1.5 collective-permute-start
  40.6 6.4 %fusion.16 = bf16[4,128,1024]{2,1,0:T(8,128)(2,1)S(1)} fusion(bf16[4,128,1024]{2,1,0:T(8,128)(2,1)S(1)} %gather_fusion, bf16[1,4,1024,1024]{3,2,1,0:T(8,128)(2,1)} %param.4), kind=kOutput, calls=%fused_computation.25 | convolution fusion | flops 1074266112 | bytes 10485760 | tf_op jit(solution)/shard_map/sik,sjk->sij/dot_general | solution.py:71
  47.1 4.9 %collective-permute-done.4 = bf16[4,64,1024]{2,1,0:T(8,128)(2,1)S(1)} collective-permute-done((bf16[4,64,1024]{2,1,0:T(8,128)(2,1)S(1)}, bf16[4,64,1024]{2,1,0:T(8,128)(2,1)S(1)}, u32[]{:S(2)}, u32[]{:S(2)}) %collective-permute-start.4) | collective-permute-done | bytes 524320 | tf_op jit(solution)/shard_map/ppermute | solution.py:15
  52.2 2.4 %collective-permute-start.7 = (bf16[4,64,1024]{2,1,0:T(8,128)(2,1)S(1)}, bf16[4,64,1024]{2,1,0:T(8,128)(2,1)S(1)}, u32[]{:S(2)}, u32[]{:S(2)}) collective-permute-start(bf16[4,64,1024]{2,1,0:T(8,128)(2,1)S(1)} %collective-permute-done.4), channel_id=1, source_target_pairs={{0,96},{16,112},{32,0},{48,16},{64,32},{80,48},{96,64},{112,80},{1... | collective-permute-start | bytes 1572872 | tf_op jit(solution)/shard_map/ppermute | solution.py:11
  54.6 6.7 %collective-permute-done.1 = bf16[4,128,1024]{2,1,0:T(8,128)(2,1)S(1)} collective-permute-done((bf16[4,128,1024]{2,1,0:T(8,128)(2,1)S(1)}, bf16[4,128,1024]{2,1,0:T(8,128)(2,1)S(1)}, u32[]{:S(2)}, u32[]{:S(2)}) %collective-permute-start.1) | collective-permute-done | bytes 1048608 | tf_op jit(solution)/shard_map/ppermute | solution.py:11
  61.4 1.6 collective-permute-start.3
  63.8 10.8 %collective-permute-done.6 = bf16[4,64,1024]{2,1,0:T(8,128)(2,1)S(1)} collective-permute-done((bf16[4,64,1024]{2,1,0:T(8,128)(2,1)S(1)}, bf16[4,64,1024]{2,1,0:T(8,128)(2,1)S(1)}, u32[]{:S(2)}, u32[]{:S(2)}) %collective-permute-start.6) | collective-permute-done | bytes 524320 | tf_op jit(solution)/shard_map/ppermute | solution.py:11
  74.7 2.9 %collective-permute-start.9 = (bf16[4,32,1024]{2,1,0:T(8,128)(2,1)S(1)}, bf16[4,32,1024]{2,1,0:T(8,128)(2,1)S(1)}, u32[]{:S(2)}, u32[]{:S(2)}) collective-permute-start(bf16[4,32,1024]{2,1,0:T(8,128)(2,1)S(1)} %slice.223), channel_id=1, source_target_pairs={{0,96},{16,112},{32,0},{48,16},{64,32},{80,48},{96,64},{112,80},{1... | collective-permute-start | bytes 786440 | tf_op jit(solution)/shard_map/ppermute | solution.py:11
  77.6 3.0 %fusion.19 = bf16[4,128,1024]{2,1,0:T(8,128)(2,1)S(1)} fusion(bf16[4,128,1024]{2,1,0:T(8,128)(2,1)S(1)} %collective-permute-done, bf16[1,4,1024,1024]{3,2,1,0:T(8,128)(2,1)S(1)} %bitcast.137), kind=kOutput, calls=%fused_computation.26 | convolution fusion | flops 1074266112 | bytes 10485760 | tf_op jit(solution)/shard_map/sik,sjk->sij/dot_general | solution.py:71
  80.6 2.9 %fusion.22 = bf16[4,128,1024]{2,1,0:T(8,128)(2,1)S(1)} fusion(bf16[4,128,1024]{2,1,0:T(8,128)(2,1)S(1)} %collective-permute-done.1, bf16[1,4,1024,1024]{3,2,1,0:T(8,128)(2,1)S(1)} %bitcast.137), kind=kOutput, calls=%fused_computation.27 | convolution fusion | flops 1074266112 | bytes 10485760 | tf_op jit(solution)/shard_map/sik,sjk->sij/dot_general | solution.py:71
  83.8 2.0 collective-permute-done.2
  85.8 2.9 %fusion.25 = bf16[4,128,1024]{2,1,0:T(8,128)(2,1)S(1)} fusion(bf16[1,4,1024,1024]{3,2,1,0:T(8,128)(2,1)S(1)} %bitcast.137, bf16[4,64,1024]{2,1,0:T(8,128)(2,1)S(1)} %collective-permute-done.3, bf16[4,64,1024]{2,1,0:T(8,128)(2,1)S(1)} %collective-permute-done.2), kind=kOutput, calls=%fused_computation.28 | convolution fusion | flops 1076363264 | bytes 10485760 | tf_op jit(solution)/shard_map/sik,sjk->sij/dot_general | solution.py:71
  89.1 1.8 copy-done.2
  90.9 3.3 %fusion.45 = f32[1024,1024]{1,0:T(8,128)} fusion(bf16[4,512,1024]{2,1,0:T(8,128)(2,1)S(1)} %pad_maximum_fusion.1, bf16[4,1024,512]{2,1,0:T(8,128)(2,1)S(1)} %copy-done.2), kind=kOutput, calls=%fused_computation.49 | convolution fusion | flops 1073741824 | bytes 6291456 | tf_op jit(solution)/shard_map/dot_general | solution.py:80
  94.2 3.2 %fusion.46 = f32[1024,1024]{1,0:T(8,128)} fusion(bf16[4,512,1024]{2,1,0:T(8,128)(2,1)S(1)} %pad_maximum_fusion.1, bf16[4,1024,512]{2,1,0:T(8,128)(2,1)S(1)} %copy-done.2), kind=kOutput, calls=%fused_computation.52 | convolution fusion | flops 1073741824 | bytes 6291456 | tf_op jit(solution)/shard_map/dot_general | solution.py:80
  97.4 3.2 %fusion.47 = f32[1024,1024]{1,0:T(8,128)} fusion(bf16[4,512,1024]{2,1,0:T(8,128)(2,1)S(1)} %pad_maximum_fusion.1, bf16[4,1024,512]{2,1,0:T(8,128)(2,1)S(1)} %copy-done.2), kind=kOutput, calls=%fused_computation.55 | convolution fusion | flops 1073741824 | bytes 6291456 | tf_op jit(solution)/shard_map/dot_general | solution.py:80
  100.6 3.2 %fusion.48 = f32[1024,1024]{1,0:T(8,128)} fusion(bf16[4,512,1024]{2,1,0:T(8,128)(2,1)S(1)} %pad_maximum_fusion.1, bf16[4,1024,512]{2,1,0:T(8,128)(2,1)S(1)} %copy-done.2), kind=kOutput, calls=%fused_computation.58 | convolution fusion | flops 1073741824 | bytes 6291456 | tf_op jit(solution)/shard_map/dot_general | solution.py:80
  103.8 4.3 %collective-permute-done.10 = bf16[4,64,1024]{2,1,0:T(8,128)(2,1)S(1)} collective-permute-done((bf16[4,64,1024]{2,1,0:T(8,128)(2,1)S(1)}, bf16[4,64,1024]{2,1,0:T(8,128)(2,1)S(1)}, u32[]{:S(2)}, u32[]{:S(2)}) %collective-permute-start.10) | collective-permute-done | bytes 524320 | tf_op jit(solution)/shard_map/ppermute | solution.py:15
  108.1 2.9 %fusion.37 = bf16[4,128,1024]{2,1,0:T(8,128)(2,1)S(1)} fusion(bf16[1,4,1024,1024]{3,2,1,0:T(8,128)(2,1)S(1)} %bitcast.137, bf16[4,64,1024]{2,1,0:T(8,128)(2,1)S(1)} %collective-permute-done.10, bf16[4,32,1024]{2,1,0:T(8,128)(2,1)S(1)} %collective-permute-done.9, bf16[4,32,1024]{2,1,0:T(8,128)(2,1)S(1)} %collective-permute-done.8), kind=kOutput, calls=%fused_computation.32 | convolution fusion | flops 1077411840 | bytes 10485760 | tf_op jit(solution)/shard_map/sik,sjk->sij/dot_general | solution.py:71
  111.2 2.9 %fusion.31 = bf16[4,128,1024]{2,1,0:T(8,128)(2,1)S(1)} fusion(bf16[1,4,1024,1024]{3,2,1,0:T(8,128)(2,1)S(1)} %bitcast.137, bf16[4,64,1024]{2,1,0:T(8,128)(2,1)S(1)} %get-tuple-element.14, bf16[4,64,1024]{2,1,0:T(8,128)(2,1)S(1)} %collective-permute-done.6), kind=kOutput, calls=%fused_computation.30 | convolution fusion | flops 1076363264 | bytes 10485760 | tf_op jit(solution)/shard_map/sik,sjk->sij/dot_general | solution.py:71
  114.1 2.9 %fusion.34 = bf16[4,128,1024]{2,1,0:T(8,128)(2,1)S(1)} fusion(bf16[1,4,1024,1024]{3,2,1,0:T(8,128)(2,1)S(1)} %bitcast.137, bf16[4,64,1024]{2,1,0:T(8,128)(2,1)S(1)} %get-tuple-element.13, bf16[4,64,1024]{2,1,0:T(8,128)(2,1)S(1)} %collective-permute-done.7), kind=kOutput, calls=%fused_computation.31 | convolution fusion | flops 1076363264 | bytes 10485760 | tf_op jit(solution)/shard_map/sik,sjk->sij/dot_general | solution.py:71
  117.0 2.9 %fusion.28 = bf16[4,128,1024]{2,1,0:T(8,128)(2,1)S(1)} fusion(bf16[1,4,1024,1024]{3,2,1,0:T(8,128)(2,1)S(1)} %bitcast.137, bf16[4,64,1024]{2,1,0:T(8,128)(2,1)S(1)} %get-tuple-element.12, bf16[4,64,1024]{2,1,0:T(8,128)(2,1)S(1)} %collective-permute-done.4), kind=kOutput, calls=%fused_computation.29 | convolution fusion | flops 1076363264 | bytes 10485760 | tf_op jit(solution)/shard_map/sik,sjk->sij/dot_general | solution.py:71
  119.9 0.7 pad_maximum_fusion.3
  120.6 1.5 copy-done.1
  122.1 3.2 %fusion.44 = f32[1024,1024]{1,0:T(8,128)} fusion(bf16[4,512,1024]{2,1,0:T(8,128)(2,1)S(1)} %pad_maximum_fusion.3, bf16[4,1024,512]{2,1,0:T(8,128)(2,1)S(1)} %copy-done.1), kind=kOutput, calls=%fused_computation.46 | convolution fusion | flops 1073741824 | bytes 6291456 | tf_op jit(solution)/shard_map/dot_general | solution.py:84
  125.4 3.3 %fusion.43 = f32[1024,1024]{1,0:T(8,128)} fusion(bf16[4,512,1024]{2,1,0:T(8,128)(2,1)S(1)} %pad_maximum_fusion.3, bf16[4,1024,512]{2,1,0:T(8,128)(2,1)S(1)} %copy-done.1), kind=kOutput, calls=%fused_computation.43 | convolution fusion | flops 1073741824 | bytes 6291456 | tf_op jit(solution)/shard_map/dot_general | solution.py:84
  128.6 3.2 %fusion.42 = f32[1024,1024]{1,0:T(8,128)} fusion(bf16[4,512,1024]{2,1,0:T(8,128)(2,1)S(1)} %pad_maximum_fusion.3, bf16[4,1024,512]{2,1,0:T(8,128)(2,1)S(1)} %copy-done.1), kind=kOutput, calls=%fused_computation.40 | convolution fusion | flops 1073741824 | bytes 6291456 | tf_op jit(solution)/shard_map/dot_general | solution.py:84
  131.9 9.5 %add_convert_fusion = bf16[1024,1024]{1,0:T(8,128)(2,1)S(1)} fusion(f32[1024,1024]{1,0:T(8,128)} %fusion.42, f32[1024,1024]{1,0:T(8,128)} %fusion.43, f32[1024,1024]{1,0:T(8,128)} %fusion.44, f32[1024,1024]{1,0:T(8,128)S(1)} %copy-done.3, f32[1024,1024]{1,0:T(8,128)} %fusion.46, f32[1024,1024]{1,0:T(8,128)} %fusion.48, f32[1024,1024]{1,0:T(8,128)} %fusion.47, ...), kind=kOutput, calls=%fused_computation.22 | convolution fusion | flops 1082130432 | bytes 33554432 | tf_op jit(solution)/shard_map/dot_general | solution.py:84
  141.8 1.0 constant_dynamic-update-slice_fusion.2
  143.5 0.7 slice_dynamic-update-slice_fusion.10
  144.2 0.7 slice_dynamic-update-slice_fusion.8
  144.8 0.7 slice_dynamic-update-slice_fusion.6
  145.6 0.7 slice_dynamic-update-slice_fusion.4
  146.3 0.8 slice_dynamic-update-slice_fusion.2
  147.0 0.7 slice_dynamic-update-slice_fusion
  147.8 1.7 copy.13
  149.5 1.9 mul.45
  151.6 1.6 copy.14
  153.3 11.3 %all-to-all-start.1 = ((bf16[16,2,288,128]{3,2,1,0:T(8,128)(2,1)}), bf16[16,2,288,128]{3,2,1,0:T(8,128)(2,1)S(1)}, u32[]{:S(2)}, u32[]{:S(2)}) async-start(bf16[16,2,288,128]{3,2,1,0:T(8,128)(2,1)} %copy.14), calls=%async_computation.1 | async-start | bytes 4718592 | tf_op jit(solution)/shard_map/all_to_all | solution.py:109
  164.6 31.1 %all-to-all-done.1 = bf16[16,2,288,128]{3,2,1,0:T(8,128)(2,1)S(1)} async-done(((bf16[16,2,288,128]{3,2,1,0:T(8,128)(2,1)}), bf16[16,2,288,128]{3,2,1,0:T(8,128)(2,1)S(1)}, u32[]{:S(2)}, u32[]{:S(2)}) %all-to-all-start.1) | async-done | bytes 2359328 | tf_op jit(solution)/shard_map/all_to_all | solution.py:109
  195.9 0.7 fusion.41
  196.7 1.3 gather_fusion.1
  198.1 13.3 %all_to_all.19 = f32[16,1,8]{2,1,0:T(1,128)S(1)} all-to-all(f32[16,1,8]{2,1,0:T(1,128)S(1)} %bitcast.150), channel_id=1, replica_groups=mesh['tsink'=8,'mom'=16] {'mom'}, dimensions={0} | all-to-all | bytes 1024 | tf_op jit(solution)/shard_map/all_to_all | solution.py:117
  (74 shorter events, 5.7 us)
Async XLA Ops:
  0.6 6.3 %copy-start.7 = (s32[4]{0:T(128)S(1)}, s32[4]{0:T(128)}, u32[]{:S(2)}) copy-start(s32[4]{0:T(128)} %param.6) | copy-start | bytes 52
  0.6 36.8 %all-to-all-start = ((bf16[8,128,1024]{2,1,0:T(8,128)(2,1)}), bf16[8,128,1024]{2,1,0:T(8,128)(2,1)S(1)}, u32[]{:S(2)}, u32[]{:S(2)}) async-start(bf16[8,128,1024]{2,1,0:T(8,128)(2,1)} %bitcast.149), calls=%async_computation | async-start | bytes 4194304 | tf_op jit(solution)/shard_map/all_to_all | solution.py:25
  7.5 4.5 %copy-start.4 = (bf16[4608,128]{1,0:T(8,128)(2,1)}, bf16[4608,128]{1,0:T(8,128)(2,1)S(1)}, u32[]{:S(2)}) copy-start(bf16[4608,128]{1,0:T(8,128)(2,1)S(1)} %fusion.67) | copy-start | bytes 3538948
  38.1 23.2 %collective-permute-start.1 = (bf16[4,128,1024]{2,1,0:T(8,128)(2,1)S(1)}, bf16[4,128,1024]{2,1,0:T(8,128)(2,1)S(1)}, u32[]{:S(2)}, u32[]{:S(2)}) collective-permute-start(bf16[4,128,1024]{2,1,0:T(8,128)(2,1)S(1)} %gather_fusion), channel_id=1, source_target_pairs={{0,96},{16,112},{32,0},{48,16},{64,32},{80,48},{96,64},{112,80},{1... | collective-permute-start | bytes 3145736 | tf_op jit(solution)/shard_map/ppermute | solution.py:11
  39.0 24.4 %collective-permute-start = (bf16[4,128,1024]{2,1,0:T(8,128)(2,1)S(1)}, bf16[4,128,1024]{2,1,0:T(8,128)(2,1)S(1)}, u32[]{:S(2)}, u32[]{:S(2)}) collective-permute-start(bf16[4,128,1024]{2,1,0:T(8,128)(2,1)S(1)} %gather_fusion), channel_id=1, source_target_pairs={{0,32},{16,48},{32,64},{48,80},{64,96},{80,112},{96,0},{112,16},{1... | collective-permute-start | bytes 3145736 | tf_op jit(solution)/shard_map/ppermute | solution.py:11
  40.4 37.2 %slice-start = ((s8[8388608]{0:T(1024)(128)(4,1)}), s8[4194304]{0:T(1024)(128)(4,1)S(1)}, s32[]{:S(2)}) async-start(s8[8388608]{0:T(1024)(128)(4,1)} %bitcast.136), calls=%async_computation.3 | async-start | bytes 8388608
  40.5 37.1 %slice-start.1 = ((s8[8388608]{0:T(1024)(128)(4,1)}), s8[4194304]{0:T(1024)(128)(4,1)S(1)}, s32[]{:S(2)}) async-start(s8[8388608]{0:T(1024)(128)(4,1)} %bitcast.136), calls=%async_computation.4 | async-start | bytes 8388608
  40.5 11.4 %collective-permute-start.4 = (bf16[4,64,1024]{2,1,0:T(8,128)(2,1)S(1)}, bf16[4,64,1024]{2,1,0:T(8,128)(2,1)S(1)}, u32[]{:S(2)}, u32[]{:S(2)}) collective-permute-start(bf16[4,64,1024]{2,1,0:T(8,128)(2,1)S(1)} %get-tuple-element.18), channel_id=1, source_target_pairs={{0,16},{16,0},{32,48},{48,32},{64,80},{80,64},{96,112},{112,96},{1... | collective-permute-start | bytes 1572872 | tf_op jit(solution)/shard_map/ppermute | solution.py:15
  52.0 22.6 %collective-permute-start.6 = (bf16[4,64,1024]{2,1,0:T(8,128)(2,1)S(1)}, bf16[4,64,1024]{2,1,0:T(8,128)(2,1)S(1)}, u32[]{:S(2)}, u32[]{:S(2)}) collective-permute-start(bf16[4,64,1024]{2,1,0:T(8,128)(2,1)S(1)} %collective-permute-done.4), channel_id=1, source_target_pairs={{0,32},{16,48},{32,64},{48,80},{64,96},{80,112},{96,0},{112,16},{1... | collective-permute-start | bytes 1572872 | tf_op jit(solution)/shard_map/ppermute | solution.py:11
  52.2 22.4 %collective-permute-start.7 = (bf16[4,64,1024]{2,1,0:T(8,128)(2,1)S(1)}, bf16[4,64,1024]{2,1,0:T(8,128)(2,1)S(1)}, u32[]{:S(2)}, u32[]{:S(2)}) collective-permute-start(bf16[4,64,1024]{2,1,0:T(8,128)(2,1)S(1)} %collective-permute-done.4), channel_id=1, source_target_pairs={{0,96},{16,112},{32,0},{48,16},{64,32},{80,48},{96,64},{112,80},{1... | collective-permute-start | bytes 1572872 | tf_op jit(solution)/shard_map/ppermute | solution.py:11
  61.4 22.4 %collective-permute-start.3 = (bf16[4,64,1024]{2,1,0:T(8,128)(2,1)S(1)}, bf16[4,64,1024]{2,1,0:T(8,128)(2,1)S(1)}, u32[]{:S(2)}, u32[]{:S(2)}) collective-permute-start(bf16[4,64,1024]{2,1,0:T(8,128)(2,1)S(1)} %get-tuple-element.20), channel_id=1, source_target_pairs={{0,96},{16,112},{32,0},{48,16},{64,32},{80,48},{96,64},{112,80},{1... | collective-permute-start | bytes 1572872 | tf_op jit(solution)/shard_map/ppermute | solution.py:11
  63.4 22.4 %collective-permute-start.2 = (bf16[4,64,1024]{2,1,0:T(8,128)(2,1)S(1)}, bf16[4,64,1024]{2,1,0:T(8,128)(2,1)S(1)}, u32[]{:S(2)}, u32[]{:S(2)}) collective-permute-start(bf16[4,64,1024]{2,1,0:T(8,128)(2,1)S(1)} %get-tuple-element.15), channel_id=1, source_target_pairs={{0,32},{16,48},{32,64},{48,80},{64,96},{80,112},{96,0},{112,16},{1... | collective-permute-start | bytes 1572872 | tf_op jit(solution)/shard_map/ppermute | solution.py:11
  63.7 47.3 %collective-permute-start.5 = (bf16[3,4,64,1024]{3,2,1,0:T(8,128)(2,1)S(1)}, bf16[3,4,64,1024]{3,2,1,0:T(8,128)(2,1)S(1)}, u32[]{:S(2)}, u32[]{:S(2)}) collective-permute-start(bf16[3,4,64,1024]{3,2,1,0:T(8,128)(2,1)S(1)} %pad_maximum_fusion.5), channel_id=1, source_target_pairs={{0,16},{16,0},{32,48},{48,32},{64,80},{80,64},{96,112},{112,96},{1... | collective-permute-start | bytes 4718600 | tf_op jit(solution)/shard_map/ppermute | solution.py:15
  74.6 29.3 %collective-permute-start.8 = (bf16[4,32,1024]{2,1,0:T(8,128)(2,1)S(1)}, bf16[4,32,1024]{2,1,0:T(8,128)(2,1)S(1)}, u32[]{:S(2)}, u32[]{:S(2)}) collective-permute-start(bf16[4,32,1024]{2,1,0:T(8,128)(2,1)S(1)} %slice.222), channel_id=1, source_target_pairs={{0,32},{16,48},{32,64},{48,80},{64,96},{80,112},{96,0},{112,16},{1... | collective-permute-start | bytes 786440 | tf_op jit(solution)/shard_map/ppermute | solution.py:11
  74.7 29.1 %collective-permute-start.9 = (bf16[4,32,1024]{2,1,0:T(8,128)(2,1)S(1)}, bf16[4,32,1024]{2,1,0:T(8,128)(2,1)S(1)}, u32[]{:S(2)}, u32[]{:S(2)}) collective-permute-start(bf16[4,32,1024]{2,1,0:T(8,128)(2,1)S(1)} %slice.223), channel_id=1, source_target_pairs={{0,96},{16,112},{32,0},{48,16},{64,32},{80,48},{96,64},{112,80},{1... | collective-permute-start | bytes 786440 | tf_op jit(solution)/shard_map/ppermute | solution.py:11
  88.7 2.2 %copy-start.2 = (bf16[4,1024,512]{2,1,0:T(8,128)(2,1)S(1)}, bf16[4,1024,512]{2,1,0:T(8,128)(2,1)}, u32[]{:S(2)}) copy-start(bf16[4,1024,512]{2,1,0:T(8,128)(2,1)} %get-tuple-element.21) | copy-start | bytes 12582916
  94.2 13.9 %collective-permute-start.10 = (bf16[4,64,1024]{2,1,0:T(8,128)(2,1)S(1)}, bf16[4,64,1024]{2,1,0:T(8,128)(2,1)S(1)}, u32[]{:S(2)}, u32[]{:S(2)}) collective-permute-start(bf16[4,64,1024]{2,1,0:T(8,128)(2,1)S(1)} %collective-permute-done.3), channel_id=1, source_target_pairs={{0,16},{16,0},{32,48},{48,32},{64,80},{80,64},{96,112},{112,96},{1... | collective-permute-start | bytes 1572872 | tf_op jit(solution)/shard_map/ppermute | solution.py:15
  119.9 2.2 %copy-start.1 = (bf16[4,1024,512]{2,1,0:T(8,128)(2,1)S(1)}, bf16[4,1024,512]{2,1,0:T(8,128)(2,1)}, u32[]{:S(2)}) copy-start(bf16[4,1024,512]{2,1,0:T(8,128)(2,1)} %get-tuple-element.22) | copy-start | bytes 12582916
  128.6 3.2 %copy-start.3 = (f32[1024,1024]{1,0:T(8,128)S(1)}, f32[1024,1024]{1,0:T(8,128)}, u32[]{:S(2)}) copy-start(f32[1024,1024]{1,0:T(8,128)} %fusion.45) | copy-start | bytes 12582916
  141.4 6.4 %copy-start = (bf16[1024,1024]{1,0:T(8,128)(2,1)}, bf16[1024,1024]{1,0:T(8,128)(2,1)S(1)}, u32[]{:S(2)}) copy-start(bf16[1024,1024]{1,0:T(8,128)(2,1)S(1)} %add_convert_fusion) | copy-start | bytes 6291460
  141.8 5.2 %copy-start.5 = (bf16[4608,128]{1,0:T(8,128)(2,1)}, bf16[4608,128]{1,0:T(8,128)(2,1)S(1)}, u32[]{:S(2)}) copy-start(bf16[4608,128]{1,0:T(8,128)(2,1)S(1)} %slice_dynamic-update-slice_fusion.1) | copy-start | bytes 3538948
  153.3 11.4 %copy-start.6 = (s32[128,2]{0,1:T(2,128)S(1)}, s32[128,2]{0,1:T(2,128)}, u32[]{:S(2)}) copy-start(s32[128,2]{0,1:T(2,128)} %param.7) | copy-start | bytes 3076
  153.3 42.5 %all-to-all-start.1 = ((bf16[16,2,288,128]{3,2,1,0:T(8,128)(2,1)}), bf16[16,2,288,128]{3,2,1,0:T(8,128)(2,1)S(1)}, u32[]{:S(2)}, u32[]{:S(2)}) async-start(bf16[16,2,288,128]{3,2,1,0:T(8,128)(2,1)} %copy.14), calls=%async_computation.1 | async-start | bytes 4718592 | tf_op jit(solution)/shard_map/all_to_all | solution.py:109

commit v8 on v4

--- a/solution.py
+++ b/solution.py
@@ -85,12 +85,12 @@
     upper = jnp.concatenate(upper, axis=0) * weight
     upper_t = jnp.concatenate(upper_t, axis=0)
     share = upper.shape[0] // n_m
-    slices = jnp.stack(
+    slices = jnp.concatenate(
         [upper.reshape(n_m, share, width), upper_t.reshape(n_m, share, width)], axis=1
     )
     received = lax.all_to_all(slices, "mom", 0, 0)
-    own_rows = received[:, 0].reshape(n_m, share * width)
-    own_cols = received[:, 1].reshape(n_m, share * width)
+    own_rows = received[:, :share].reshape(n_m, share * width)
+    own_cols = received[:, share:].reshape(n_m, share * width)
     partial = lax.dot_general(
         own_rows, own_cols, (((1,), (1,)), ((), ())), preferred_element_type=jnp.float32
     )

time: 204 us -> 204 us (level)
    concatenate x0 -> x1, other arithmetic: none -> 2.88 us  [body(): jnp.concatenate([upper.reshape(n_m, share, width), upper_t.reshape(n_m, s...]
where the time goes in v8:
time: 204 us; the launch traced here: 203 us
  waiting for transfers between devices  93.7 us (46%)
  matrix products  44 us (22%)
  starting transfers between devices  35.7 us (18%)
  local copies, waits for them, and re-layouts  17.6 us (9%)
  other arithmetic  11.4 us (6%)
    ppermute x8, waiting for transfers between devices, shifted(): return lax.ppermute(block, 'tsink', pairs)  31.4 us
    all_to_all x1, waiting for transfers between devices, body(): received = lax.all_to_all(slices, 'mom', 0, 0)  31.2 us
    all_to_all x1, waiting for transfers between devices, source_pieces(): received = lax.all_to_all(pieces, 'tsink', 0, 0)  26.7 us
    dot_general x8, matrix products, body(): jnp.einsum('sik,sjk->sij', piece, propagators, preferred_element_type=jnp...  25.8 us
    dot_general x4, matrix products, body(): jnp.dot(propagators[source], halves[source], preferred_element_type=jnp.f...  17.5 us
    all_to_all x1, starting transfers between devices, body(): received = lax.all_to_all(slices, 'mom', 0, 0)  11.8 us
    ppermute x8, starting transfers between devices, shifted(): return lax.ppermute(block, 'tsink', pairs)  11.2 us
    unnamed x23, local copies, waits for them, and re-layouts  9.82 us
  transfers between devices with their start and end apart: 12, of which 6 were waited for; matrix products, arithmetic and copies ran while one was open for 16% of the time, Pallas kernels for 0%

profile of v8, /device:TPU:1, one launch (start us, length us, event | category | flops | bytes accessed | tf_op | source)
XLA Modules:
  0.0 203.5 jit_solution(7709369521497922566)
XLA Ops:
  0.6 6.2 %all-to-all-start = ((bf16[8,128,1024]{2,1,0:T(8,128)(2,1)}), bf16[8,128,1024]{2,1,0:T(8,128)(2,1)S(1)}, u32[]{:S(2)}, u32[]{:S(2)}) async-start(bf16[8,128,1024]{2,1,0:T(8,128)(2,1)} %bitcast.108), calls=%async_computation | async-start | bytes 4194304 | tf_op jit(solution)/shard_map/all_to_all | solution.py:24
  7.6 0.7 fusion.98
  8.4 0.8 fusion.97
  9.1 0.8 fusion.96
  9.9 0.9 fusion.95
  10.8 26.7 %all-to-all-done = bf16[8,128,1024]{2,1,0:T(8,128)(2,1)S(1)} async-done(((bf16[8,128,1024]{2,1,0:T(8,128)(2,1)}), bf16[8,128,1024]{2,1,0:T(8,128)(2,1)S(1)}, u32[]{:S(2)}, u32[]{:S(2)}) %all-to-all-start) | async-done | bytes 2097184 | tf_op jit(solution)/shard_map/all_to_all | solution.py:24
  38.2 2.7 %collective-permute-start.2 = (bf16[4,128,1024]{2,1,0:T(8,128)(2,1)S(1)}, bf16[4,128,1024]{2,1,0:T(8,128)(2,1)S(1)}, u32[]{:S(2)}, u32[]{:S(2)}) collective-permute-start(bf16[4,128,1024]{2,1,0:T(8,128)(2,1)S(1)} %gather_fusion), channel_id=1, source_target_pairs={{0,96},{16,112},{32,0},{48,16},{64,32},{80,48},{96,64},{112,80},{1... | collective-permute-start | bytes 3145736 | tf_op jit(solution)/shard_map/ppermute | solution.py:11
  40.8 0.9 fusion.94
  41.7 0.8 fusion.93
  42.5 1.1 broadcast_in_dim.108
  43.6 2.3 %copy-done = bf16[1,4,1024,1024]{3,2,1,0:T(8,128)(2,1)S(1)} copy-done((bf16[1,4,1024,1024]{3,2,1,0:T(8,128)(2,1)S(1)}, bf16[1,4,1024,1024]{3,2,1,0:T(8,128)(2,1)}, u32[]{:S(2)}) %copy-start) | copy-done | bytes 8388632
  45.9 2.9 %fusion.73 = bf16[4,1024,1024]{2,1,0:T(8,128)(2,1)S(1)} fusion(bf16[4,1024,1024]{2,1,0:T(8,128)(2,1)S(1)} %broadcast_in_dim.108, s32[]{:T(128)S(6)} %select_n.121, bf16[4,128,1024]{2,1,0:T(8,128)(2,1)S(1)} %gather_fusion, bf16[1,4,1024,1024]{3,2,1,0:T(8,128)(2,1)S(1)} %copy-done), kind=kOutput, calls=%fused_computation.51 | convolution fusion | flops 1074266112 | bytes 10485764 | tf_op jit(solution)/shard_map/sik,sjk->sij/dot_general | solution.py:60
  48.8 13.7 %collective-permute-done.1 = bf16[4,128,1024]{2,1,0:T(8,128)(2,1)S(1)} collective-permute-done((bf16[4,128,1024]{2,1,0:T(8,128)(2,1)S(1)}, bf16[4,128,1024]{2,1,0:T(8,128)(2,1)S(1)}, u32[]{:S(2)}, u32[]{:S(2)}) %collective-permute-start.1) | collective-permute-done | bytes 1048608 | tf_op jit(solution)/shard_map/ppermute | solution.py:11
  62.7 2.7 %collective-permute-start.4 = (bf16[4,64,1024]{2,1,0:T(8,128)(2,1)S(1)}, bf16[4,64,1024]{2,1,0:T(8,128)(2,1)}, u32[]{:S(2)}, u32[]{:S(2)}) collective-permute-start(bf16[4,64,1024]{2,1,0:T(8,128)(2,1)S(1)} %slice.137), channel_id=1, source_target_pairs={{0,96},{16,112},{32,0},{48,16},{64,32},{80,48},{96,64},{112,80},{1... | collective-permute-start | bytes 1572872 | tf_op jit(solution)/shard_map/ppermute | solution.py:11
  65.4 2.7 %collective-permute-start.6 = (bf16[4,128,1024]{2,1,0:T(8,128)(2,1)}, bf16[4,128,1024]{2,1,0:T(8,128)(2,1)S(1)}, u32[]{:S(2)}, u32[]{:S(2)}) collective-permute-start(bf16[4,128,1024]{2,1,0:T(8,128)(2,1)} %collective-permute-done), channel_id=1, source_target_pairs={{0,96},{16,112},{32,0},{48,16},{64,32},{80,48},{96,64},{112,80},{1... | collective-permute-start | bytes 3145736 | tf_op jit(solution)/shard_map/ppermute | solution.py:11
  68.1 4.2 %fusion.70 = bf16[4,1024,1024]{2,1,0:T(8,128)(2,1)S(1)} fusion(bf16[4,1024,1024]{2,1,0:T(8,128)(2,1)S(1)} %fusion.73, s32[]{:T(128)S(6)} %select_n.122, bf16[4,128,1024]{2,1,0:T(8,128)(2,1)} %collective-permute-done, bf16[1,4,1024,1024]{3,2,1,0:T(8,128)(2,1)S(1)} %copy-done), kind=kOutput, calls=%fused_computation.50 | convolution fusion | flops 1074266112 | bytes 10485764 | tf_op jit(solution)/shard_map/sik,sjk->sij/dot_general | solution.py:60
  72.3 3.0 %fusion.67 = bf16[4,1024,1024]{2,1,0:T(8,128)(2,1)S(1)} fusion(bf16[4,1024,1024]{2,1,0:T(8,128)(2,1)S(1)} %fusion.70, s32[]{:T(128)S(6)} %select_n.124, bf16[4,128,1024]{2,1,0:T(8,128)(2,1)S(1)} %collective-permute-done.1, bf16[1,4,1024,1024]{3,2,1,0:T(8,128)(2,1)S(1)} %copy-done), kind=kOutput, calls=%fused_computation.49 | convolution fusion | flops 1074266112 | bytes 10485764 | tf_op jit(solution)/shard_map/sik,sjk->sij/dot_general | solution.py:60
  75.3 3.0 %fusion.64 = bf16[4,1024,1024]{2,1,0:T(8,128)(2,1)S(1)} fusion(bf16[4,1024,1024]{2,1,0:T(8,128)(2,1)S(1)} %fusion.67, s32[]{:T(128)S(6)} %select_n.126, bf16[4,128,1024]{2,1,0:T(8,128)(2,1)S(1)} %collective-permute-done.2, bf16[1,4,1024,1024]{3,2,1,0:T(8,128)(2,1)S(1)} %copy-done), kind=kOutput, calls=%fused_computation.48 | convolution fusion | flops 1074266112 | bytes 10485764 | tf_op jit(solution)/shard_map/sik,sjk->sij/dot_general | solution.py:60
  78.3 4.0 %fusion.61 = bf16[4,1024,1024]{2,1,0:T(8,128)(2,1)S(1)} fusion(bf16[4,1024,1024]{2,1,0:T(8,128)(2,1)S(1)} %fusion.64, s32[]{:T(128)S(6)} %select_n.128, bf16[1,4,1024,1024]{3,2,1,0:T(8,128)(2,1)S(1)} %copy-done, bf16[4,64,1024]{2,1,0:T(8,128)(2,1)} %collective-permute-done.4, bf16[4,64,1024]{2,1,0:T(8,128)(2,1)S(1)} %collective-permute-done.3), kind=kOutput, calls=%fused_computation.47 | convolution fusion | flops 1076363264 | bytes 10485764 | tf_op jit(solution)/shard_map/sik,sjk->sij/dot_general | solution.py:60
  82.3 15.1 %collective-permute-done.5 = bf16[4,128,1024]{2,1,0:T(8,128)(2,1)S(1)} collective-permute-done((bf16[4,128,1024]{2,1,0:T(8,128)(2,1)}, bf16[4,128,1024]{2,1,0:T(8,128)(2,1)S(1)}, u32[]{:S(2)}, u32[]{:S(2)}) %collective-permute-start.5) | collective-permute-done | bytes 1048608 | tf_op jit(solution)/shard_map/ppermute | solution.py:11
  97.5 2.9 %collective-permute-start.8 = (bf16[4,64,1024]{2,1,0:T(8,128)(2,1)S(1)}, bf16[4,64,1024]{2,1,0:T(8,128)(2,1)S(1)}, u32[]{:S(2)}, u32[]{:S(2)}) collective-permute-start(bf16[4,64,1024]{2,1,0:T(8,128)(2,1)S(1)} %slice.139), channel_id=1, source_target_pairs={{0,96},{16,112},{32,0},{48,16},{64,32},{80,48},{96,64},{112,80},{1... | collective-permute-start | bytes 1572872 | tf_op jit(solution)/shard_map/ppermute | solution.py:11
  100.5 2.9 %fusion.58 = bf16[4,1024,1024]{2,1,0:T(8,128)(2,1)S(1)} fusion(bf16[4,1024,1024]{2,1,0:T(8,128)(2,1)S(1)} %fusion.61, s32[]{:T(128)S(6)} %select_n.129, bf16[4,128,1024]{2,1,0:T(8,128)(2,1)S(1)} %collective-permute-done.5, bf16[1,4,1024,1024]{3,2,1,0:T(8,128)(2,1)S(1)} %copy-done), kind=kOutput, calls=%fused_computation.46 | convolution fusion | flops 1074266112 | bytes 10485764 | tf_op jit(solution)/shard_map/sik,sjk->sij/dot_general | solution.py:60
  103.4 2.9 %fusion.55 = bf16[4,1024,1024]{2,1,0:T(8,128)(2,1)S(1)} fusion(bf16[4,1024,1024]{2,1,0:T(8,128)(2,1)S(1)} %fusion.58, s32[]{:T(128)S(6)} %select_n.130, bf16[4,128,1024]{2,1,0:T(8,128)(2,1)S(1)} %collective-permute-done.6, bf16[1,4,1024,1024]{3,2,1,0:T(8,128)(2,1)S(1)} %copy-done), kind=kOutput, calls=%fused_computation.45 | convolution fusion | flops 1074266112 | bytes 10485764 | tf_op jit(solution)/shard_map/sik,sjk->sij/dot_general | solution.py:60
  106.3 2.6 %collective-permute-done.7 = bf16[4,64,1024]{2,1,0:T(8,128)(2,1)S(1)} collective-permute-done((bf16[4,64,1024]{2,1,0:T(8,128)(2,1)S(1)}, bf16[4,64,1024]{2,1,0:T(8,128)(2,1)S(1)}, u32[]{:S(2)}, u32[]{:S(2)}) %collective-permute-start.7) | collective-permute-done | bytes 524320 | tf_op jit(solution)/shard_map/ppermute | solution.py:11
  108.9 2.9 %fusion.52 = bf16[4,1024,1024]{2,1,0:T(8,128)(2,1)S(1)} fusion(bf16[4,1024,1024]{2,1,0:T(8,128)(2,1)S(1)} %fusion.55, s32[]{:T(128)S(6)} %select_n.131, bf16[1,4,1024,1024]{3,2,1,0:T(8,128)(2,1)S(1)} %copy-done, bf16[4,64,1024]{2,1,0:T(8,128)(2,1)S(1)} %collective-permute-done.8, bf16[4,64,1024]{2,1,0:T(8,128)(2,1)S(1)} %collective-permute-done.7), kind=kOutput, calls=%fused_computation.44 | convolution fusion | flops 1076363264 | bytes 10485764 | tf_op jit(solution)/shard_map/sik,sjk->sij/dot_general | solution.py:60
  111.8 2.4 %fusion.16 = f32[1024,1024]{1,0:T(8,128)S(1)} fusion(bf16[4,1024,1024]{2,1,0:T(8,128)(2,1)S(1)} %fusion.52, bf16[1,4,1024,1024]{3,2,1,0:T(8,128)(2,1)S(1)} %copy-done), kind=kOutput, calls=%fused_computation.21 | convolution fusion | flops 2147483648 | bytes 8388608 | tf_op jit(solution)/shard_map/dot_general | solution.py:66
  114.2 4.3 %fusion.17 = f32[1024,1024]{1,0:T(8,128)} fusion(bf16[4,1024,1024]{2,1,0:T(8,128)(2,1)S(1)} %fusion.52, bf16[1,4,1024,1024]{3,2,1,0:T(8,128)(2,1)S(1)} %copy-done), kind=kOutput, calls=%fused_computation.23 | convolution fusion | flops 2147483648 | bytes 8388608 | tf_op jit(solution)/shard_map/dot_general | solution.py:66
  118.5 4.7 %fusion.18 = f32[1024,1024]{1,0:T(8,128)} fusion(bf16[4,1024,1024]{2,1,0:T(8,128)(2,1)S(1)} %fusion.52, bf16[1,4,1024,1024]{3,2,1,0:T(8,128)(2,1)S(1)} %copy-done), kind=kOutput, calls=%fused_computation.25 | convolution fusion | flops 2147483648 | bytes 8388608 | tf_op jit(solution)/shard_map/dot_general | solution.py:66
  123.2 6.1 %add_convert_fusion = bf16[1024,1024]{1,0:T(8,128)(2,1)S(1)} fusion(f32[1024,1024]{1,0:T(8,128)S(1)} %fusion.16, f32[1024,1024]{1,0:T(8,128)} %fusion.17, f32[1024,1024]{1,0:T(8,128)} %fusion.18, bf16[1,4,1024,1024]{3,2,1,0:T(8,128)(2,1)S(1)} %copy-done, bf16[4,1024,1024]{2,1,0:T(8,128)(2,1)S(1)} %fusion.52), kind=kOutput, calls=%fused_computation.18 | convolution fusion | flops 2151677952 | bytes 18874368 | tf_op jit(solution)/shard_map/dot_general | solution.py:66
  130.1 0.9 fusion.92
  131.0 1.5 mul.39
  132.5 1.4 copy.15
  134.6 0.7 slice_dynamic-update-slice_fusion.10
  135.3 0.7 slice_dynamic-update-slice_fusion.8
  136.0 0.7 slice_dynamic-update-slice_fusion.6
  136.7 0.7 slice_dynamic-update-slice_fusion.4
  137.4 0.7 slice_dynamic-update-slice_fusion.2
  138.2 0.8 slice_dynamic-update-slice_fusion
  138.9 2.9 %pad_maximum_fusion = bf16[16,576,128]{2,1,0:T(8,128)(2,1)} fusion(bf16[16,288,128]{2,1,0:T(8,128)(2,1)} %bitcast.109, bf16[16,288,128]{2,1,0:T(8,128)(2,1)S(1)} %bitcast.107), kind=kLoop, calls=%fused_computation.19 | loop fusion | flops 4718592 | bytes 4718592 | tf_op jit(solution)/shard_map/concatenate | solution.py:88
  141.8 11.8 %all-to-all-start.1 = ((bf16[16,576,128]{2,1,0:T(8,128)(2,1)}), bf16[16,576,128]{2,1,0:T(8,128)(2,1)}, u32[]{:S(2)}, u32[]{:S(2)}) async-start(bf16[16,576,128]{2,1,0:T(8,128)(2,1)} %pad_maximum_fusion), calls=%async_computation.1 | async-start | bytes 4718592 | tf_op jit(solution)/shard_map/all_to_all | solution.py:91
  153.6 31.2 %all-to-all-done.1 = bf16[16,576,128]{2,1,0:T(8,128)(2,1)} async-done(((bf16[16,576,128]{2,1,0:T(8,128)(2,1)}), bf16[16,576,128]{2,1,0:T(8,128)(2,1)}, u32[]{:S(2)}, u32[]{:S(2)}) %all-to-all-start.1) | async-done | bytes 2359328 | tf_op jit(solution)/shard_map/all_to_all | solution.py:91
  184.8 1.8 fusion.107
  186.6 0.7 fusion.81
  187.4 1.3 gather_fusion.1
  188.7 0.7 all_to_all.14
  189.4 6.5 %all-to-all-start.2 = ((f32[16,1,8]{2,1,0:T(1,128)}), f32[16,1,8]{2,1,0:T(1,128)S(1)}, u32[]{:S(2)}, u32[]{:S(2)}) async-start(f32[16,1,8]{2,1,0:T(1,128)} %bitcast.17), calls=%async_computation.2 | async-start | bytes 16384 | tf_op jit(solution)/shard_map/all_to_all | solution.py:99
  195.9 2.6 %copy.20 = bf16[1,1,1024,1024]{3,2,1,0:T(8,128)(2,1)} copy(bf16[1,1,1024,1024]{2,3,1,0:T(8,128)(2,1)S(1)} %bitcast.106) | data formatting | bytes 4194304
  198.5 4.5 %all-to-all-done.2 = f32[16,1,8]{2,1,0:T(1,128)S(1)} async-done(((f32[16,1,8]{2,1,0:T(1,128)}), f32[16,1,8]{2,1,0:T(1,128)S(1)}, u32[]{:S(2)}, u32[]{:S(2)}) %all-to-all-start.2) | async-done | bytes 544 | tf_op jit(solution)/shard_map/all_to_all | solution.py:99
  (47 shorter events, 3.7 us)
Async XLA Ops:
  0.6 6.3 %copy-start.3 = (s32[4]{0:T(128)S(1)}, s32[4]{0:T(128)}, u32[]{:S(2)}) copy-start(s32[4]{0:T(128)} %param.6) | copy-start | bytes 52
  0.6 36.8 %all-to-all-start = ((bf16[8,128,1024]{2,1,0:T(8,128)(2,1)}), bf16[8,128,1024]{2,1,0:T(8,128)(2,1)S(1)}, u32[]{:S(2)}, u32[]{:S(2)}) async-start(bf16[8,128,1024]{2,1,0:T(8,128)(2,1)} %bitcast.108), calls=%async_computation | async-start | bytes 4194304 | tf_op jit(solution)/shard_map/all_to_all | solution.py:24
  38.1 24.4 %collective-permute-start.1 = (bf16[4,128,1024]{2,1,0:T(8,128)(2,1)S(1)}, bf16[4,128,1024]{2,1,0:T(8,128)(2,1)S(1)}, u32[]{:S(2)}, u32[]{:S(2)}) collective-permute-start(bf16[4,128,1024]{2,1,0:T(8,128)(2,1)S(1)} %gather_fusion), channel_id=1, source_target_pairs={{0,32},{16,48},{32,64},{48,80},{64,96},{80,112},{96,0},{112,16},{1... | collective-permute-start | bytes 3145736 | tf_op jit(solution)/shard_map/ppermute | solution.py:11
  38.2 24.5 %collective-permute-start.2 = (bf16[4,128,1024]{2,1,0:T(8,128)(2,1)S(1)}, bf16[4,128,1024]{2,1,0:T(8,128)(2,1)S(1)}, u32[]{:S(2)}, u32[]{:S(2)}) collective-permute-start(bf16[4,128,1024]{2,1,0:T(8,128)(2,1)S(1)} %gather_fusion), channel_id=1, source_target_pairs={{0,96},{16,112},{32,0},{48,16},{64,32},{80,48},{96,64},{112,80},{1... | collective-permute-start | bytes 3145736 | tf_op jit(solution)/shard_map/ppermute | solution.py:11
  40.8 24.6 %collective-permute-start = (bf16[4,128,1024]{2,1,0:T(8,128)(2,1)S(1)}, bf16[4,128,1024]{2,1,0:T(8,128)(2,1)}, u32[]{:S(2)}, u32[]{:S(2)}) collective-permute-start(bf16[4,128,1024]{2,1,0:T(8,128)(2,1)S(1)} %gather_fusion), channel_id=1, source_target_pairs={{0,16},{16,0},{32,48},{48,32},{64,80},{80,64},{96,112},{112,96},{1... | collective-permute-start | bytes 3145736 | tf_op jit(solution)/shard_map/ppermute | solution.py:15
  42.5 3.4 %copy-start = (bf16[1,4,1024,1024]{3,2,1,0:T(8,128)(2,1)S(1)}, bf16[1,4,1024,1024]{3,2,1,0:T(8,128)(2,1)}, u32[]{:S(2)}) copy-start(bf16[1,4,1024,1024]{3,2,1,0:T(8,128)(2,1)} %param.4) | copy-start | bytes 25165828
  62.5 15.7 %collective-permute-start.3 = (bf16[4,64,1024]{2,1,0:T(8,128)(2,1)S(1)}, bf16[4,64,1024]{2,1,0:T(8,128)(2,1)S(1)}, u32[]{:S(2)}, u32[]{:S(2)}) collective-permute-start(bf16[4,64,1024]{2,1,0:T(8,128)(2,1)S(1)} %slice.136), channel_id=1, source_target_pairs={{0,32},{16,48},{32,64},{48,80},{64,96},{80,112},{96,0},{112,16},{1... | collective-permute-start | bytes 1572872 | tf_op jit(solution)/shard_map/ppermute | solution.py:11
  62.7 15.6 %collective-permute-start.4 = (bf16[4,64,1024]{2,1,0:T(8,128)(2,1)S(1)}, bf16[4,64,1024]{2,1,0:T(8,128)(2,1)}, u32[]{:S(2)}, u32[]{:S(2)}) collective-permute-start(bf16[4,64,1024]{2,1,0:T(8,128)(2,1)S(1)} %slice.137), channel_id=1, source_target_pairs={{0,96},{16,112},{32,0},{48,16},{64,32},{80,48},{96,64},{112,80},{1... | collective-permute-start | bytes 1572872 | tf_op jit(solution)/shard_map/ppermute | solution.py:11
  65.4 31.9 %collective-permute-start.5 = (bf16[4,128,1024]{2,1,0:T(8,128)(2,1)}, bf16[4,128,1024]{2,1,0:T(8,128)(2,1)S(1)}, u32[]{:S(2)}, u32[]{:S(2)}) collective-permute-start(bf16[4,128,1024]{2,1,0:T(8,128)(2,1)} %collective-permute-done), channel_id=1, source_target_pairs={{0,32},{16,48},{32,64},{48,80},{64,96},{80,112},{96,0},{112,16},{1... | collective-permute-start | bytes 3145736 | tf_op jit(solution)/shard_map/ppermute | solution.py:11
  65.4 32.1 %collective-permute-start.6 = (bf16[4,128,1024]{2,1,0:T(8,128)(2,1)}, bf16[4,128,1024]{2,1,0:T(8,128)(2,1)S(1)}, u32[]{:S(2)}, u32[]{:S(2)}) collective-permute-start(bf16[4,128,1024]{2,1,0:T(8,128)(2,1)} %collective-permute-done), channel_id=1, source_target_pairs={{0,96},{16,112},{32,0},{48,16},{64,32},{80,48},{96,64},{112,80},{1... | collective-permute-start | bytes 3145736 | tf_op jit(solution)/shard_map/ppermute | solution.py:11
  97.4 11.5 %collective-permute-start.7 = (bf16[4,64,1024]{2,1,0:T(8,128)(2,1)S(1)}, bf16[4,64,1024]{2,1,0:T(8,128)(2,1)S(1)}, u32[]{:S(2)}, u32[]{:S(2)}) collective-permute-start(bf16[4,64,1024]{2,1,0:T(8,128)(2,1)S(1)} %slice.138), channel_id=1, source_target_pairs={{0,32},{16,48},{32,64},{48,80},{64,96},{80,112},{96,0},{112,16},{1... | collective-permute-start | bytes 1572872 | tf_op jit(solution)/shard_map/ppermute | solution.py:11
  97.5 11.3 %collective-permute-start.8 = (bf16[4,64,1024]{2,1,0:T(8,128)(2,1)S(1)}, bf16[4,64,1024]{2,1,0:T(8,128)(2,1)S(1)}, u32[]{:S(2)}, u32[]{:S(2)}) collective-permute-start(bf16[4,64,1024]{2,1,0:T(8,128)(2,1)S(1)} %slice.139), channel_id=1, source_target_pairs={{0,96},{16,112},{32,0},{48,16},{64,32},{80,48},{96,64},{112,80},{1... | collective-permute-start | bytes 1572872 | tf_op jit(solution)/shard_map/ppermute | solution.py:11
  134.0 5.0 %copy-start.1 = (bf16[4608,128]{1,0:T(8,128)(2,1)S(1)}, bf16[4608,128]{1,0:T(8,128)(2,1)}, u32[]{:S(2)}) copy-start(bf16[4608,128]{1,0:T(8,128)(2,1)} %copy.15) | copy-start | bytes 3538948
  141.8 11.8 %copy-start.2 = (s32[128,2]{0,1:T(2,128)S(1)}, s32[128,2]{0,1:T(2,128)}, u32[]{:S(2)}) copy-start(s32[128,2]{0,1:T(2,128)} %param.7) | copy-start | bytes 3076
  141.8 43.0 %all-to-all-start.1 = ((bf16[16,576,128]{2,1,0:T(8,128)(2,1)}), bf16[16,576,128]{2,1,0:T(8,128)(2,1)}, u32[]{:S(2)}, u32[]{:S(2)}) async-start(bf16[16,576,128]{2,1,0:T(8,128)(2,1)} %pad_maximum_fusion), calls=%async_computation.1 | async-start | bytes 4718592 | tf_op jit(solution)/shard_map/all_to_all | solution.py:91
  189.4 13.6 %all-to-all-start.2 = ((f32[16,1,8]{2,1,0:T(1,128)}), f32[16,1,8]{2,1,0:T(1,128)S(1)}, u32[]{:S(2)}, u32[]{:S(2)}) async-start(f32[16,1,8]{2,1,0:T(1,128)} %bitcast.17), calls=%async_computation.2 | async-start | bytes 16384 | tf_op jit(solution)/shard_map/all_to_all | solution.py:99

commit v9 on v3

--- a/solution.py
+++ b/solution.py
@@ -1,3 +1,4 @@
+import numpy as np
 import jax
 import jax.numpy as jnp
 from jax import lax
@@ -69,17 +70,30 @@
     meson = summed.astype(jnp.bfloat16)
 
     n_m = lax.axis_size("mom")
-    rows = block_order // n_m
-    slices = jnp.stack(
-        [meson.reshape(n_m, rows, block_order), meson.T.reshape(n_m, rows, block_order)],
-        axis=1,
+    width = 128
+    n_b = block_order // width
+    grid = meson.reshape(n_b, width, n_b, width).transpose(0, 2, 1, 3).reshape(n_b * n_b, width, width)
+    pairs = [(row, col) for col in range(n_b) for row in range(col + 1)]
+    upper = grid[np.array([row * n_b + col for row, col in pairs])]
+    upper_t = jnp.swapaxes(grid[np.array([col * n_b + row for row, col in pairs])], 1, 2)
+    row_index = lax.broadcasted_iota(jnp.int32, (width, width), 0)
+    col_index = lax.broadcasted_iota(jnp.int32, (width, width), 1)
+    triangle = jnp.where(row_index < col_index, 1.0, jnp.where(row_index == col_index, 0.5, 0.0))
+    on_diagonal = np.array([row == col for row, col in pairs])[:, None, None]
+    weight = jnp.where(on_diagonal, triangle[None], 1.0).astype(jnp.bfloat16)
+    upper = (upper * weight).reshape(-1, width)
+    upper_t = upper_t.reshape(-1, width)
+    share = upper.shape[0] // n_m
+    slices = jnp.concatenate(
+        [upper.reshape(n_m, share, width), upper_t.reshape(n_m, share, width)], axis=1
     )
     received = lax.all_to_all(slices, "mom", 0, 0)
-    own_rows = received[:, 0].reshape(n_m, rows * block_order)
-    own_cols = received[:, 1].reshape(n_m, rows * block_order)
+    own_rows = received[:, :share].reshape(n_m, share * width)
+    own_cols = received[:, share:].reshape(n_m, share * width)
     partial = lax.dot_general(
         own_rows, own_cols, (((1,), (1,)), ((), ())), preferred_element_type=jnp.float32
     )
+    partial = partial + partial.T
     per_diagram = partial[diagrams[:, 0], diagrams[:, 1]]
     spread = lax.all_to_all(per_diagram.reshape(n_m, -1), "mom", 0, 0)
     correlators = (jnp.sum(spread, axis=0) / block_order)[:, None]

time: 236 us -> 202 us (0.86); the launches traced: 232 us -> 202 us
  waiting for transfers between devices: 122 us -> 98.7 us
  starting transfers between devices: 42.6 us -> 35.7 us
  matrix products: 46.9 us -> 44.3 us
  local copies, waits for them, and re-layouts: 16.4 us -> 18.8 us
    all_to_all x1, waiting for transfers between devices: 53.1 us -> 31.1 us  [body(): received = lax.all_to_all(slices, 'mom', 0, 0)]
    all_to_all x1, starting transfers between devices: 13.3 us -> 6.53 us  [body(): spread = lax.all_to_all(per_diagram.reshape(n_m, -1), 'mom', 0, 0)]
    dot_general x1, matrix products: 4.43 us -> 0.73 us  [body(): lax.dot_general(own_rows, own_cols, (((1,), (1,)), ((), ())), preferred_e...]
    reshape x0 -> x1, local copies, waits for them, and re-layouts: none -> 3.28 us  [body(): meson.reshape(n_b, width, n_b, width).transpose(0, 2, 1, 3)]
    gather x0 -> x2, local copies, waits for them, and re-layouts: none -> 2.58 us  [the longest x1 1.8 us: body(): upper = grid[np.array([row * n_b + col for row, col in pairs])]]
    slice x1, local copies, waits for them, and re-layouts: 2.72 us -> 0.15 us  [body(): own_rows = received[:, :share].reshape(n_m, share * width)]
    convert_element_type x1 -> x0, local copies, waits for them, and re-layouts: 2.56 us -> none  [body(): meson = summed.astype(jnp.bfloat16)]
    another operation x1 -> x0, local copies, waits for them, and re-layouts: 2.42 us -> none  [body(): jnp.stack([meson.reshape(n_m, rows, block_order), meson.T.reshape(n_m, ro...]
  transfers between devices with their start and end apart: 12 -> 12, of which waited for: 6 -> 6; matrix products, arithmetic and copies ran while one was open for 11% -> 13% of each run, Pallas kernels for 0% -> 0%
where the time goes in v9:
time: 202 us
  waiting for transfers between devices  98.7 us (49%)
  matrix products  44.3 us (22%)
  starting transfers between devices  35.7 us (18%)
  local copies, waits for them, and re-layouts  18.8 us (9%)
  other arithmetic  3.17 us (2%)
    ppermute x8, waiting for transfers between devices, shifted(): return lax.ppermute(block, 'tsink', pairs)  32.5 us
    all_to_all x1, waiting for transfers between devices, body(): received = lax.all_to_all(slices, 'mom', 0, 0)  31.1 us
    all_to_all x1, waiting for transfers between devices, source_pieces(): received = lax.all_to_all(pieces, 'tsink', 0, 0)  30.6 us
    dot_general x8, matrix products, body(): jnp.einsum('sik,sjk->sij', piece, propagators, preferred_element_type=jnp...  26 us
    dot_general x4, matrix products, body(): jnp.dot(propagators[source], halves[source], preferred_element_type=jnp.f...  17.6 us
    all_to_all x1, starting transfers between devices, body(): received = lax.all_to_all(slices, 'mom', 0, 0)  11.6 us
    ppermute x8, starting transfers between devices, shifted(): return lax.ppermute(block, 'tsink', pairs)  11.2 us
    unnamed x22, local copies, waits for them, and re-layouts  7.04 us
  transfers between devices with their start and end apart: 12, of which 6 were waited for; matrix products, arithmetic and copies ran while one was open for 13% of the time, Pallas kernels for 0%

profile of v9, /device:TPU:1, one launch (start us, length us, event | category | flops | bytes accessed | tf_op | source)
XLA Modules:
  0.0 201.7 jit_solution(5893398792710980666)
XLA Ops:
  0.7 6.3 %all-to-all-start = ((bf16[8,128,1024]{2,1,0:T(8,128)(2,1)}), bf16[8,128,1024]{2,1,0:T(8,128)(2,1)S(1)}, u32[]{:S(2)}, u32[]{:S(2)}) async-start(bf16[8,128,1024]{2,1,0:T(8,128)(2,1)} %bitcast.117), calls=%async_computation | async-start | bytes 4194304 | tf_op jit(solution)/shard_map/all_to_all | solution.py:25
  7.0 30.6 %all-to-all-done = bf16[8,128,1024]{2,1,0:T(8,128)(2,1)S(1)} async-done(((bf16[8,128,1024]{2,1,0:T(8,128)(2,1)}), bf16[8,128,1024]{2,1,0:T(8,128)(2,1)S(1)}, u32[]{:S(2)}, u32[]{:S(2)}) %all-to-all-start) | async-done | bytes 2097184 | tf_op jit(solution)/shard_map/all_to_all | solution.py:25
  37.6 0.6 gather_fusion
  38.2 0.1 collective-permute-start.1
  38.3 2.7 %collective-permute-start.2 = (bf16[4,128,1024]{2,1,0:T(8,128)(2,1)S(1)}, bf16[4,128,1024]{2,1,0:T(8,128)(2,1)S(1)}, u32[]{:S(2)}, u32[]{:S(2)}) collective-permute-start(bf16[4,128,1024]{2,1,0:T(8,128)(2,1)S(1)} %gather_fusion), channel_id=1, source_target_pairs={{0,96},{16,112},{32,0},{48,16},{64,32},{80,48},{96,64},{112,80},{1... | collective-permute-start | bytes 3145736 | tf_op jit(solution)/shard_map/ppermute | solution.py:12
  41.0 0.1 broadcast_in_dim.64
  41.1 0.1 broadcast_in_dim.65
  41.3 1.1 broadcast_in_dim.59
  42.4 2.3 %copy-done = bf16[1,4,1024,1024]{3,2,1,0:T(8,128)(2,1)S(1)} copy-done((bf16[1,4,1024,1024]{3,2,1,0:T(8,128)(2,1)S(1)}, bf16[1,4,1024,1024]{3,2,1,0:T(8,128)(2,1)}, u32[]{:S(2)}) %copy-start) | copy-done | bytes 8388632
  44.7 3.0 %fusion.73 = bf16[4,1024,1024]{2,1,0:T(8,128)(2,1)S(1)} fusion(bf16[4,1024,1024]{2,1,0:T(8,128)(2,1)S(1)} %broadcast_in_dim.59, s32[]{:T(128)S(6)} %select_n.84, bf16[4,128,1024]{2,1,0:T(8,128)(2,1)S(1)} %gather_fusion, bf16[1,4,1024,1024]{3,2,1,0:T(8,128)(2,1)S(1)} %copy-done), kind=kOutput, calls=%fused_computation.54 | convolution fusion | flops 1074266112 | bytes 10485764 | tf_op jit(solution)/shard_map/sik,sjk->sij/dot_general | solution.py:61
  47.7 15.0 %collective-permute-done.1 = bf16[4,128,1024]{2,1,0:T(8,128)(2,1)S(1)} collective-permute-done((bf16[4,128,1024]{2,1,0:T(8,128)(2,1)S(1)}, bf16[4,128,1024]{2,1,0:T(8,128)(2,1)S(1)}, u32[]{:S(2)}, u32[]{:S(2)}) %collective-permute-start.1) | collective-permute-done | bytes 1048608 | tf_op jit(solution)/shard_map/ppermute | solution.py:12
  62.7 0.1 collective-permute-start.3
  62.9 2.7 %collective-permute-start.4 = (bf16[4,64,1024]{2,1,0:T(8,128)(2,1)S(1)}, bf16[4,64,1024]{2,1,0:T(8,128)(2,1)}, u32[]{:S(2)}, u32[]{:S(2)}) collective-permute-start(bf16[4,64,1024]{2,1,0:T(8,128)(2,1)S(1)} %slice.77), channel_id=1, source_target_pairs={{0,96},{16,112},{32,0},{48,16},{64,32},{80,48},{96,64},{112,80},{1... | collective-permute-start | bytes 1572872 | tf_op jit(solution)/shard_map/ppermute | solution.py:12
  65.6 2.7 %collective-permute-start.6 = (bf16[4,128,1024]{2,1,0:T(8,128)(2,1)}, bf16[4,128,1024]{2,1,0:T(8,128)(2,1)S(1)}, u32[]{:S(2)}, u32[]{:S(2)}) collective-permute-start(bf16[4,128,1024]{2,1,0:T(8,128)(2,1)} %collective-permute-done), channel_id=1, source_target_pairs={{0,96},{16,112},{32,0},{48,16},{64,32},{80,48},{96,64},{112,80},{1... | collective-permute-start | bytes 3145736 | tf_op jit(solution)/shard_map/ppermute | solution.py:12
  68.3 4.3 %fusion.70 = bf16[4,1024,1024]{2,1,0:T(8,128)(2,1)S(1)} fusion(bf16[4,1024,1024]{2,1,0:T(8,128)(2,1)S(1)} %fusion.73, s32[]{:T(128)S(6)} %select_n.85, bf16[4,128,1024]{2,1,0:T(8,128)(2,1)} %collective-permute-done, bf16[1,4,1024,1024]{3,2,1,0:T(8,128)(2,1)S(1)} %copy-done), kind=kOutput, calls=%fused_computation.53 | convolution fusion | flops 1074266112 | bytes 10485764 | tf_op jit(solution)/shard_map/sik,sjk->sij/dot_general | solution.py:61
  72.5 3.0 %fusion.67 = bf16[4,1024,1024]{2,1,0:T(8,128)(2,1)S(1)} fusion(bf16[4,1024,1024]{2,1,0:T(8,128)(2,1)S(1)} %fusion.70, s32[]{:T(128)S(6)} %select_n.87, bf16[4,128,1024]{2,1,0:T(8,128)(2,1)S(1)} %collective-permute-done.1, bf16[1,4,1024,1024]{3,2,1,0:T(8,128)(2,1)S(1)} %copy-done), kind=kOutput, calls=%fused_computation.52 | convolution fusion | flops 1074266112 | bytes 10485764 | tf_op jit(solution)/shard_map/sik,sjk->sij/dot_general | solution.py:61
  75.5 3.0 %fusion.64 = bf16[4,1024,1024]{2,1,0:T(8,128)(2,1)S(1)} fusion(bf16[4,1024,1024]{2,1,0:T(8,128)(2,1)S(1)} %fusion.67, s32[]{:T(128)S(6)} %select_n.89, bf16[4,128,1024]{2,1,0:T(8,128)(2,1)S(1)} %collective-permute-done.2, bf16[1,4,1024,1024]{3,2,1,0:T(8,128)(2,1)S(1)} %copy-done), kind=kOutput, calls=%fused_computation.51 | convolution fusion | flops 1074266112 | bytes 10485764 | tf_op jit(solution)/shard_map/sik,sjk->sij/dot_general | solution.py:61
  78.5 4.0 %fusion.61 = bf16[4,1024,1024]{2,1,0:T(8,128)(2,1)S(1)} fusion(bf16[4,1024,1024]{2,1,0:T(8,128)(2,1)S(1)} %fusion.64, s32[]{:T(128)S(6)} %select_n.91, bf16[1,4,1024,1024]{3,2,1,0:T(8,128)(2,1)S(1)} %copy-done, bf16[4,64,1024]{2,1,0:T(8,128)(2,1)} %collective-permute-done.4, bf16[4,64,1024]{2,1,0:T(8,128)(2,1)S(1)} %collective-permute-done.3), kind=kOutput, calls=%fused_computation.50 | convolution fusion | flops 1076363264 | bytes 10485764 | tf_op jit(solution)/shard_map/sik,sjk->sij/dot_general | solution.py:61
  82.6 14.9 %collective-permute-done.5 = bf16[4,128,1024]{2,1,0:T(8,128)(2,1)S(1)} collective-permute-done((bf16[4,128,1024]{2,1,0:T(8,128)(2,1)}, bf16[4,128,1024]{2,1,0:T(8,128)(2,1)S(1)}, u32[]{:S(2)}, u32[]{:S(2)}) %collective-permute-start.5) | collective-permute-done | bytes 1048608 | tf_op jit(solution)/shard_map/ppermute | solution.py:12
  97.6 0.1 collective-permute-start.7
  97.7 2.9 %collective-permute-start.8 = (bf16[4,64,1024]{2,1,0:T(8,128)(2,1)S(1)}, bf16[4,64,1024]{2,1,0:T(8,128)(2,1)S(1)}, u32[]{:S(2)}, u32[]{:S(2)}) collective-permute-start(bf16[4,64,1024]{2,1,0:T(8,128)(2,1)S(1)} %slice.79), channel_id=1, source_target_pairs={{0,96},{16,112},{32,0},{48,16},{64,32},{80,48},{96,64},{112,80},{1... | collective-permute-start | bytes 1572872 | tf_op jit(solution)/shard_map/ppermute | solution.py:12
  100.6 2.9 %fusion.58 = bf16[4,1024,1024]{2,1,0:T(8,128)(2,1)S(1)} fusion(bf16[4,1024,1024]{2,1,0:T(8,128)(2,1)S(1)} %fusion.61, s32[]{:T(128)S(6)} %select_n.92, bf16[4,128,1024]{2,1,0:T(8,128)(2,1)S(1)} %collective-permute-done.5, bf16[1,4,1024,1024]{3,2,1,0:T(8,128)(2,1)S(1)} %copy-done), kind=kOutput, calls=%fused_computation.49 | convolution fusion | flops 1074266112 | bytes 10485764 | tf_op jit(solution)/shard_map/sik,sjk->sij/dot_general | solution.py:61
  103.6 2.9 %fusion.55 = bf16[4,1024,1024]{2,1,0:T(8,128)(2,1)S(1)} fusion(bf16[4,1024,1024]{2,1,0:T(8,128)(2,1)S(1)} %fusion.58, s32[]{:T(128)S(6)} %select_n.93, bf16[4,128,1024]{2,1,0:T(8,128)(2,1)S(1)} %collective-permute-done.6, bf16[1,4,1024,1024]{3,2,1,0:T(8,128)(2,1)S(1)} %copy-done), kind=kOutput, calls=%fused_computation.48 | convolution fusion | flops 1074266112 | bytes 10485764 | tf_op jit(solution)/shard_map/sik,sjk->sij/dot_general | solution.py:61
  106.5 2.6 %collective-permute-done.7 = bf16[4,64,1024]{2,1,0:T(8,128)(2,1)S(1)} collective-permute-done((bf16[4,64,1024]{2,1,0:T(8,128)(2,1)S(1)}, bf16[4,64,1024]{2,1,0:T(8,128)(2,1)S(1)}, u32[]{:S(2)}, u32[]{:S(2)}) %collective-permute-start.7) | collective-permute-done | bytes 524320 | tf_op jit(solution)/shard_map/ppermute | solution.py:12
  109.0 2.9 %fusion.52 = bf16[4,1024,1024]{2,1,0:T(8,128)(2,1)S(1)} fusion(bf16[4,1024,1024]{2,1,0:T(8,128)(2,1)S(1)} %fusion.55, s32[]{:T(128)S(6)} %select_n.94, bf16[1,4,1024,1024]{3,2,1,0:T(8,128)(2,1)S(1)} %copy-done, bf16[4,64,1024]{2,1,0:T(8,128)(2,1)S(1)} %collective-permute-done.8, bf16[4,64,1024]{2,1,0:T(8,128)(2,1)S(1)} %collective-permute-done.7), kind=kOutput, calls=%fused_computation.47 | convolution fusion | flops 1076363264 | bytes 10485764 | tf_op jit(solution)/shard_map/sik,sjk->sij/dot_general | solution.py:61
  112.0 2.4 %fusion.16 = f32[1024,1024]{1,0:T(8,128)S(1)} fusion(bf16[4,1024,1024]{2,1,0:T(8,128)(2,1)S(1)} %fusion.52, bf16[1,4,1024,1024]{3,2,1,0:T(8,128)(2,1)S(1)} %copy-done), kind=kOutput, calls=%fused_computation.24 | convolution fusion | flops 2147483648 | bytes 8388608 | tf_op jit(solution)/shard_map/dot_general | solution.py:67
  114.4 4.3 %fusion.17 = f32[1024,1024]{1,0:T(8,128)} fusion(bf16[4,1024,1024]{2,1,0:T(8,128)(2,1)S(1)} %fusion.52, bf16[1,4,1024,1024]{3,2,1,0:T(8,128)(2,1)S(1)} %copy-done), kind=kOutput, calls=%fused_computation.26 | convolution fusion | flops 2147483648 | bytes 8388608 | tf_op jit(solution)/shard_map/dot_general | solution.py:67
  118.7 4.7 %fusion.18 = f32[1024,1024]{1,0:T(8,128)} fusion(bf16[4,1024,1024]{2,1,0:T(8,128)(2,1)S(1)} %fusion.52, bf16[1,4,1024,1024]{3,2,1,0:T(8,128)(2,1)S(1)} %copy-done), kind=kOutput, calls=%fused_computation.28 | convolution fusion | flops 2147483648 | bytes 8388608 | tf_op jit(solution)/shard_map/dot_general | solution.py:67
  123.4 6.2 %add_convert_fusion = bf16[1024,1024]{1,0:T(8,128)(2,1)S(1)} fusion(f32[1024,1024]{1,0:T(8,128)S(1)} %fusion.16, f32[1024,1024]{1,0:T(8,128)} %fusion.17, f32[1024,1024]{1,0:T(8,128)} %fusion.18, bf16[1,4,1024,1024]{3,2,1,0:T(8,128)(2,1)S(1)} %copy-done, bf16[4,1024,1024]{2,1,0:T(8,128)(2,1)S(1)} %fusion.52), kind=kOutput, calls=%fused_computation.20 | convolution fusion | flops 2151677952 | bytes 18874368 | tf_op jit(solution)/shard_map/dot_general | solution.py:67
  129.6 2.0 copy.30
  131.6 3.3 %copy.21 = bf16[8,128,8,128]{3,1,2,0:T(8,128)(2,1)S(1)} copy(bf16[8,128,8,128]{1,0,3,2:T(8,128)(2,1)} %bitcast.112) | data formatting | bytes 4194304 | tf_op jit(solution)/shard_map/reshape | solution.py:75
  134.8 1.8 gather_fusion.1
  136.7 0.8 gather_fusion.2
  137.4 1.4 copy.22
  138.9 0.3 broadcast_in_dim.70
  139.2 0.9 fusion.78
  140.0 0.1 copy-done.4
  140.2 1.7 pad_maximum_fusion
  141.8 11.6 %all-to-all-start.1 = ((bf16[16,576,128]{2,1,0:T(8,128)(2,1)}), bf16[16,576,128]{2,1,0:T(8,128)(2,1)S(1)}, u32[]{:S(2)}, u32[]{:S(2)}) async-start(bf16[16,576,128]{2,1,0:T(8,128)(2,1)} %pad_maximum_fusion), calls=%async_computation.1 | async-start | bytes 4718592 | tf_op jit(solution)/shard_map/all_to_all | solution.py:90
  153.5 31.1 %all-to-all-done.1 = bf16[16,576,128]{2,1,0:T(8,128)(2,1)S(1)} async-done(((bf16[16,576,128]{2,1,0:T(8,128)(2,1)}), bf16[16,576,128]{2,1,0:T(8,128)(2,1)S(1)}, u32[]{:S(2)}, u32[]{:S(2)}) %all-to-all-start.1) | async-done | bytes 2359328 | tf_op jit(solution)/shard_map/all_to_all | solution.py:90
  184.6 0.2 fusion.101
  184.8 0.7 fusion.82
  185.6 1.3 gather_fusion.3
  186.9 0.7 all_to_all.14
  187.6 6.5 %all-to-all-start.2 = ((f32[16,1,8]{2,1,0:T(1,128)}), f32[16,1,8]{2,1,0:T(1,128)S(1)}, u32[]{:S(2)}, u32[]{:S(2)}) async-start(f32[16,1,8]{2,1,0:T(1,128)} %bitcast.22), calls=%async_computation.2 | async-start | bytes 16384 | tf_op jit(solution)/shard_map/all_to_all | solution.py:98
  194.1 2.6 %copy.27 = bf16[1,1,1024,1024]{3,2,1,0:T(8,128)(2,1)} copy(bf16[1,1,1024,1024]{2,3,1,0:T(8,128)(2,1)S(1)} %bitcast.111) | data formatting | bytes 4194304
  196.7 4.5 %all-to-all-done.2 = f32[16,1,8]{2,1,0:T(1,128)S(1)} async-done(((f32[16,1,8]{2,1,0:T(1,128)}), f32[16,1,8]{2,1,0:T(1,128)S(1)}, u32[]{:S(2)}, u32[]{:S(2)}) %all-to-all-start.2) | async-done | bytes 544 | tf_op jit(solution)/shard_map/all_to_all | solution.py:98
  201.1 0.5 multiply_bitcast_fusion
  (39 shorter events, 0.4 us)
Async XLA Ops:
  0.6 40.4 %copy-start.7 = (pred[36]{0:T(512)(128)(4,1)S(1)}, pred[36]{0:T(512)(128)(4,1)}, u32[]{:S(2)}) copy-start(pred[36]{0:T(512)(128)(4,1)} %constant.79) | copy-start | bytes 112
  0.6 40.6 %copy-start.6 = (s32[36]{0:T(128)S(1)}, s32[36]{0:T(128)}, u32[]{:S(2)}) copy-start(s32[36]{0:T(128)} %constant.94) | copy-start | bytes 436
  0.7 40.6 %copy-start.5 = (s32[36]{0:T(128)S(1)}, s32[36]{0:T(128)}, u32[]{:S(2)}) copy-start(s32[36]{0:T(128)} %constant.95) | copy-start | bytes 436
  0.7 6.3 %copy-start.9 = (s32[4]{0:T(128)S(1)}, s32[4]{0:T(128)}, u32[]{:S(2)}) copy-start(s32[4]{0:T(128)} %param.11) | copy-start | bytes 52
  0.7 37.0 %all-to-all-start = ((bf16[8,128,1024]{2,1,0:T(8,128)(2,1)}), bf16[8,128,1024]{2,1,0:T(8,128)(2,1)S(1)}, u32[]{:S(2)}, u32[]{:S(2)}) async-start(bf16[8,128,1024]{2,1,0:T(8,128)(2,1)} %bitcast.117), calls=%async_computation | async-start | bytes 4194304 | tf_op jit(solution)/shard_map/all_to_all | solution.py:25
  38.2 24.4 %collective-permute-start.1 = (bf16[4,128,1024]{2,1,0:T(8,128)(2,1)S(1)}, bf16[4,128,1024]{2,1,0:T(8,128)(2,1)S(1)}, u32[]{:S(2)}, u32[]{:S(2)}) collective-permute-start(bf16[4,128,1024]{2,1,0:T(8,128)(2,1)S(1)} %gather_fusion), channel_id=1, source_target_pairs={{0,32},{16,48},{32,64},{48,80},{64,96},{80,112},{96,0},{112,16},{1... | collective-permute-start | bytes 3145736 | tf_op jit(solution)/shard_map/ppermute | solution.py:12
  38.3 24.5 %collective-permute-start.2 = (bf16[4,128,1024]{2,1,0:T(8,128)(2,1)S(1)}, bf16[4,128,1024]{2,1,0:T(8,128)(2,1)S(1)}, u32[]{:S(2)}, u32[]{:S(2)}) collective-permute-start(bf16[4,128,1024]{2,1,0:T(8,128)(2,1)S(1)} %gather_fusion), channel_id=1, source_target_pairs={{0,96},{16,112},{32,0},{48,16},{64,32},{80,48},{96,64},{112,80},{1... | collective-permute-start | bytes 3145736 | tf_op jit(solution)/shard_map/ppermute | solution.py:12
  41.0 24.6 %collective-permute-start = (bf16[4,128,1024]{2,1,0:T(8,128)(2,1)S(1)}, bf16[4,128,1024]{2,1,0:T(8,128)(2,1)}, u32[]{:S(2)}, u32[]{:S(2)}) collective-permute-start(bf16[4,128,1024]{2,1,0:T(8,128)(2,1)S(1)} %gather_fusion), channel_id=1, source_target_pairs={{0,16},{16,0},{32,48},{48,32},{64,80},{80,64},{96,112},{112,96},{1... | collective-permute-start | bytes 3145736 | tf_op jit(solution)/shard_map/ppermute | solution.py:16
  41.3 3.4 %copy-start = (bf16[1,4,1024,1024]{3,2,1,0:T(8,128)(2,1)S(1)}, bf16[1,4,1024,1024]{3,2,1,0:T(8,128)(2,1)}, u32[]{:S(2)}) copy-start(bf16[1,4,1024,1024]{3,2,1,0:T(8,128)(2,1)} %param.9) | copy-start | bytes 25165828
  62.7 15.8 %collective-permute-start.3 = (bf16[4,64,1024]{2,1,0:T(8,128)(2,1)S(1)}, bf16[4,64,1024]{2,1,0:T(8,128)(2,1)S(1)}, u32[]{:S(2)}, u32[]{:S(2)}) collective-permute-start(bf16[4,64,1024]{2,1,0:T(8,128)(2,1)S(1)} %slice.76), channel_id=1, source_target_pairs={{0,32},{16,48},{32,64},{48,80},{64,96},{80,112},{96,0},{112,16},{1... | collective-permute-start | bytes 1572872 | tf_op jit(solution)/shard_map/ppermute | solution.py:12
  62.9 15.7 %collective-permute-start.4 = (bf16[4,64,1024]{2,1,0:T(8,128)(2,1)S(1)}, bf16[4,64,1024]{2,1,0:T(8,128)(2,1)}, u32[]{:S(2)}, u32[]{:S(2)}) collective-permute-start(bf16[4,64,1024]{2,1,0:T(8,128)(2,1)S(1)} %slice.77), channel_id=1, source_target_pairs={{0,96},{16,112},{32,0},{48,16},{64,32},{80,48},{96,64},{112,80},{1... | collective-permute-start | bytes 1572872 | tf_op jit(solution)/shard_map/ppermute | solution.py:12
  65.6 31.9 %collective-permute-start.5 = (bf16[4,128,1024]{2,1,0:T(8,128)(2,1)}, bf16[4,128,1024]{2,1,0:T(8,128)(2,1)S(1)}, u32[]{:S(2)}, u32[]{:S(2)}) collective-permute-start(bf16[4,128,1024]{2,1,0:T(8,128)(2,1)} %collective-permute-done), channel_id=1, source_target_pairs={{0,32},{16,48},{32,64},{48,80},{64,96},{80,112},{96,0},{112,16},{1... | collective-permute-start | bytes 3145736 | tf_op jit(solution)/shard_map/ppermute | solution.py:12
  65.6 32.1 %collective-permute-start.6 = (bf16[4,128,1024]{2,1,0:T(8,128)(2,1)}, bf16[4,128,1024]{2,1,0:T(8,128)(2,1)S(1)}, u32[]{:S(2)}, u32[]{:S(2)}) collective-permute-start(bf16[4,128,1024]{2,1,0:T(8,128)(2,1)} %collective-permute-done), channel_id=1, source_target_pairs={{0,96},{16,112},{32,0},{48,16},{64,32},{80,48},{96,64},{112,80},{1... | collective-permute-start | bytes 3145736 | tf_op jit(solution)/shard_map/ppermute | solution.py:12
  97.6 11.5 %collective-permute-start.7 = (bf16[4,64,1024]{2,1,0:T(8,128)(2,1)S(1)}, bf16[4,64,1024]{2,1,0:T(8,128)(2,1)S(1)}, u32[]{:S(2)}, u32[]{:S(2)}) collective-permute-start(bf16[4,64,1024]{2,1,0:T(8,128)(2,1)S(1)} %slice.78), channel_id=1, source_target_pairs={{0,32},{16,48},{32,64},{48,80},{64,96},{80,112},{96,0},{112,16},{1... | collective-permute-start | bytes 1572872 | tf_op jit(solution)/shard_map/ppermute | solution.py:12
  97.7 11.3 %collective-permute-start.8 = (bf16[4,64,1024]{2,1,0:T(8,128)(2,1)S(1)}, bf16[4,64,1024]{2,1,0:T(8,128)(2,1)S(1)}, u32[]{:S(2)}, u32[]{:S(2)}) collective-permute-start(bf16[4,64,1024]{2,1,0:T(8,128)(2,1)S(1)} %slice.79), channel_id=1, source_target_pairs={{0,96},{16,112},{32,0},{48,16},{64,32},{80,48},{96,64},{112,80},{1... | collective-permute-start | bytes 1572872 | tf_op jit(solution)/shard_map/ppermute | solution.py:12
  129.5 2.0 %copy-start.1 = (bf16[1024,1024]{1,0:T(8,128)(2,1)}, bf16[1024,1024]{1,0:T(8,128)(2,1)S(1)}, u32[]{:S(2)}) copy-start(bf16[1024,1024]{1,0:T(8,128)(2,1)S(1)} %add_convert_fusion) | copy-start | bytes 6291460
  137.4 1.7 copy-start.3
  138.9 1.3 copy-start.4
  140.2 13.3 %copy-start.8 = (s32[128,2]{0,1:T(2,128)S(1)}, s32[128,2]{0,1:T(2,128)}, u32[]{:S(2)}) copy-start(s32[128,2]{0,1:T(2,128)} %param.12) | copy-start | bytes 3076
  141.8 42.8 %all-to-all-start.1 = ((bf16[16,576,128]{2,1,0:T(8,128)(2,1)}), bf16[16,576,128]{2,1,0:T(8,128)(2,1)S(1)}, u32[]{:S(2)}, u32[]{:S(2)}) async-start(bf16[16,576,128]{2,1,0:T(8,128)(2,1)} %pad_maximum_fusion), calls=%async_computation.1 | async-start | bytes 4718592 | tf_op jit(solution)/shard_map/all_to_all | solution.py:90
  184.8 9.3 %copy-start.2 = (bf16[1024,1024]{1,0:T(8,128)(2,1)S(1)}, bf16[1024,1024]{1,0:T(8,128)(2,1)}, u32[]{:S(2)}) copy-start(bf16[1024,1024]{1,0:T(8,128)(2,1)} %copy-done.1) | copy-start | bytes 6291460
  187.6 13.6 %all-to-all-start.2 = ((f32[16,1,8]{2,1,0:T(1,128)}), f32[16,1,8]{2,1,0:T(1,128)S(1)}, u32[]{:S(2)}, u32[]{:S(2)}) async-start(f32[16,1,8]{2,1,0:T(1,128)} %bitcast.22), calls=%async_computation.2 | async-start | bytes 16384 | tf_op jit(solution)/shard_map/all_to_all | solution.py:98
